TPU v7x, 128 devices: a whole 4x4x4 slice. The times are simulated.
128 devices in a mesh: leaf: 8 (over z, core), expert: 8 (over x_hi, y), tensor: 2 (over x_lo).
Axes of the slice: x: 4 (x_hi: 2, x_lo: 2; x = x_hi * 2 + x_lo), y: 4, z: 4, core: 2. Of those that a mesh axis runs over, the one named last changes fastest.
Arguments:
- drafts: bfloat16 [2048, 6144], P('leaf', ('expert', 'tensor')), may hold values from -6 to 6
- children: bfloat16 [4096, 6144], P('leaf', ('expert', 'tensor')), may hold values from -6 to 6
- child_order: int32 [16], replicated, may hold values from 0 to 15, each once
- spans: int32 [4096], P('leaf'), may hold values from 0 to 15
- span_bias: float32 [48, 16], P(('expert', 'tensor')), may hold values from -4 to 4
- out_weight: bfloat16 [6144, 6144], P(('expert', 'tensor')), may hold values from -0.078125 to 0.078125
- norm_gain: float32 [6144], replicated, may hold values from 0.1 to 1.9
- router: bfloat16 [6144, 8], replicated, may hold values from -0.078125 to 0.078125
- routes: int32 [2048, 2], P(('leaf', 'expert')), may hold values from 0 to 7, all different within a row; in each aligned block of 32 rows (0 to 31, 32 to 63, ...) at most 16 rows name the same one
- w_gate: bfloat16 [8, 6144, 8192], P('expert', None, ('leaf', 'tensor')), may hold values from -0.078125 to 0.078125
- w_up: bfloat16 [8, 6144, 8192], P('expert', None, ('leaf', 'tensor')), may hold values from -0.078125 to 0.078125
- w_down: bfloat16 [8, 8192, 6144], P('expert', ('leaf', 'tensor')), may hold values from -0.0625 to 0.0625
Outputs:
- merged_out: float32 [2048, 6144], P(('leaf', 'expert'))
Inputs may be any that keep to these rules, and one draw needn't show every extreme that they name: `routes`: each row names two different experts; within the rows of one index pair of leaf and expert (32 aligned rows) no expert is named more than 16 times, and exactly 16 times in some of them. `child_order`: A permutation: every parent has exactly two children.
All inputs are finite; a program needn't handle non-finite values.
Results may differ from a plain program's by a relative error of at most 0.013.
Values may be sent and summed in bfloat16 or wider, within the bound.
No kernel may reach another device: no remote copies, remote signals or barrier semaphores. Data moves between devices by JAX's collectives and lax.ppermute only.
A program may use at most 128 MiB of HBM per device.

v0:
```python
import math

import jax
import jax.numpy as jnp
from jax import lax
from jax.sharding import PartitionSpec as P

R = 256
PAR_DEV = 1


def per_device(
    drafts,
    children,
    child_order,
    spans,
    span_bias,
    out_weight,
    norm_gain,
    router,
    routes,
    w_gate,
    w_up,
    w_down,
):
    local_rows, local_width = drafts.shape
    heads_here = span_bias.shape[0]
    head_size = local_width // heads_here
    span_count = span_bias.shape[1]
    width = out_weight.shape[1]
    scale = 1.0 / math.sqrt(head_size)
    leaf_index = lax.axis_index("leaf")
    query_parent = leaf_index * PAR_DEV + jnp.arange(local_rows, dtype=jnp.int32) // R
    queries = drafts.reshape(local_rows, heads_here, head_size)
    bias_table = span_bias.T
    run_max = jnp.full((heads_here, local_rows), -1e30, jnp.float32)
    keys = lax.all_gather(children, "leaf", axis=0, tiled=True)
    key_spans = lax.all_gather(spans, "leaf", axis=0, tiled=True)
    key_count = keys.shape[0]
    child_ids = jnp.arange(key_count, dtype=jnp.int32) // R
    key_parent = jnp.take(child_order, child_ids) // 2
    key_heads = keys.reshape(key_count, heads_here, head_size)
    scores = (
        jnp.einsum("qhd,khd->hqk", queries, key_heads, preferred_element_type=jnp.float32) * scale
    )
    span_hot = (key_spans[:, None] == jnp.arange(span_count, dtype=jnp.int32)[None, :]).astype(
        jnp.float32
    )
    bias = jnp.dot(span_hot, bias_table, precision=lax.Precision.HIGHEST)
    scores = scores + bias.T[:, None, :]
    allowed = (query_parent[:, None] == key_parent[None, :])[None, :, :]
    masked = jnp.where(allowed, scores, -1e30)
    new_max = jnp.maximum(run_max, jnp.max(masked, axis=-1))
    weights = jnp.where(allowed, jnp.exp(masked - new_max[..., None]), 0.0)
    new_total = jnp.sum(weights, axis=-1)
    values = jnp.einsum(
        "hqk,khd->hqd", weights, key_heads.astype(jnp.float32), precision=lax.Precision.HIGHEST
    )
    attended = (
        (values / new_total[..., None])
        .transpose(1, 0, 2)
        .reshape(local_rows, local_width)
        .astype(jnp.bfloat16)
    )
    term = jnp.dot(attended, out_weight, preferred_element_type=jnp.float32)
    offset = lax.axis_index(("expert", "tensor")) * local_width
    own_cols = lax.dynamic_slice(term, (0, offset), (local_rows, local_width)) + drafts.astype(
        jnp.float32
    )
    term = lax.dynamic_update_slice(term, own_cols, (0, offset))
    share = lax.psum_scatter(term, ("expert", "tensor"), scatter_dimension=0, tiled=True)
    merged = lax.all_gather(share, "tensor", axis=0, tiled=True)
    mean_square = jnp.mean(merged * merged, axis=-1, keepdims=True)
    normed = (merged * lax.rsqrt(mean_square + 1e-05) * norm_gain).astype(jnp.bfloat16)
    logits = jnp.dot(normed, router, preferred_element_type=jnp.float32)
    experts = router.shape[1]
    tok_count = routes.shape[0]
    capacity = 4 * tok_count // lax.axis_size("expert")
    choice_hot = routes[:, :, None] == jnp.arange(experts, dtype=jnp.int32)[None, None, :]
    chosen = jnp.sum(jnp.where(choice_hot, logits[:, None, :], 0.0), axis=-1)
    gates = jax.nn.softmax(chosen, axis=-1)
    pairs = routes.reshape(-1)
    pair_hot = (pairs[:, None] == jnp.arange(experts, dtype=jnp.int32)[None, :]).astype(jnp.int32)
    earlier = jnp.cumsum(pair_hot, axis=0) - pair_hot
    slot_index = jnp.sum(earlier * pair_hot, axis=1)
    target = pairs * capacity + slot_index
    place_hot = (
        jnp.arange(experts * capacity, dtype=jnp.int32)[:, None] == target[None, :]
    ).astype(jnp.bfloat16)
    place_rows = jnp.sum(place_hot.reshape(experts * capacity, tok_count, 2), axis=-1)
    outgoing = jnp.dot(place_rows, normed, preferred_element_type=jnp.float32).astype(jnp.bfloat16)
    outgoing = outgoing.reshape(experts, capacity, width)
    arrived = lax.all_to_all(outgoing, "expert", split_axis=0, concat_axis=0, tiled=True).reshape(
        -1, width
    )
    piece = lax.all_gather(arrived, "leaf", axis=0, tiled=True)
    gate_v = jnp.dot(piece, w_gate[0], preferred_element_type=jnp.float32)
    up_v = jnp.dot(piece, w_up[0], preferred_element_type=jnp.float32)
    hidden = (jax.nn.silu(gate_v) * up_v).astype(jnp.bfloat16)
    part_rows = lax.psum_scatter(
        jnp.dot(hidden, w_down[0], preferred_element_type=jnp.float32).astype(jnp.bfloat16),
        ("leaf", "tensor"),
        scatter_dimension=0,
        tiled=True,
    )
    returned = lax.all_gather(part_rows, "tensor", axis=0, tiled=True)
    back = lax.all_to_all(
        returned.reshape(-1, capacity, width), "expert", split_axis=0, concat_axis=0, tiled=True
    ).reshape(-1, width)
    picked = jnp.take(back, target, axis=0).astype(jnp.float32).reshape(tok_count, 2, width)
    mixed = gates[:, 0:1] * picked[:, 0] + gates[:, 1:2] * picked[:, 1]
    return merged + mixed


def solution(mesh):
    in_specs = (
        P("leaf", ("expert", "tensor")),
        P("leaf", ("expert", "tensor")),
        P(),
        P("leaf"),
        P(("expert", "tensor"), None),
        P(("expert", "tensor"), None),
        P(),
        P(),
        P(("leaf", "expert"), None),
        P("expert", None, ("leaf", "tensor")),
        P("expert", None, ("leaf", "tensor")),
        P("expert", ("leaf", "tensor"), None),
    )
    out_specs = P(("leaf", "expert"), None)
    return jax.shard_map(
        per_device, mesh=mesh, in_specs=in_specs, out_specs=out_specs, check_vma=False
    )
```

profile of v0, /device:TPU:32, one launch (start us, length us, event | category | flops | bytes accessed | tf_op | source)
XLA Modules:
  0.0 676.7 jit_solution(13883977162747496001)
XLA Ops:
  6.5 1.9 copy.59
  8.6 1.1 copy.58
  9.6 12.6 %all-gather = s32[8,1,512]{2,1,0:T(1,128)S(1)} all-gather(s32[1,1,512]{2,1,0:T(1,128)} %bitcast.92), channel_id=1, replica_groups=mesh['leaf'=8,'expert'=8,'tensor'=2] {'leaf'}, dimensions={0}, use_global_device_ids=true | all-gather | bytes 18432 | tf_op jit(solution)/shard_map/all_gather | solution.py:38
  22.8 1.9 fusion.46
  24.8 4.2 compare_select_fusion.1
  29.0 5.6 add_select_fusion.1
  34.6 0.9 convolution_bitcast_fusion
  35.4 0.6 broadcast_compare_fusion
  36.1 1.9 all-gather.5.cloned.1.call-done
  38.0 4.9 fusion
  42.9 4.7 fusion.1
  47.7 10.3 %fusion.18 = bf16[256,3,128]{0,2,1:T(8,128)(2,1)S(1)} fusion(bf16[4096,3,128]{0,2,1:T(8,128)(2,1)S(1)} %bitcast.94, f32[3,256,4096]{2,1,0:T(8,128)S(1)} %get-tuple-element.26, f32[3,256]{1,0:T(4,128)S(1)} %broadcast_maximum_fusion, f32[3,4096]{1,0:T(4,128)S(1)} %convolution_bitcast_fusion, pred[256,4096]{1,0:T(8,128)(4,1)S(1)} %broadcast_compare_fusion, ...), kind=kOutput, calls=%fused_computation.24 | convolution fusion | flops 4847763456 | bytes 17029120 | tf_op jit(solution)/shard_map/hqk,khd->hqd/dot_general | solution.py:56
  58.1 4.5 fusion.47
  62.6 1.8 add_dynamic-update-slice_fusion
  64.9 0.2 select_reduce_fusion
  65.4 138.1 %reduce-scatter.3.cloned.1.call-done = f32[16,6144]{1,0:T(8,128)} async-done(((f32[256,6144]{1,0:T(8,128)}), f32[16,6144]{1,0:T(8,128)}) %reduce-scatter.3.cloned.1.call-update) | async-done | bytes 393232 | tf_op jit(solution)/shard_map/reduce_scatter | solution.py:71
  203.5 12.0 %all_gather.17 = f32[32,6144]{1,0:T(8,128)S(1)} all-gather(f32[16,6144]{1,0:T(8,128)} %reduce-scatter.3.cloned.1.call-done), channel_id=1, replica_groups=mesh['leaf'=8,'expert'=8,'tensor'=2] {'tensor'}, dimensions={0}, use_global_device_ids=true | all-gather | bytes 1179648 | tf_op jit(solution)/shard_map/all_gather | solution.py:72
  215.7 0.6 convolution_convert_fusion.1
  216.3 28.3 %all_to_all.10 = bf16[8,16,6144]{2,1,0:T(8,128)(2,1)} all-to-all(bf16[8,16,6144]{2,1,0:T(8,128)(2,1)S(1)} %bitcast.83), channel_id=1, replica_groups=mesh['leaf'=8,'expert'=8,'tensor'=2] {'expert'}, dimensions={0} | all-to-all | bytes 3145728 | tf_op jit(solution)/shard_map/all_to_all | solution.py:93
  244.7 64.3 %all-gather.7.cloned.1.call-done = bf16[1024,6144]{1,0:T(8,128)(2,1)} async-done(((bf16[128,6144]{1,0:T(8,128)(2,1)}), bf16[1024,6144]{1,0:T(8,128)(2,1)}) %all-gather.7.cloned.1.call-update) | async-done | bytes 12582928 | tf_op jit(solution)/shard_map/all_gather | solution.py:96
  309.0 11.6 %fusion.4 = f32[1024,512]{1,0:T(8,128)S(1)} fusion(bf16[1024,6144]{1,0:T(8,128)(2,1)} %all-gather.7.cloned.1.call-done, bf16[1,6144,512]{2,1,0:T(8,128)(2,1)} %param.22), kind=kOutput, calls=%fused_computation.9 | convolution fusion | flops 6442450944 | bytes 20971520 | tf_op jit(solution)/shard_map/dot_general | solution.py:98
  320.6 8.9 %multiply_convert_fusion = bf16[1024,512]{1,0:T(8,128)(2,1)S(1)} fusion(f32[1024,512]{1,0:T(8,128)S(1)} %fusion.4, bf16[1024,6144]{1,0:T(8,128)(2,1)S(1)} %copy-done.4, bf16[1,6144,512]{2,1,0:T(8,128)(2,1)} %param.21), kind=kOutput, calls=%fused_computation.20 | convolution fusion | flops 6445596672 | bytes 22020096 | tf_op jit(solution)/shard_map/dot_general | solution.py:97
  329.5 12.5 %convolution_convert_fusion = bf16[1024,6144]{1,0:T(8,128)(2,1)} fusion(bf16[1024,512]{1,0:T(8,128)(2,1)S(1)} %multiply_convert_fusion, bf16[1,512,6144]{2,1,0:T(8,128)(2,1)} %param.23), kind=kOutput, calls=%fused_computation.3 | convolution fusion | flops 6448742400 | bytes 19922944 | tf_op jit(solution)/shard_map/dot_general | solution.py:101
  342.1 265.6 %reduce-scatter.5.cloned.1.call-done = bf16[64,6144]{1,0:T(8,128)(2,1)} async-done(((bf16[1024,6144]{1,0:T(8,128)(2,1)}), bf16[64,6144]{1,0:T(8,128)(2,1)}) %reduce-scatter.5.cloned.1.call-update) | async-done | bytes 786448 | tf_op jit(solution)/shard_map/reduce_scatter | solution.py:100
  607.7 32.2 %all-gather.9.cloned.1.call-done = bf16[128,6144]{1,0:T(8,128)(2,1)} async-done(((bf16[64,6144]{1,0:T(8,128)(2,1)}), bf16[128,6144]{1,0:T(8,128)(2,1)}) %all-gather.9.cloned.1.call-update) | async-done | bytes 1572880 | tf_op jit(solution)/shard_map/all_gather | solution.py:106
  639.9 6.4 all-to-all-start.1
  646.5 0.3 fusion.44
  646.9 20.2 %all-to-all-done.1 = bf16[8,16,6144]{2,1,0:T(8,128)(2,1)S(1)} async-done(((bf16[8,16,6144]{2,1,0:T(8,128)(2,1)}), bf16[8,16,6144]{2,1,0:T(8,128)(2,1)S(1)}, u32[]{:S(2)}, u32[]{:S(2)}) %all-to-all-start.1) | async-done | bytes 1572896 | tf_op jit(solution)/shard_map/all_to_all | solution.py:107
  667.1 1.0 gather_fusion
  668.1 0.5 gather.12
  668.6 0.5 fusion.23
  669.1 1.1 fusion.21
  (58 shorter events, 1.9 us)
Async XLA Ops:
  6.5 640.0 %copy-start = (bf16[6144,8]{0,1:T(8,128)(2,1)S(1)}, bf16[6144,8]{0,1:T(8,128)(2,1)}, u32[]{:S(2)}) copy-start(bf16[6144,8]{0,1:T(8,128)(2,1)} %param.19) | copy-start | bytes 294916
  6.5 31.4 %all-gather.5.cloned.1.call-start = ((), (), s32[]{:S(2)}) async-start(), calls=%async_computation.4 | async-start | bytes 3538944 | tf_op jit(solution)/shard_map/all_gather | solution.py:37
  8.5 195.0 %reduce-scatter.3.cloned.1.call-start = ((), (), s32[]{:S(2)}) async-start(), calls=%async_computation.5 | async-start | bytes 6684672 | tf_op jit(solution)/shard_map/reduce_scatter | solution.py:71
  42.9 4.8 copy-start.5
  42.9 15.2 %slice-start = ((s8[4718592]{0:T(1024)(128)(4,1)}), s8[4194304]{0:T(1024)(128)(4,1)S(1)}, s32[]{:S(2)}) async-start(s8[4718592]{0:T(1024)(128)(4,1)} %bitcast.84), calls=%async_computation.9 | async-start | bytes 8388608
  47.6 10.4 %slice-start.1 = ((s8[4718592]{0:T(1024)(128)(4,1)}), s8[524288]{0:T(1024)(128)(4,1)S(1)}, s32[]{:S(2)}) async-start(s8[4718592]{0:T(1024)(128)(4,1)} %bitcast.84), calls=%async_computation.10 | async-start | bytes 1048576
  58.0 4.6 copy-start.1
  62.6 1.9 copy-start.3
  62.6 153.1 %copy-start.2 = (f32[6144]{0:T(1024)S(1)}, f32[6144]{0:T(1024)}, u32[]{:S(2)}) copy-start(f32[6144]{0:T(1024)} %param.18) | copy-start | bytes 73732
  64.5 244.5 %all-gather.7.cloned.1.call-start = ((), (), s32[]{:S(2)}) async-start(), calls=%async_computation.6 | async-start | bytes 14155776 | tf_op jit(solution)/shard_map/all_gather | solution.py:96
  244.6 363.0 %reduce-scatter.5.cloned.1.call-start = ((), (), s32[]{:S(2)}) async-start(), calls=%async_computation.7 | async-start | bytes 13369344 | tf_op jit(solution)/shard_map/reduce_scatter | solution.py:100
  309.0 11.6 %copy-start.4 = (bf16[1024,6144]{1,0:T(8,128)(2,1)S(1)}, bf16[1024,6144]{1,0:T(8,128)(2,1)}, u32[]{:S(2)}) copy-start(bf16[1024,6144]{1,0:T(8,128)(2,1)} %all-gather.7.cloned.1.call-done) | copy-start | bytes 37748740
  342.0 297.9 %all-gather.9.cloned.1.call-start = ((), (), s32[]{:S(2)}) async-start(), calls=%async_computation.8 | async-start | bytes 2359296 | tf_op jit(solution)/shard_map/all_gather | solution.py:106
  639.9 27.2 %all-to-all-start.1 = ((bf16[8,16,6144]{2,1,0:T(8,128)(2,1)}), bf16[8,16,6144]{2,1,0:T(8,128)(2,1)S(1)}, u32[]{:S(2)}, u32[]{:S(2)}) async-start(bf16[8,16,6144]{2,1,0:T(8,128)(2,1)} %bitcast.86), calls=%async_computation.3 | async-start | bytes 3145728 | tf_op jit(solution)/shard_map/all_to_all | solution.py:107
Sparse Core Ops, SparseCore 0:
  9.1 28.8 all-gather.4
  64.6 138.8 reduce-scatter.2
  244.8 64.1 all-gather.6
  342.1 265.4 reduce-scatter.4
  609.1 30.6 all-gather.8
where the time goes:
time: 678 us; the launch traced here: 677 us
  waiting for transfers between devices  522 us (77%)
  matrix products  54.5 us (8%)
  blocking collectives  52.9 us (8%)
  other arithmetic  19.8 us (3%)
  between operations  13.4 us (2%)
  local copies, waits for them, and re-layouts  7.08 us (1%)
    reduce_scatter x1, waiting for transfers between devices, per_device(): lax.psum_scatter(jnp.dot(hidden, w_down[0], preferred_element_type=jnp.fl...  266 us
    reduce_scatter x1, waiting for transfers between devices, per_device(): lax.psum_scatter(term, ('expert', 'tensor'), scatter_dimension=0, tiled=T...  138 us
    all_gather x1, waiting for transfers between devices, per_device(): piece = lax.all_gather(arrived, 'leaf', axis=0, tiled=True)  64.3 us
    all_gather x1, waiting for transfers between devices, per_device(): returned = lax.all_gather(part_rows, 'tensor', axis=0, tiled=True)  32.2 us
    all_to_all x1, blocking collectives, per_device(): lax.all_to_all(outgoing, 'expert', split_axis=0, concat_axis=0, tiled=True)  28.3 us
    all_to_all x1, waiting for transfers between devices, per_device(): lax.all_to_all(returned.reshape(-1, capacity, width), 'expert', split_axi...  20.2 us
  transfers between devices with their start and end apart: 6, of which 6 were waited for; matrix products, arithmetic and copies ran while one was open for 2% of the time, Pallas kernels for 0%

commit v1 on v0

v1 whole, which is shorter than its diff:
```python
import math

import jax
import jax.numpy as jnp
from jax import lax
from jax.sharding import PartitionSpec as P

R = 256


def attend_parent(queries, keys, key_spans, span_bias, scale):
    rows, local_width = queries.shape
    heads_here, span_count = span_bias.shape
    head_size = local_width // heads_here
    key_count = keys.shape[0]
    q = queries.reshape(rows, heads_here, head_size)
    k = keys.reshape(key_count, heads_here, head_size)
    scores = jnp.einsum("qhd,khd->hqk", q, k, preferred_element_type=jnp.float32) * scale
    span_hot = (key_spans[:, None] == jnp.arange(span_count, dtype=jnp.int32)[None, :]).astype(
        jnp.float32
    )
    bias = jnp.dot(span_hot, span_bias.T, precision=lax.Precision.HIGHEST)
    scores = scores + bias.T[:, None, :]
    top = jnp.max(scores, axis=-1, keepdims=True)
    weights = jnp.exp(scores - top)
    total = jnp.sum(weights, axis=-1, keepdims=True)
    values = jnp.einsum(
        "hqk,khd->hqd", weights, k.astype(jnp.float32), precision=lax.Precision.HIGHEST
    )
    return (values / total).transpose(1, 0, 2).reshape(rows, local_width).astype(jnp.bfloat16)


def per_device(
    drafts,
    children,
    child_order,
    spans,
    span_bias,
    out_weight,
    norm_gain,
    router,
    routes,
    w_gate,
    w_up,
    w_down,
):
    local_rows, local_width = drafts.shape
    heads_here = span_bias.shape[0]
    head_size = local_width // heads_here
    width = out_weight.shape[1]
    scale = 1.0 / math.sqrt(head_size)
    parents_here = local_rows // R
    leaf_index = lax.axis_index("leaf")
    keys = lax.all_gather(children, "leaf", axis=0, tiled=True)
    key_spans = lax.all_gather(spans, "leaf", axis=0, tiled=True)
    count = child_order.shape[0]
    ids = jnp.arange(count, dtype=jnp.int32)
    inverse = jnp.sum(jnp.where(child_order[None, :] == ids[:, None], ids[None, :], 0), axis=1)
    pieces = []
    for i in range(parents_here):
        parent = leaf_index * parents_here + i
        first = inverse[2 * parent]
        second = inverse[2 * parent + 1]
        own_keys = jnp.concatenate(
            [
                lax.dynamic_slice_in_dim(keys, first * R, R, 0),
                lax.dynamic_slice_in_dim(keys, second * R, R, 0),
            ],
            axis=0,
        )
        own_spans = jnp.concatenate(
            [
                lax.dynamic_slice_in_dim(key_spans, first * R, R, 0),
                lax.dynamic_slice_in_dim(key_spans, second * R, R, 0),
            ],
            axis=0,
        )
        pieces.append(attend_parent(drafts[i * R : (i + 1) * R], own_keys, own_spans, span_bias, scale))
    attended = pieces[0] if parents_here == 1 else jnp.concatenate(pieces, axis=0)
    term = jnp.dot(attended, out_weight, preferred_element_type=jnp.float32).astype(jnp.bfloat16)
    group = lax.axis_size(("expert", "tensor"))
    share_rows = local_rows // group
    arrived_terms = lax.all_to_all(
        term.reshape(group, share_rows, width), ("expert", "tensor"), 0, 0, tiled=True
    )
    own_drafts = lax.all_to_all(drafts, ("expert", "tensor"), 0, 1, tiled=True)
    share = jnp.sum(arrived_terms.astype(jnp.float32), axis=0) + own_drafts.astype(jnp.float32)
    merged = lax.all_gather(share, "tensor", axis=0, tiled=True)
    mean_square = jnp.mean(merged * merged, axis=-1, keepdims=True)
    normed = (merged * lax.rsqrt(mean_square + 1e-05) * norm_gain).astype(jnp.bfloat16)
    logits = jnp.dot(normed, router, preferred_element_type=jnp.float32)
    experts = router.shape[1]
    tok_count = routes.shape[0]
    capacity = 4 * tok_count // lax.axis_size("expert")
    choice_hot = routes[:, :, None] == jnp.arange(experts, dtype=jnp.int32)[None, None, :]
    chosen = jnp.sum(jnp.where(choice_hot, logits[:, None, :], 0.0), axis=-1)
    gates = jax.nn.softmax(chosen, axis=-1)
    pairs = routes.reshape(-1)
    pair_hot = (pairs[:, None] == jnp.arange(experts, dtype=jnp.int32)[None, :]).astype(jnp.int32)
    earlier = jnp.cumsum(pair_hot, axis=0) - pair_hot
    slot_index = jnp.sum(earlier * pair_hot, axis=1)
    target = pairs * capacity + slot_index
    place_hot = (
        jnp.arange(experts * capacity, dtype=jnp.int32)[:, None] == target[None, :]
    ).astype(jnp.bfloat16)
    place_rows = jnp.sum(place_hot.reshape(experts * capacity, tok_count, 2), axis=-1)
    outgoing = jnp.dot(place_rows, normed, preferred_element_type=jnp.float32).astype(jnp.bfloat16)
    outgoing = outgoing.reshape(experts, capacity, width)
    arrived = lax.all_to_all(outgoing, "expert", split_axis=0, concat_axis=0, tiled=True).reshape(
        -1, width
    )
    piece = lax.all_gather(arrived, "leaf", axis=0, tiled=True)
    gate_v = jnp.dot(piece, w_gate[0], preferred_element_type=jnp.float32)
    up_v = jnp.dot(piece, w_up[0], preferred_element_type=jnp.float32)
    hidden = (jax.nn.silu(gate_v) * up_v).astype(jnp.bfloat16)
    down = jnp.dot(hidden, w_down[0], preferred_element_type=jnp.float32).astype(jnp.bfloat16)
    part_rows = lax.psum_scatter(down, "leaf", scatter_dimension=0, tiled=True)
    back = lax.all_to_all(
        part_rows.reshape(-1, capacity, width), "expert", split_axis=0, concat_axis=0, tiled=True
    ).reshape(-1, width)
    picked = jnp.take(back, target, axis=0)
    halves = lax.all_gather(picked, "tensor", axis=0, tiled=False)
    expert_out = jnp.sum(halves.astype(jnp.float32), axis=0).astype(jnp.bfloat16)
    picked = expert_out.astype(jnp.float32).reshape(tok_count, 2, width)
    mixed = gates[:, 0:1] * picked[:, 0] + gates[:, 1:2] * picked[:, 1]
    return merged + mixed


def solution(mesh):
    in_specs = (
        P("leaf", ("expert", "tensor")),
        P("leaf", ("expert", "tensor")),
        P(),
        P("leaf"),
        P(("expert", "tensor"), None),
        P(("expert", "tensor"), None),
        P(),
        P(),
        P(("leaf", "expert"), None),
        P("expert", None, ("leaf", "tensor")),
        P("expert", None, ("leaf", "tensor")),
        P("expert", ("leaf", "tensor"), None),
    )
    out_specs = P(("leaf", "expert"), None)
    return jax.shard_map(
        per_device, mesh=mesh, in_specs=in_specs, out_specs=out_specs, check_vma=False
    )
```

time: 678 us -> 380 us (0.56)
  waiting for transfers between devices: 522 us -> 237 us
  matrix products: 54.5 us -> 39.5 us
  starting transfers between devices: 6.58 us -> 21.2 us
  other arithmetic: 19.8 us -> 6.53 us
    reduce_scatter x2 -> x1, waiting for transfers between devices: 404 us -> 71 us  [per_device(): part_rows = lax.psum_scatter(down, 'leaf', scatter_dimension=0, tiled=True)]
    all_to_all x1 -> x3, waiting for transfers between devices: 20.2 us -> 68 us  [the longest x1 46 us: per_device(): lax.all_to_all(term.reshape(group, share_rows, width), ('expert', 'tensor...]
    dot_general x4, matrix products: 20.6 us -> 5.81 us  [the longest x1 3.51 us: per_device(): jnp.dot(attended, out_weight, preferred_element_type=jnp.float32)]
    all_to_all x1 -> x3, starting transfers between devices: 6.41 us -> 20.9 us  [the longest x1 7.05 us: per_device(): own_drafts = lax.all_to_all(drafts, ('expert', 'tensor'), 0, 1, tiled=True)]
  transfers between devices with their start and end apart: 6 -> 7, of which waited for: 6 -> 6; matrix products, arithmetic and copies ran while one was open for 2% -> 3% of each run, Pallas kernels for 0% -> 0%
where the time goes in v1:
time: 380 us; the launch traced here: 379 us
  waiting for transfers between devices  237 us (62%)
  blocking collectives  49.3 us (13%)
  matrix products  39.5 us (10%)
  starting transfers between devices  21.2 us (6%)
  between operations  14.6 us (4%)
  local copies, waits for them, and re-layouts  10.6 us (3%)
  other arithmetic  6.53 us (2%)
    reduce_scatter x1, waiting for transfers between devices, per_device(): part_rows = lax.psum_scatter(down, 'leaf', scatter_dimension=0, tiled=True)  71 us
    all_gather x1, waiting for transfers between devices, per_device(): piece = lax.all_gather(arrived, 'leaf', axis=0, tiled=True)  64.1 us
    all_to_all x1, waiting for transfers between devices, per_device(): lax.all_to_all(term.reshape(group, share_rows, width), ('expert', 'tensor...  46 us
    all_gather x1, waiting for transfers between devices, per_device(): halves = lax.all_gather(picked, 'tensor', axis=0, tiled=False)  28.6 us
    all_to_all x1, blocking collectives, per_device(): lax.all_to_all(outgoing, 'expert', split_axis=0, concat_axis=0, tiled=True)  25.2 us
    all_to_all x1, waiting for transfers between devices, per_device(): lax.all_to_all(part_rows.reshape(-1, capacity, width), 'expert', split_ax...  22 us
    all_gather x1, blocking collectives, per_device(): key_spans = lax.all_gather(spans, 'leaf', axis=0, tiled=True)  12.6 us
    dot_general x1, matrix products, per_device(): jnp.dot(hidden, w_down[0], preferred_element_type=jnp.float32)  12.4 us
  transfers between devices with their start and end apart: 7, of which 6 were waited for; matrix products, arithmetic and copies ran while one was open for 3% of the time, Pallas kernels for 0%

profile of v1, /device:TPU:32, one launch (start us, length us, event | category | flops | bytes accessed | tf_op | source)
XLA Modules:
  0.0 378.6 jit_solution(11452479018206716020)
XLA Ops:
  6.5 1.9 copy.43
  8.5 7.0 %all-to-all-start.1 = ((bf16[16,16,384]{2,1,0:T(8,128)(2,1)}), bf16[16,16,384]{2,1,0:T(8,128)(2,1)S(1)}, u32[]{:S(2)}, u32[]{:S(2)}) async-start(bf16[16,16,384]{2,1,0:T(8,128)(2,1)} %bitcast.95), calls=%async_computation.1 | async-start | bytes 393216 | tf_op jit(solution)/shard_map/all_to_all | solution.py:86
  15.6 0.8 select_reduce_fusion.2
  16.3 0.7 fusion.35
  18.3 1.1 copy.44
  19.3 12.6 %all-gather = s32[8,1,512]{2,1,0:T(1,128)S(1)} all-gather(s32[1,1,512]{2,1,0:T(1,128)} %bitcast.99), channel_id=1, replica_groups=mesh['leaf'=8,'expert'=8,'tensor'=2] {'leaf'}, dimensions={0}, use_global_device_ids=true | all-gather | bytes 18432 | tf_op jit(solution)/shard_map/all_gather | solution.py:55
  32.1 1.0 convolution_bitcast_fusion
  33.1 5.0 %all-gather.5.cloned.1.call-done = bf16[4096,384]{0,1:T(8,128)(2,1)} async-done(((bf16[512,384]{0,1:T(8,128)(2,1)}), bf16[4096,384]{0,1:T(8,128)(2,1)}) %all-gather.5.cloned.1.call-update) | async-done | bytes 3145744 | tf_op jit(solution)/shard_map/all_gather | solution.py:54
  38.1 1.1 constant_dynamic-slice_fusion.1
  39.9 0.9 fusion.17
  40.7 0.8 copy-done.1
  41.5 3.5 convolution_convert_fusion.1
  45.0 7.0 %all-to-all-start = ((bf16[16,16,6144]{2,1,0:T(8,128)(2,1)}), bf16[16,16,6144]{2,1,0:T(8,128)(2,1)S(1)}, u32[]{:S(2)}, u32[]{:S(2)}) async-start(bf16[16,16,6144]{2,1,0:T(8,128)(2,1)} %bitcast.87), calls=%async_computation | async-start | bytes 6291456 | tf_op jit(solution)/shard_map/all_to_all | solution.py:83
  52.9 0.8 copy.58
  53.7 46.0 %all-to-all-done = bf16[16,16,6144]{2,1,0:T(8,128)(2,1)S(1)} async-done(((bf16[16,16,6144]{2,1,0:T(8,128)(2,1)}), bf16[16,16,6144]{2,1,0:T(8,128)(2,1)S(1)}, u32[]{:S(2)}, u32[]{:S(2)}) %all-to-all-start) | async-done | bytes 3145760 | tf_op jit(solution)/shard_map/all_to_all | solution.py:83
  100.8 11.4 %all_gather.18 = f32[32,6144]{1,0:T(8,128)S(1)} all-gather(f32[16,6144]{1,0:T(8,128)S(1)} %add.105), channel_id=1, replica_groups=mesh['leaf'=8,'expert'=8,'tensor'=2] {'tensor'}, dimensions={0}, use_global_device_ids=true | all-gather | bytes 1179648 | tf_op jit(solution)/shard_map/all_gather | solution.py:88
  112.4 0.6 convolution_convert_fusion.2
  113.0 25.2 %all_to_all.28 = bf16[8,16,6144]{2,1,0:T(8,128)(2,1)} all-to-all(bf16[8,16,6144]{2,1,0:T(8,128)(2,1)S(1)} %bitcast.89), channel_id=1, replica_groups=mesh['leaf'=8,'expert'=8,'tensor'=2] {'expert'}, dimensions={0} | all-to-all | bytes 3145728 | tf_op jit(solution)/shard_map/all_to_all | solution.py:109
  138.5 64.1 %all-gather.7.cloned.1.call-done = bf16[1024,6144]{1,0:T(8,128)(2,1)} async-done(((bf16[128,6144]{1,0:T(8,128)(2,1)}), bf16[1024,6144]{1,0:T(8,128)(2,1)}) %all-gather.7.cloned.1.call-update) | async-done | bytes 12582928 | tf_op jit(solution)/shard_map/all_gather | solution.py:112
  202.6 11.6 %fusion.1 = f32[1024,512]{1,0:T(8,128)S(1)} fusion(bf16[1024,6144]{1,0:T(8,128)(2,1)} %all-gather.7.cloned.1.call-done, bf16[1,6144,512]{2,1,0:T(8,128)(2,1)} %param.22), kind=kOutput, calls=%fused_computation.5 | convolution fusion | flops 6442450944 | bytes 20971520 | tf_op jit(solution)/shard_map/dot_general | solution.py:114
  214.2 8.9 %multiply_convert_fusion = bf16[1024,512]{1,0:T(8,128)(2,1)S(1)} fusion(f32[1024,512]{1,0:T(8,128)S(1)} %fusion.1, bf16[1024,6144]{1,0:T(8,128)(2,1)S(1)} %copy-done.5, bf16[1,6144,512]{2,1,0:T(8,128)(2,1)} %param.21), kind=kOutput, calls=%fused_computation.10 | convolution fusion | flops 6445596672 | bytes 22020096 | tf_op jit(solution)/shard_map/dot_general | solution.py:113
  223.1 12.4 %convolution_convert_fusion = bf16[1024,6144]{1,0:T(8,128)(2,1)} fusion(bf16[1024,512]{1,0:T(8,128)(2,1)S(1)} %multiply_convert_fusion, bf16[1,512,6144]{2,1,0:T(8,128)(2,1)} %param.23), kind=kOutput, calls=%fused_computation.1 | convolution fusion | flops 6448742400 | bytes 19922944 | tf_op jit(solution)/shard_map/dot_general | solution.py:116
  235.5 71.0 %reduce-scatter.2.cloned.1.call-done = bf16[128,6144]{1,0:T(8,128)(2,1)} async-done(((bf16[1024,6144]{1,0:T(8,128)(2,1)}), bf16[128,6144]{1,0:T(8,128)(2,1)}) %reduce-scatter.2.cloned.1.call-update) | async-done | bytes 1572880 | tf_op jit(solution)/shard_map/reduce_scatter | solution.py:117
  306.5 6.9 %all-to-all-start.3 = ((bf16[8,16,6144]{2,1,0:T(8,128)(2,1)}), bf16[8,16,6144]{2,1,0:T(8,128)(2,1)S(1)}, u32[]{:S(2)}, u32[]{:S(2)}) async-start(bf16[8,16,6144]{2,1,0:T(8,128)(2,1)} %bitcast.90), calls=%async_computation.4 | async-start | bytes 3145728 | tf_op jit(solution)/shard_map/all_to_all | solution.py:118
  313.6 22.0 %all-to-all-done.3 = bf16[8,16,6144]{2,1,0:T(8,128)(2,1)S(1)} async-done(((bf16[8,16,6144]{2,1,0:T(8,128)(2,1)}), bf16[8,16,6144]{2,1,0:T(8,128)(2,1)S(1)}, u32[]{:S(2)}, u32[]{:S(2)}) %all-to-all-start.3) | async-done | bytes 1572896 | tf_op jit(solution)/shard_map/all_to_all | solution.py:118
  335.5 1.0 gather_fusion
  336.6 1.0 bitcast_select_fusion
  338.0 28.6 %all-gather.9.cloned.1.call-done = bf16[2,64,6144]{2,1,0:T(8,128)(2,1)} async-done(((bf16[1,64,6144]{2,1,0:T(8,128)(2,1)}), bf16[2,64,6144]{2,1,0:T(8,128)(2,1)}) %all-gather.9.cloned.1.call-update) | async-done | bytes 1572880 | tf_op jit(solution)/shard_map/all_gather | solution.py:122
  366.7 1.8 reduce_sum.101
  368.4 1.0 reshape.142
  369.4 1.2 fusion.33
  370.6 1.4 fusion.22
  (49 shorter events, 3.7 us)
Async XLA Ops:
  6.5 331.1 %copy-start = (bf16[6144,8]{0,1:T(8,128)(2,1)S(1)}, bf16[6144,8]{0,1:T(8,128)(2,1)}, u32[]{:S(2)}) copy-start(bf16[6144,8]{0,1:T(8,128)(2,1)} %param.19) | copy-start | bytes 294916
  6.5 31.5 %all-gather.5.cloned.1.call-start = ((), (), s32[]{:S(2)}) async-start(), calls=%async_computation.5 | async-start | bytes 3538944 | tf_op jit(solution)/shard_map/all_gather | solution.py:54
  8.5 36.5 %all-to-all-start.1 = ((bf16[16,16,384]{2,1,0:T(8,128)(2,1)}), bf16[16,16,384]{2,1,0:T(8,128)(2,1)S(1)}, u32[]{:S(2)}, u32[]{:S(2)}) async-start(bf16[16,16,384]{2,1,0:T(8,128)(2,1)} %bitcast.95), calls=%async_computation.1 | async-start | bytes 393216 | tf_op jit(solution)/shard_map/all_to_all | solution.py:86
  39.2 2.3 copy-start.1
  45.0 7.0 %copy-start.4 = (s32[32,2]{0,1:T(2,128)S(1)}, s32[32,2]{0,1:T(2,128)}, u32[]{:S(2)}) copy-start(s32[32,2]{0,1:T(2,128)} %param.20) | copy-start | bytes 772
  45.0 54.7 %all-to-all-start = ((bf16[16,16,6144]{2,1,0:T(8,128)(2,1)}), bf16[16,16,6144]{2,1,0:T(8,128)(2,1)S(1)}, u32[]{:S(2)}, u32[]{:S(2)}) async-start(bf16[16,16,6144]{2,1,0:T(8,128)(2,1)} %bitcast.87), calls=%async_computation | async-start | bytes 6291456 | tf_op jit(solution)/shard_map/all_to_all | solution.py:83
  52.0 150.6 %all-gather.7.cloned.1.call-start = ((), (), s32[]{:S(2)}) async-start(), calls=%async_computation.6 | async-start | bytes 14155776 | tf_op jit(solution)/shard_map/all_gather | solution.py:112
  99.7 1.0 copy-start.2
  100.2 12.2 %copy-start.3 = (f32[6144]{0:T(1024)S(1)}, f32[6144]{0:T(1024)}, u32[]{:S(2)}) copy-start(f32[6144]{0:T(1024)} %param.18) | copy-start | bytes 73732
  138.3 168.2 %reduce-scatter.2.cloned.1.call-start = ((), (), s32[]{:S(2)}) async-start(), calls=%async_computation.7 | async-start | bytes 14155776 | tf_op jit(solution)/shard_map/reduce_scatter | solution.py:117
  202.6 11.6 %copy-start.5 = (bf16[1024,6144]{1,0:T(8,128)(2,1)S(1)}, bf16[1024,6144]{1,0:T(8,128)(2,1)}, u32[]{:S(2)}) copy-start(bf16[1024,6144]{1,0:T(8,128)(2,1)} %all-gather.7.cloned.1.call-done) | copy-start | bytes 37748740
  306.5 29.1 %all-to-all-start.3 = ((bf16[8,16,6144]{2,1,0:T(8,128)(2,1)}), bf16[8,16,6144]{2,1,0:T(8,128)(2,1)S(1)}, u32[]{:S(2)}, u32[]{:S(2)}) async-start(bf16[8,16,6144]{2,1,0:T(8,128)(2,1)} %bitcast.90), calls=%async_computation.4 | async-start | bytes 3145728 | tf_op jit(solution)/shard_map/all_to_all | solution.py:118
  313.4 53.2 %all-gather.9.cloned.1.call-start = ((), (), s32[]{:S(2)}) async-start(), calls=%async_computation.8 | async-start | bytes 2359296 | tf_op jit(solution)/shard_map/all_gather | solution.py:122
Sparse Core Ops, SparseCore 0:
  9.1 28.9 all-gather.4
  138.4 64.1 all-gather.6
  235.6 70.8 reduce-scatter.1
  337.7 28.8 all-gather.8

commit v2 on v1

--- a/solution.py
+++ b/solution.py
@@ -30,6 +30,12 @@
     return (values / total).transpose(1, 0, 2).reshape(rows, local_width).astype(jnp.bfloat16)
 
 
+def pair_gather(share):
+    other = lax.ppermute(share, "tensor", perm=[(0, 1), (1, 0)])
+    low = lax.axis_index("tensor") == 0
+    return jnp.concatenate([jnp.where(low, share, other), jnp.where(low, other, share)], axis=0)
+
+
 def per_device(
     drafts,
     children,
@@ -51,30 +57,32 @@
     scale = 1.0 / math.sqrt(head_size)
     parents_here = local_rows // R
     leaf_index = lax.axis_index("leaf")
-    keys = lax.all_gather(children, "leaf", axis=0, tiled=True)
-    key_spans = lax.all_gather(spans, "leaf", axis=0, tiled=True)
+    child_rows = children.shape[0]
+    children_here = child_rows // R
+    span_rows = -(-spans.shape[0] // local_width)
+    span_rows = -(-span_rows // 8) * 8
+    span_block = jnp.pad(spans.astype(jnp.bfloat16), (0, span_rows * local_width - spans.shape[0]))
+    payload = jnp.concatenate([children, span_block.reshape(span_rows, local_width)], axis=0)
+    gathered = lax.all_gather(payload, "leaf", axis=0, tiled=False)
+    span_table = gathered[:, child_rows:].reshape(gathered.shape[0], span_rows * local_width)
     count = child_order.shape[0]
     ids = jnp.arange(count, dtype=jnp.int32)
     inverse = jnp.sum(jnp.where(child_order[None, :] == ids[:, None], ids[None, :], 0), axis=1)
+
+    def child_keys(child):
+        holder = child // children_here
+        offset = (child % children_here) * R
+        rows = lax.dynamic_slice(gathered, (holder, offset, 0), (1, R, local_width))[0]
+        marks = lax.dynamic_slice(span_table, (holder, offset), (1, R))[0]
+        return rows, marks.astype(jnp.int32)
+
     pieces = []
     for i in range(parents_here):
         parent = leaf_index * parents_here + i
-        first = inverse[2 * parent]
-        second = inverse[2 * parent + 1]
-        own_keys = jnp.concatenate(
-            [
-                lax.dynamic_slice_in_dim(keys, first * R, R, 0),
-                lax.dynamic_slice_in_dim(keys, second * R, R, 0),
-            ],
-            axis=0,
-        )
-        own_spans = jnp.concatenate(
-            [
-                lax.dynamic_slice_in_dim(key_spans, first * R, R, 0),
-                lax.dynamic_slice_in_dim(key_spans, second * R, R, 0),
-            ],
-            axis=0,
-        )
+        first_rows, first_spans = child_keys(inverse[2 * parent])
+        second_rows, second_spans = child_keys(inverse[2 * parent + 1])
+        own_keys = jnp.concatenate([first_rows, second_rows], axis=0)
+        own_spans = jnp.concatenate([first_spans, second_spans], axis=0)
         pieces.append(attend_parent(drafts[i * R : (i + 1) * R], own_keys, own_spans, span_bias, scale))
     attended = pieces[0] if parents_here == 1 else jnp.concatenate(pieces, axis=0)
     term = jnp.dot(attended, out_weight, preferred_element_type=jnp.float32).astype(jnp.bfloat16)
@@ -85,7 +93,7 @@
     )
     own_drafts = lax.all_to_all(drafts, ("expert", "tensor"), 0, 1, tiled=True)
     share = jnp.sum(arrived_terms.astype(jnp.float32), axis=0) + own_drafts.astype(jnp.float32)
-    merged = lax.all_gather(share, "tensor", axis=0, tiled=True)
+    merged = pair_gather(share)
     mean_square = jnp.mean(merged * merged, axis=-1, keepdims=True)
     normed = (merged * lax.rsqrt(mean_square + 1e-05) * norm_gain).astype(jnp.bfloat16)
     logits = jnp.dot(normed, router, preferred_element_type=jnp.float32)
@@ -109,18 +117,23 @@
     arrived = lax.all_to_all(outgoing, "expert", split_axis=0, concat_axis=0, tiled=True).reshape(
         -1, width
     )
-    piece = lax.all_gather(arrived, "leaf", axis=0, tiled=True)
-    gate_v = jnp.dot(piece, w_gate[0], preferred_element_type=jnp.float32)
-    up_v = jnp.dot(piece, w_up[0], preferred_element_type=jnp.float32)
-    hidden = (jax.nn.silu(gate_v) * up_v).astype(jnp.bfloat16)
-    down = jnp.dot(hidden, w_down[0], preferred_element_type=jnp.float32).astype(jnp.bfloat16)
-    part_rows = lax.psum_scatter(down, "leaf", scatter_dimension=0, tiled=True)
+    chunks = 2
+    chunk_rows = arrived.shape[0] // chunks
+    returned = []
+    for c in range(chunks):
+        piece = lax.all_gather(arrived[c * chunk_rows : (c + 1) * chunk_rows], "leaf", axis=0, tiled=True)
+        gate_v = jnp.dot(piece, w_gate[0], preferred_element_type=jnp.float32)
+        up_v = jnp.dot(piece, w_up[0], preferred_element_type=jnp.float32)
+        hidden = (jax.nn.silu(gate_v) * up_v).astype(jnp.bfloat16)
+        down = jnp.dot(hidden, w_down[0], preferred_element_type=jnp.float32).astype(jnp.bfloat16)
+        returned.append(lax.psum_scatter(down, "leaf", scatter_dimension=0, tiled=True))
+    part_rows = jnp.concatenate(returned, axis=0)
     back = lax.all_to_all(
         part_rows.reshape(-1, capacity, width), "expert", split_axis=0, concat_axis=0, tiled=True
     ).reshape(-1, width)
     picked = jnp.take(back, target, axis=0)
-    halves = lax.all_gather(picked, "tensor", axis=0, tiled=False)
-    expert_out = jnp.sum(halves.astype(jnp.float32), axis=0).astype(jnp.bfloat16)
+    other = lax.ppermute(picked, "tensor", perm=[(0, 1), (1, 0)])
+    expert_out = (picked.astype(jnp.float32) + other.astype(jnp.float32)).astype(jnp.bfloat16)
     picked = expert_out.astype(jnp.float32).reshape(tok_count, 2, width)
     mixed = gates[:, 0:1] * picked[:, 0] + gates[:, 1:2] * picked[:, 1]
     return merged + mixed

time: 380 us -> 376 us (0.989)
  blocking collectives: 49.3 us -> 25.1 us
  matrix products: 39.5 us -> 46 us
  other arithmetic: 6.53 us -> 12.7 us
    ppermute x0 -> x2, waiting for transfers between devices: none -> 26.6 us  [the longest x1 18.6 us: per_device(): other = lax.ppermute(picked, 'tensor', perm=[(0, 1), (1, 0)])]
    all_gather x2 -> x0, blocking collectives: 24.1 us -> none  [the longest x1 12.6 us: per_device(): key_spans = lax.all_gather(spans, 'leaf', axis=0, tiled=True)]
    all_gather x3, waiting for transfers between devices: 97.7 us -> 74 us  [the longest x2 59.2 us: per_device(): lax.all_gather(arrived[c * chunk_rows:(c + 1) * chunk_rows], 'leaf', axis...]
    dot_general x1 -> x2, matrix products: 8.89 us -> 16.4 us  [per_device(): gate_v = jnp.dot(piece, w_gate[0], preferred_element_type=jnp.float32)]
    concatenate x2 -> x3, other arithmetic: 0.04 us -> 4.47 us  [the longest x1 2.67 us: per_device(): part_rows = jnp.concatenate(returned, axis=0)]
    reduce_scatter x1 -> x2, waiting for transfers between devices: 71 us -> 68.1 us  [per_device(): lax.psum_scatter(down, 'leaf', scatter_dimension=0, tiled=True)]
    dot_general x1 -> x2, matrix products: 12.4 us -> 10.8 us  [per_device(): jnp.dot(hidden, w_down[0], preferred_element_type=jnp.float32)]
    dot_general x1 -> x2, matrix products: 11.6 us -> 12.8 us  [per_device(): up_v = jnp.dot(piece, w_up[0], preferred_element_type=jnp.float32)]
  transfers between devices with their start and end apart: 7 -> 10, of which waited for: 6 -> 9; matrix products, arithmetic and copies ran while one was open for 3% -> 14% of each run, Pallas kernels for 0% -> 0%
where the time goes in v2:
time: 376 us; the launch traced here: 375 us
  waiting for transfers between devices  238 us (63%)
  matrix products  46 us (12%)
  blocking collectives  25.1 us (7%)
  starting transfers between devices  24.3 us (6%)
  between operations  18.4 us (5%)
  other arithmetic  12.7 us (3%)
  local copies, waits for them, and re-layouts  11 us (3%)
    reduce_scatter x2, waiting for transfers between devices, per_device(): lax.psum_scatter(down, 'leaf', scatter_dimension=0, tiled=True)  68.1 us
    all_gather x2, waiting for transfers between devices, per_device(): lax.all_gather(arrived[c * chunk_rows:(c + 1) * chunk_rows], 'leaf', axis...  59.2 us
    all_to_all x1, waiting for transfers between devices, per_device(): lax.all_to_all(term.reshape(group, share_rows, width), ('expert', 'tensor...  46.5 us
    all_to_all x1, blocking collectives, per_device(): lax.all_to_all(outgoing, 'expert', split_axis=0, concat_axis=0, tiled=True)  25.1 us
    all_to_all x1, waiting for transfers between devices, per_device(): lax.all_to_all(part_rows.reshape(-1, capacity, width), 'expert', split_ax...  21.9 us
    ppermute x1, waiting for transfers between devices, per_device(): other = lax.ppermute(picked, 'tensor', perm=[(0, 1), (1, 0)])  18.6 us
    dot_general x2, matrix products, per_device(): gate_v = jnp.dot(piece, w_gate[0], preferred_element_type=jnp.float32)  16.4 us
    all_gather x1, waiting for transfers between devices, per_device(): gathered = lax.all_gather(payload, 'leaf', axis=0, tiled=False)  14.8 us
  transfers between devices with their start and end apart: 10, of which 9 were waited for; matrix products, arithmetic and copies ran while one was open for 14% of the time, Pallas kernels for 0%

profile of v2, /device:TPU:32, one launch (start us, length us, event | category | flops | bytes accessed | tf_op | source)
XLA Modules:
  0.0 375.4 jit_solution(3424828647165259367)
XLA Ops:
  7.3 1.8 pad_maximum_fusion.2
  9.1 7.0 %all-to-all-start.1 = ((bf16[16,16,384]{2,1,0:T(8,128)(2,1)}), bf16[16,16,384]{2,1,0:T(8,128)(2,1)S(1)}, u32[]{:S(2)}, u32[]{:S(2)}) async-start(bf16[16,16,384]{2,1,0:T(8,128)(2,1)} %bitcast.112), calls=%async_computation.1 | async-start | bytes 393216 | tf_op jit(solution)/shard_map/all_to_all | solution.py:94
  22.4 1.1 copy.84
  23.5 14.8 %all-gather.9.cloned.1.call-done = bf16[4160,384]{1,0:T(8,128)(2,1)} async-done(((bf16[520,384]{1,0:T(8,128)(2,1)}), bf16[4160,384]{1,0:T(8,128)(2,1)}) %all-gather.9.cloned.1.call-update) | async-done | bytes 3194896 | tf_op jit(solution)/shard_map/all_gather | solution.py:66
  39.1 1.1 constant_dynamic-slice_fusion.1
  41.9 0.9 fusion.32
  43.1 3.5 convolution_convert_fusion.2
  46.6 6.9 %all-to-all-start = ((bf16[16,16,6144]{2,1,0:T(8,128)(2,1)}), bf16[16,16,6144]{2,1,0:T(8,128)(2,1)S(1)}, u32[]{:S(2)}, u32[]{:S(2)}) async-start(bf16[16,16,6144]{2,1,0:T(8,128)(2,1)} %bitcast.106), calls=%async_computation | async-start | bytes 6291456 | tf_op jit(solution)/shard_map/all_to_all | solution.py:91
  54.8 46.5 %all-to-all-done = bf16[16,16,6144]{2,1,0:T(8,128)(2,1)S(1)} async-done(((bf16[16,16,6144]{2,1,0:T(8,128)(2,1)}), bf16[16,16,6144]{2,1,0:T(8,128)(2,1)S(1)}, u32[]{:S(2)}, u32[]{:S(2)}) %all-to-all-start) | async-done | bytes 3145760 | tf_op jit(solution)/shard_map/all_to_all | solution.py:91
  101.8 1.0 add.142
  102.8 2.4 collective-permute-start
  105.7 8.0 %collective-permute-done = f32[16,6144]{1,0:T(8,128)S(1)} collective-permute-done((f32[16,6144]{1,0:T(8,128)S(1)}, f32[16,6144]{1,0:T(8,128)S(1)}, u32[]{:S(2)}, u32[]{:S(2)}) %collective-permute-start) | collective-permute-done | bytes 393248 | tf_op jit(solution)/shard_map/ppermute | solution.py:34
  115.3 25.1 %all_to_all.28 = bf16[8,16,6144]{2,1,0:T(8,128)(2,1)S(1)} all-to-all(bf16[8,16,6144]{2,1,0:T(8,128)(2,1)S(1)} %bitcast.107), channel_id=1, replica_groups=mesh['leaf'=8,'expert'=8,'tensor'=2] {'expert'}, dimensions={0} | all-to-all | bytes 3145728 | tf_op jit(solution)/shard_map/all_to_all | solution.py:117
  140.5 1.3 fusion.52
  142.7 36.6 %all-gather.5.cloned.1.call-done = bf16[512,6144]{1,0:T(8,128)(2,1)} async-done(((bf16[64,6144]{1,0:T(8,128)(2,1)}), bf16[512,6144]{1,0:T(8,128)(2,1)}) %all-gather.5.cloned.1.call-update) | async-done | bytes 6291472 | tf_op jit(solution)/shard_map/all_gather | solution.py:124
  179.4 8.2 %fusion.8 = f32[512,512]{1,0:T(8,128)S(1)} fusion(bf16[512,6144]{1,0:T(8,128)(2,1)} %all-gather.5.cloned.1.call-done, bf16[1,6144,512]{2,1,0:T(8,128)(2,1)} %param.21), kind=kOutput, calls=%fused_computation.13 | convolution fusion | flops 3221225472 | bytes 13631488 | tf_op jit(solution)/shard_map/dot_general | solution.py:125
  187.6 6.4 %fusion.23 = bf16[512,512]{1,0:T(8,128)(2,1)S(1)} fusion(bf16[512,6144]{1,0:T(8,128)(2,1)S(1)} %copy-done.7, bf16[1,6144,512]{2,1,0:T(8,128)(2,1)} %param.22, f32[512,512]{1,0:T(8,128)S(1)} %fusion.8), kind=kOutput, calls=%fused_computation.27 | convolution fusion | flops 3222798336 | bytes 14155776 | tf_op jit(solution)/shard_map/dot_general | solution.py:126
  194.0 5.4 %convolution_convert_fusion.1 = bf16[512,6144]{1,0:T(8,128)(2,1)} fusion(bf16[512,512]{1,0:T(8,128)(2,1)S(1)} %fusion.23, bf16[1,512,6144]{2,1,0:T(8,128)(2,1)S(1)} %bitcast.121), kind=kOutput, calls=%fused_computation.2 | convolution fusion | flops 3224371200 | bytes 13107200 | tf_op jit(solution)/shard_map/dot_general | solution.py:128
  199.6 22.6 %all-gather.7.cloned.1.call-done = bf16[512,6144]{1,0:T(8,128)(2,1)} async-done(((bf16[64,6144]{1,0:T(8,128)(2,1)}), bf16[512,6144]{1,0:T(8,128)(2,1)}) %all-gather.7.cloned.1.call-update) | async-done | bytes 6291472 | tf_op jit(solution)/shard_map/all_gather | solution.py:124
  222.2 8.2 %fusion.6 = f32[512,512]{1,0:T(8,128)S(1)} fusion(bf16[512,6144]{1,0:T(8,128)(2,1)} %all-gather.7.cloned.1.call-done, bf16[1,6144,512]{2,1,0:T(8,128)(2,1)} %param.21), kind=kOutput, calls=%fused_computation.11 | convolution fusion | flops 3221225472 | bytes 13631488 | tf_op jit(solution)/shard_map/dot_general | solution.py:125
  230.4 6.4 %fusion.20 = bf16[512,512]{1,0:T(8,128)(2,1)S(1)} fusion(bf16[512,6144]{1,0:T(8,128)(2,1)S(1)} %copy-done.6, bf16[1,6144,512]{2,1,0:T(8,128)(2,1)} %param.22, f32[512,512]{1,0:T(8,128)S(1)} %fusion.6), kind=kOutput, calls=%fused_computation.26 | convolution fusion | flops 3222798336 | bytes 14155776 | tf_op jit(solution)/shard_map/dot_general | solution.py:126
  236.9 5.4 %convolution_convert_fusion = bf16[512,6144]{1,0:T(8,128)(2,1)} fusion(bf16[512,512]{1,0:T(8,128)(2,1)S(1)} %fusion.20, bf16[1,512,6144]{2,1,0:T(8,128)(2,1)S(1)} %bitcast.123), kind=kOutput, calls=%fused_computation.1 | convolution fusion | flops 3224371200 | bytes 13107200 | tf_op jit(solution)/shard_map/dot_general | solution.py:128
  242.3 23.5 %reduce-scatter.3.cloned.1.call-done = bf16[64,6144]{1,0:T(8,128)(2,1)} async-done(((bf16[512,6144]{1,0:T(8,128)(2,1)}), bf16[64,6144]{1,0:T(8,128)(2,1)}) %reduce-scatter.3.cloned.1.call-update) | async-done | bytes 786448 | tf_op jit(solution)/shard_map/reduce_scatter | solution.py:129
  265.8 44.6 %reduce-scatter.5.cloned.1.call-done = bf16[64,6144]{1,0:T(8,128)(2,1)} async-done(((bf16[512,6144]{1,0:T(8,128)(2,1)}), bf16[64,6144]{1,0:T(8,128)(2,1)}) %reduce-scatter.5.cloned.1.call-update) | async-done | bytes 786448 | tf_op jit(solution)/shard_map/reduce_scatter | solution.py:129
  310.4 2.7 pad_maximum_fusion
  313.1 6.7 %all-to-all-start.3 = ((bf16[8,16,6144]{2,1,0:T(8,128)(2,1)}), bf16[8,16,6144]{2,1,0:T(8,128)(2,1)S(1)}, u32[]{:S(2)}, u32[]{:S(2)}) async-start(bf16[8,16,6144]{2,1,0:T(8,128)(2,1)} %bitcast.21), calls=%async_computation.5 | async-start | bytes 3145728 | tf_op jit(solution)/shard_map/all_to_all | solution.py:131
  319.9 21.9 %all-to-all-done.3 = bf16[8,16,6144]{2,1,0:T(8,128)(2,1)S(1)} async-done(((bf16[8,16,6144]{2,1,0:T(8,128)(2,1)}), bf16[8,16,6144]{2,1,0:T(8,128)(2,1)S(1)}, u32[]{:S(2)}, u32[]{:S(2)}) %all-to-all-start.3) | async-done | bytes 1572896 | tf_op jit(solution)/shard_map/all_to_all | solution.py:131
  341.8 1.0 gather_fusion
  344.2 18.6 %collective-permute-done.1 = bf16[64,6144]{1,0:T(8,128)(2,1)} collective-permute-done((bf16[64,6144]{1,0:T(8,128)(2,1)S(1)}, bf16[64,6144]{1,0:T(8,128)(2,1)}, u32[]{:S(2)}, u32[]{:S(2)}) %collective-permute-start.1) | collective-permute-done | bytes 786464 | tf_op jit(solution)/shard_map/ppermute | solution.py:135
  362.8 1.4 fusion.35
  365.1 1.2 fusion.51
  366.3 2.6 fusion.38
  (85 shorter events, 12.1 us)
Async XLA Ops:
  6.5 337.3 %copy-start = (bf16[6144,8]{0,1:T(8,128)(2,1)S(1)}, bf16[6144,8]{0,1:T(8,128)(2,1)}, u32[]{:S(2)}) copy-start(bf16[6144,8]{0,1:T(8,128)(2,1)} %param.19) | copy-start | bytes 294916
  6.5 34.4 %copy-start.8 = (f32[3,16]{1,0:T(4,128)S(1)}, f32[3,16]{1,0:T(4,128)}, u32[]{:S(2)}) copy-start(f32[3,16]{1,0:T(4,128)} %param.16) | copy-start | bytes 580
  6.5 31.7 %all-gather.9.cloned.1.call-start = ((), (), s32[]{:S(2)}) async-start(), calls=%async_computation.10 | async-start | bytes 3594240 | tf_op jit(solution)/shard_map/all_gather | solution.py:66
  9.1 37.5 %all-to-all-start.1 = ((bf16[16,16,384]{2,1,0:T(8,128)(2,1)}), bf16[16,16,384]{2,1,0:T(8,128)(2,1)S(1)}, u32[]{:S(2)}, u32[]{:S(2)}) async-start(bf16[16,16,384]{2,1,0:T(8,128)(2,1)} %bitcast.112), calls=%async_computation.1 | async-start | bytes 393216 | tf_op jit(solution)/shard_map/all_to_all | solution.py:94
  40.8 2.3 copy-start.1
  46.6 7.0 %copy-start.5 = (s32[32,2]{0,1:T(2,128)S(1)}, s32[32,2]{0,1:T(2,128)}, u32[]{:S(2)}) copy-start(s32[32,2]{0,1:T(2,128)} %param.20) | copy-start | bytes 772
  46.6 54.7 %all-to-all-start = ((bf16[16,16,6144]{2,1,0:T(8,128)(2,1)}), bf16[16,16,6144]{2,1,0:T(8,128)(2,1)S(1)}, u32[]{:S(2)}, u32[]{:S(2)}) async-start(bf16[16,16,6144]{2,1,0:T(8,128)(2,1)} %bitcast.106), calls=%async_computation | async-start | bytes 6291456 | tf_op jit(solution)/shard_map/all_to_all | solution.py:91
  53.6 61.0 %copy-start.4 = (f32[6144]{0:T(1024)S(1)}, f32[6144]{0:T(1024)}, u32[]{:S(2)}) copy-start(f32[6144]{0:T(1024)} %param.18) | copy-start | bytes 73732
  53.6 125.8 %all-gather.5.cloned.1.call-start = ((), (), s32[]{:S(2)}) async-start(), calls=%async_computation.6 | async-start | bytes 7077888 | tf_op jit(solution)/shard_map/all_gather | solution.py:124
  102.8 10.8 %collective-permute-start = (f32[16,6144]{1,0:T(8,128)S(1)}, f32[16,6144]{1,0:T(8,128)S(1)}, u32[]{:S(2)}, u32[]{:S(2)}) collective-permute-start(f32[16,6144]{1,0:T(8,128)S(1)} %add.142), channel_id=1, source_target_pairs={{0,1},{1,0},{2,3},{3,2},{4,5},{5,4},{6,7},{7,6},{8,9},{9,8},{10,11... | collective-permute-start | bytes 1179656 | tf_op jit(solution)/shard_map/ppermute | solution.py:34
  113.7 0.8 copy-start.2
  113.7 0.9 copy-start.3
  141.8 80.4 %all-gather.7.cloned.1.call-start = ((), (), s32[]{:S(2)}) async-start(), calls=%async_computation.8 | async-start | bytes 7077888 | tf_op jit(solution)/shard_map/all_gather | solution.py:124
  142.5 123.3 %reduce-scatter.3.cloned.1.call-start = ((), (), s32[]{:S(2)}) async-start(), calls=%async_computation.7 | async-start | bytes 7077888 | tf_op jit(solution)/shard_map/reduce_scatter | solution.py:129
  179.4 8.2 %copy-start.7 = (bf16[512,6144]{1,0:T(8,128)(2,1)S(1)}, bf16[512,6144]{1,0:T(8,128)(2,1)}, u32[]{:S(2)}) copy-start(bf16[512,6144]{1,0:T(8,128)(2,1)} %all-gather.5.cloned.1.call-done) | copy-start | bytes 18874372
  179.4 14.6 %slice-start = ((s8[6291456]{0:T(1024)(128)(4,1)}), s8[4194304]{0:T(1024)(128)(4,1)S(1)}, s32[]{:S(2)}) async-start(s8[6291456]{0:T(1024)(128)(4,1)} %bitcast.120), calls=%async_computation.11 | async-start | bytes 8388608
  187.6 6.4 %slice-start.1 = ((s8[6291456]{0:T(1024)(128)(4,1)}), s8[2097152]{0:T(1024)(128)(4,1)S(1)}, s32[]{:S(2)}) async-start(s8[6291456]{0:T(1024)(128)(4,1)} %bitcast.120), calls=%async_computation.12 | async-start | bytes 4194304
  199.5 110.9 %reduce-scatter.5.cloned.1.call-start = ((), (), s32[]{:S(2)}) async-start(), calls=%async_computation.9 | async-start | bytes 7077888 | tf_op jit(solution)/shard_map/reduce_scatter | solution.py:129
  222.2 8.2 %copy-start.6 = (bf16[512,6144]{1,0:T(8,128)(2,1)S(1)}, bf16[512,6144]{1,0:T(8,128)(2,1)}, u32[]{:S(2)}) copy-start(bf16[512,6144]{1,0:T(8,128)(2,1)} %all-gather.7.cloned.1.call-done) | copy-start | bytes 18874372
  222.2 14.7 %slice-start.2 = ((s8[6291456]{0:T(1024)(128)(4,1)}), s8[4194304]{0:T(1024)(128)(4,1)S(1)}, s32[]{:S(2)}) async-start(s8[6291456]{0:T(1024)(128)(4,1)} %bitcast.122), calls=%async_computation.13 | async-start | bytes 8388608
  230.4 6.4 %slice-start.3 = ((s8[6291456]{0:T(1024)(128)(4,1)}), s8[2097152]{0:T(1024)(128)(4,1)S(1)}, s32[]{:S(2)}) async-start(s8[6291456]{0:T(1024)(128)(4,1)} %bitcast.122), calls=%async_computation.14 | async-start | bytes 4194304
  313.1 28.8 %all-to-all-start.3 = ((bf16[8,16,6144]{2,1,0:T(8,128)(2,1)}), bf16[8,16,6144]{2,1,0:T(8,128)(2,1)S(1)}, u32[]{:S(2)}, u32[]{:S(2)}) async-start(bf16[8,16,6144]{2,1,0:T(8,128)(2,1)} %bitcast.21), calls=%async_computation.5 | async-start | bytes 3145728 | tf_op jit(solution)/shard_map/all_to_all | solution.py:131
  343.0 19.8 %collective-permute-start.1 = (bf16[64,6144]{1,0:T(8,128)(2,1)S(1)}, bf16[64,6144]{1,0:T(8,128)(2,1)}, u32[]{:S(2)}, u32[]{:S(2)}) collective-permute-start(bf16[64,6144]{1,0:T(8,128)(2,1)S(1)} %broadcast_select_fusion), channel_id=1, source_target_pairs={{0,1},{1,0},{2,3},{3,2},{4,5},{5,4},{6,7},{7,6},{8,9},{9,8},{10,11... | collective-permute-start | bytes 2359304 | tf_op jit(solution)/shard_map/ppermute | solution.py:135
Sparse Core Ops, SparseCore 0:
  9.2 29.0 all-gather.8
  141.9 37.4 all-gather.4
  181.1 41.0 all-gather.6
  224.4 41.3 reduce-scatter.2
  268.1 42.2 reduce-scatter.4

commit v3 on v2

--- a/solution.py
+++ b/solution.py
@@ -85,14 +85,18 @@
         own_spans = jnp.concatenate([first_spans, second_spans], axis=0)
         pieces.append(attend_parent(drafts[i * R : (i + 1) * R], own_keys, own_spans, span_bias, scale))
     attended = pieces[0] if parents_here == 1 else jnp.concatenate(pieces, axis=0)
-    term = jnp.dot(attended, out_weight, preferred_element_type=jnp.float32).astype(jnp.bfloat16)
+    term = jnp.dot(attended, out_weight, preferred_element_type=jnp.float32)
+    offset = lax.axis_index(("expert", "tensor")) * local_width
+    own_cols = lax.dynamic_slice(term, (0, offset), (local_rows, local_width)) + drafts.astype(
+        jnp.float32
+    )
+    term = lax.dynamic_update_slice(term, own_cols, (0, offset)).astype(jnp.bfloat16)
     group = lax.axis_size(("expert", "tensor"))
     share_rows = local_rows // group
     arrived_terms = lax.all_to_all(
         term.reshape(group, share_rows, width), ("expert", "tensor"), 0, 0, tiled=True
     )
-    own_drafts = lax.all_to_all(drafts, ("expert", "tensor"), 0, 1, tiled=True)
-    share = jnp.sum(arrived_terms.astype(jnp.float32), axis=0) + own_drafts.astype(jnp.float32)
+    share = jnp.sum(arrived_terms.astype(jnp.float32), axis=0)
     merged = pair_gather(share)
     mean_square = jnp.mean(merged * merged, axis=-1, keepdims=True)
     normed = (merged * lax.rsqrt(mean_square + 1e-05) * norm_gain).astype(jnp.bfloat16)
@@ -114,23 +118,33 @@
     place_rows = jnp.sum(place_hot.reshape(experts * capacity, tok_count, 2), axis=-1)
     outgoing = jnp.dot(place_rows, normed, preferred_element_type=jnp.float32).astype(jnp.bfloat16)
     outgoing = outgoing.reshape(experts, capacity, width)
-    arrived = lax.all_to_all(outgoing, "expert", split_axis=0, concat_axis=0, tiled=True).reshape(
-        -1, width
-    )
     chunks = 2
-    chunk_rows = arrived.shape[0] // chunks
+    chunk_slots = capacity // chunks
     returned = []
     for c in range(chunks):
-        piece = lax.all_gather(arrived[c * chunk_rows : (c + 1) * chunk_rows], "leaf", axis=0, tiled=True)
+        arrived = lax.all_to_all(
+            outgoing[:, c * chunk_slots : (c + 1) * chunk_slots],
+            "expert",
+            split_axis=0,
+            concat_axis=0,
+            tiled=True,
+        ).reshape(-1, width)
+        piece = lax.all_gather(arrived, "leaf", axis=0, tiled=True)
         gate_v = jnp.dot(piece, w_gate[0], preferred_element_type=jnp.float32)
         up_v = jnp.dot(piece, w_up[0], preferred_element_type=jnp.float32)
         hidden = (jax.nn.silu(gate_v) * up_v).astype(jnp.bfloat16)
         down = jnp.dot(hidden, w_down[0], preferred_element_type=jnp.float32).astype(jnp.bfloat16)
-        returned.append(lax.psum_scatter(down, "leaf", scatter_dimension=0, tiled=True))
-    part_rows = jnp.concatenate(returned, axis=0)
-    back = lax.all_to_all(
-        part_rows.reshape(-1, capacity, width), "expert", split_axis=0, concat_axis=0, tiled=True
-    ).reshape(-1, width)
+        part_rows = lax.psum_scatter(down, "leaf", scatter_dimension=0, tiled=True)
+        returned.append(
+            lax.all_to_all(
+                part_rows.reshape(experts, chunk_slots, width),
+                "expert",
+                split_axis=0,
+                concat_axis=0,
+                tiled=True,
+            )
+        )
+    back = jnp.concatenate(returned, axis=1).reshape(-1, width)
     picked = jnp.take(back, target, axis=0)
     other = lax.ppermute(picked, "tensor", perm=[(0, 1), (1, 0)])
     expert_out = (picked.astype(jnp.float32) + other.astype(jnp.float32)).astype(jnp.bfloat16)

time: 376 us -> 359 us (0.955)
  waiting for transfers between devices: 238 us -> 216 us
  blocking collectives: 25.1 us -> 31.5 us
    all_gather x2, waiting for transfers between devices: 59.2 us -> 45.3 us  [per_device(): piece = lax.all_gather(arrived, 'leaf', axis=0, tiled=True)]
    all_to_all x2, waiting for transfers between devices: 21.9 us -> 13.8 us  [per_device(): lax.all_to_all(part_rows.reshape(experts, chunk_slots, width), 'expert',...]
    all_gather x1, waiting for transfers between devices: 14.8 us -> 21.8 us  [per_device(): gathered = lax.all_gather(payload, 'leaf', axis=0, tiled=False)]
    reduce_scatter x2, waiting for transfers between devices: 68.1 us -> 61.5 us  [per_device(): part_rows = lax.psum_scatter(down, 'leaf', scatter_dimension=0, tiled=True)]
    all_to_all x1 -> x2, blocking collectives: 25.1 us -> 31.5 us  [per_device(): lax.all_to_all(outgoing[:, c * chunk_slots:(c + 1) * chunk_slots], 'exper...]
  transfers between devices with their start and end apart: 10 -> 10, of which waited for: 9 -> 9; matrix products, arithmetic and copies ran while one was open for 14% -> 12% of each run, Pallas kernels for 0% -> 0%
where the time goes in v3:
time: 359 us; the launch traced here: 358 us
  waiting for transfers between devices  216 us (60%)
  matrix products  45 us (13%)
  blocking collectives  31.5 us (9%)
  starting transfers between devices  24.3 us (7%)
  between operations  18.4 us (5%)
  other arithmetic  14.1 us (4%)
  local copies, waits for them, and re-layouts  8.8 us (2%)
    reduce_scatter x2, waiting for transfers between devices, per_device(): part_rows = lax.psum_scatter(down, 'leaf', scatter_dimension=0, tiled=True)  61.5 us
    all_to_all x1, waiting for transfers between devices, per_device(): lax.all_to_all(term.reshape(group, share_rows, width), ('expert', 'tensor...  47.3 us
    all_gather x2, waiting for transfers between devices, per_device(): piece = lax.all_gather(arrived, 'leaf', axis=0, tiled=True)  45.3 us
    all_to_all x2, blocking collectives, per_device(): lax.all_to_all(outgoing[:, c * chunk_slots:(c + 1) * chunk_slots], 'exper...  31.5 us
    all_gather x1, waiting for transfers between devices, per_device(): gathered = lax.all_gather(payload, 'leaf', axis=0, tiled=False)  21.8 us
    ppermute x1, waiting for transfers between devices, per_device(): other = lax.ppermute(picked, 'tensor', perm=[(0, 1), (1, 0)])  17.9 us
    dot_general x2, matrix products, per_device(): gate_v = jnp.dot(piece, w_gate[0], preferred_element_type=jnp.float32)  16.4 us
    all_to_all x2, waiting for transfers between devices, per_device(): lax.all_to_all(part_rows.reshape(experts, chunk_slots, width), 'expert',...  13.8 us
  transfers between devices with their start and end apart: 10, of which 9 were waited for; matrix products, arithmetic and copies ran while one was open for 12% of the time, Pallas kernels for 0%

profile of v3, /device:TPU:32, one launch (start us, length us, event | category | flops | bytes accessed | tf_op | source)
XLA Modules:
  0.0 358.0 jit_solution(5564254776953969372)
XLA Ops:
  7.3 1.8 pad_maximum_fusion.2
  15.3 1.1 copy.52
  16.4 21.8 %all-gather.9.cloned.1.call-done = bf16[4160,384]{1,0:T(8,128)(2,1)} async-done(((bf16[520,384]{1,0:T(8,128)(2,1)}), bf16[4160,384]{1,0:T(8,128)(2,1)}) %all-gather.9.cloned.1.call-update) | async-done | bytes 3194896 | tf_op jit(solution)/shard_map/all_gather | solution.py:66
  40.9 1.1 convolution_bitcast_fusion
  43.7 1.8 fusion.54
  45.6 2.1 convert_element_type.73
  47.7 6.9 %all-to-all-start = ((bf16[16,16,6144]{2,1,0:T(8,128)(2,1)}), bf16[16,16,6144]{2,1,0:T(8,128)(2,1)S(1)}, u32[]{:S(2)}, u32[]{:S(2)}) async-start(bf16[16,16,6144]{2,1,0:T(8,128)(2,1)} %bitcast.102), calls=%async_computation | async-start | bytes 6291456 | tf_op jit(solution)/shard_map/all_to_all | solution.py:96
  55.0 47.3 %all-to-all-done = bf16[16,16,6144]{2,1,0:T(8,128)(2,1)S(1)} async-done(((bf16[16,16,6144]{2,1,0:T(8,128)(2,1)}), bf16[16,16,6144]{2,1,0:T(8,128)(2,1)S(1)}, u32[]{:S(2)}, u32[]{:S(2)}) %all-to-all-start) | async-done | bytes 3145760 | tf_op jit(solution)/shard_map/all_to_all | solution.py:96
  102.3 1.2 convert_reduce_fusion
  103.5 2.3 collective-permute-start
  106.3 8.2 %collective-permute-done = f32[16,6144]{1,0:T(8,128)S(1)} collective-permute-done((f32[16,6144]{1,0:T(8,128)}, f32[16,6144]{1,0:T(8,128)S(1)}, u32[]{:S(2)}, u32[]{:S(2)}) %collective-permute-start) | collective-permute-done | bytes 393248 | tf_op jit(solution)/shard_map/ppermute | solution.py:34
  117.3 16.8 %all_to_all.25 = bf16[8,8,6144]{2,1,0:T(8,128)(2,1)} all-to-all(bf16[8,8,6144]{2,1,0:T(8,128)(2,1)S(1)} %get-tuple-element.11), channel_id=1, replica_groups=mesh['leaf'=8,'expert'=8,'tensor'=2] {'expert'}, dimensions={0} | all-to-all | bytes 1572864 | tf_op jit(solution)/shard_map/all_to_all | solution.py:125
  134.2 14.6 %all_to_all.26 = bf16[8,8,6144]{2,1,0:T(8,128)(2,1)} all-to-all(bf16[8,8,6144]{2,1,0:T(8,128)(2,1)S(1)} %get-tuple-element.12), channel_id=1, replica_groups=mesh['leaf'=8,'expert'=8,'tensor'=2] {'expert'}, dimensions={0} | all-to-all | bytes 1572864 | tf_op jit(solution)/shard_map/all_to_all | solution.py:125
  149.1 22.6 %all-gather.5.cloned.1.call-done = bf16[512,6144]{1,0:T(8,128)(2,1)} async-done(((bf16[64,6144]{1,0:T(8,128)(2,1)}), bf16[512,6144]{1,0:T(8,128)(2,1)}) %all-gather.5.cloned.1.call-update) | async-done | bytes 6291472 | tf_op jit(solution)/shard_map/all_gather | solution.py:132
  171.7 8.2 %fusion.8 = f32[512,512]{1,0:T(8,128)S(1)} fusion(bf16[512,6144]{1,0:T(8,128)(2,1)} %all-gather.5.cloned.1.call-done, bf16[1,6144,512]{2,1,0:T(8,128)(2,1)} %param.21), kind=kOutput, calls=%fused_computation.12 | convolution fusion | flops 3221225472 | bytes 13631488 | tf_op jit(solution)/shard_map/dot_general | solution.py:133
  180.0 6.4 %fusion.23 = bf16[512,512]{1,0:T(8,128)(2,1)S(1)} fusion(bf16[512,6144]{1,0:T(8,128)(2,1)S(1)} %copy-done.8, bf16[1,6144,512]{2,1,0:T(8,128)(2,1)} %param.22, f32[512,512]{1,0:T(8,128)S(1)} %fusion.8), kind=kOutput, calls=%fused_computation.26 | convolution fusion | flops 3222798336 | bytes 14155776 | tf_op jit(solution)/shard_map/dot_general | solution.py:134
  186.4 5.3 %convolution_convert_fusion.1 = bf16[512,6144]{1,0:T(8,128)(2,1)} fusion(bf16[512,512]{1,0:T(8,128)(2,1)S(1)} %fusion.23, bf16[1,512,6144]{2,1,0:T(8,128)(2,1)S(1)} %bitcast.117), kind=kOutput, calls=%fused_computation.2 | convolution fusion | flops 3224371200 | bytes 13107200 | tf_op jit(solution)/shard_map/dot_general | solution.py:136
  191.8 22.7 %all-gather.7.cloned.1.call-done = bf16[512,6144]{1,0:T(8,128)(2,1)} async-done(((bf16[64,6144]{1,0:T(8,128)(2,1)}), bf16[512,6144]{1,0:T(8,128)(2,1)}) %all-gather.7.cloned.1.call-update) | async-done | bytes 6291472 | tf_op jit(solution)/shard_map/all_gather | solution.py:132
  214.5 8.2 %fusion.6 = f32[512,512]{1,0:T(8,128)S(1)} fusion(bf16[512,6144]{1,0:T(8,128)(2,1)} %all-gather.7.cloned.1.call-done, bf16[1,6144,512]{2,1,0:T(8,128)(2,1)} %param.21), kind=kOutput, calls=%fused_computation.10 | convolution fusion | flops 3221225472 | bytes 13631488 | tf_op jit(solution)/shard_map/dot_general | solution.py:133
  222.7 6.4 %fusion.20 = bf16[512,512]{1,0:T(8,128)(2,1)S(1)} fusion(bf16[512,6144]{1,0:T(8,128)(2,1)S(1)} %copy-done.7, bf16[1,6144,512]{2,1,0:T(8,128)(2,1)} %param.22, f32[512,512]{1,0:T(8,128)S(1)} %fusion.6), kind=kOutput, calls=%fused_computation.25 | convolution fusion | flops 3222798336 | bytes 14155776 | tf_op jit(solution)/shard_map/dot_general | solution.py:134
  229.2 5.4 %convolution_convert_fusion = bf16[512,6144]{1,0:T(8,128)(2,1)} fusion(bf16[512,512]{1,0:T(8,128)(2,1)S(1)} %fusion.20, bf16[1,512,6144]{2,1,0:T(8,128)(2,1)S(1)} %bitcast.119), kind=kOutput, calls=%fused_computation.1 | convolution fusion | flops 3224371200 | bytes 13107200 | tf_op jit(solution)/shard_map/dot_general | solution.py:136
  234.5 23.6 %reduce-scatter.3.cloned.1.call-done = bf16[64,6144]{1,0:T(8,128)(2,1)} async-done(((bf16[512,6144]{1,0:T(8,128)(2,1)}), bf16[64,6144]{1,0:T(8,128)(2,1)}) %reduce-scatter.3.cloned.1.call-update) | async-done | bytes 786448 | tf_op jit(solution)/shard_map/reduce_scatter | solution.py:137
  258.1 6.7 %all-to-all-start.2 = ((bf16[8,8,6144]{2,1,0:T(8,128)(2,1)}), bf16[8,8,6144]{2,1,0:T(8,128)(2,1)S(1)}, u32[]{:S(2)}, u32[]{:S(2)}) async-start(bf16[8,8,6144]{2,1,0:T(8,128)(2,1)} %bitcast.107), calls=%async_computation.3 | async-start | bytes 1572864 | tf_op jit(solution)/shard_map/all_to_all | solution.py:139
  264.8 37.9 %reduce-scatter.5.cloned.1.call-done = bf16[64,6144]{1,0:T(8,128)(2,1)} async-done(((bf16[512,6144]{1,0:T(8,128)(2,1)}), bf16[64,6144]{1,0:T(8,128)(2,1)}) %reduce-scatter.5.cloned.1.call-update) | async-done | bytes 786448 | tf_op jit(solution)/shard_map/reduce_scatter | solution.py:137
  302.7 6.7 %all-to-all-start.4 = ((bf16[8,8,6144]{2,1,0:T(8,128)(2,1)}), bf16[8,8,6144]{2,1,0:T(8,128)(2,1)}, u32[]{:S(2)}, u32[]{:S(2)}) async-start(bf16[8,8,6144]{2,1,0:T(8,128)(2,1)} %bitcast.108), calls=%async_computation.6 | async-start | bytes 1572864 | tf_op jit(solution)/shard_map/all_to_all | solution.py:139
  309.6 13.8 %all-to-all-done.4 = bf16[8,8,6144]{2,1,0:T(8,128)(2,1)} async-done(((bf16[8,8,6144]{2,1,0:T(8,128)(2,1)}), bf16[8,8,6144]{2,1,0:T(8,128)(2,1)}, u32[]{:S(2)}, u32[]{:S(2)}) %all-to-all-start.4) | async-done | bytes 786464 | tf_op jit(solution)/shard_map/all_to_all | solution.py:139
  323.4 1.2 pad_maximum_fusion
  325.8 1.3 collective-permute-start.1
  327.4 17.9 %collective-permute-done.1 = bf16[64,6144]{1,0:T(8,128)(2,1)} collective-permute-done((bf16[64,6144]{1,0:T(8,128)(2,1)S(1)}, bf16[64,6144]{1,0:T(8,128)(2,1)}, u32[]{:S(2)}, u32[]{:S(2)}) %collective-permute-start.1) | collective-permute-done | bytes 786464 | tf_op jit(solution)/shard_map/ppermute | solution.py:149
  345.3 1.4 fusion.35
  347.7 1.2 fusion.51
  348.9 2.6 fusion.38
  (85 shorter events, 12.9 us)
Async XLA Ops:
  6.5 320.6 %copy-start = (bf16[6144,8]{0,1:T(8,128)(2,1)S(1)}, bf16[6144,8]{0,1:T(8,128)(2,1)}, u32[]{:S(2)}) copy-start(bf16[6144,8]{0,1:T(8,128)(2,1)} %param.19) | copy-start | bytes 294916
  6.5 31.7 %all-gather.9.cloned.1.call-start = ((), (), s32[]{:S(2)}) async-start(), calls=%async_computation.11 | async-start | bytes 3594240 | tf_op jit(solution)/shard_map/all_gather | solution.py:66
  40.8 2.9 copy-start.3
  43.6 1.8 copy-start.4
  45.6 9.1 %copy-start.6 = (s32[32,2]{0,1:T(2,128)S(1)}, s32[32,2]{0,1:T(2,128)}, u32[]{:S(2)}) copy-start(s32[32,2]{0,1:T(2,128)} %param.20) | copy-start | bytes 772
  47.7 68.8 %copy-start.5 = (f32[6144]{0:T(1024)S(1)}, f32[6144]{0:T(1024)}, u32[]{:S(2)}) copy-start(f32[6144]{0:T(1024)} %param.18) | copy-start | bytes 73732
  47.7 54.7 %all-to-all-start = ((bf16[16,16,6144]{2,1,0:T(8,128)(2,1)}), bf16[16,16,6144]{2,1,0:T(8,128)(2,1)S(1)}, u32[]{:S(2)}, u32[]{:S(2)}) async-start(bf16[16,16,6144]{2,1,0:T(8,128)(2,1)} %bitcast.102), calls=%async_computation | async-start | bytes 6291456 | tf_op jit(solution)/shard_map/all_to_all | solution.py:96
  54.6 117.1 %all-gather.5.cloned.1.call-start = ((), (), s32[]{:S(2)}) async-start(), calls=%async_computation.7 | async-start | bytes 7077888 | tf_op jit(solution)/shard_map/all_gather | solution.py:132
  103.5 11.0 %collective-permute-start = (f32[16,6144]{1,0:T(8,128)}, f32[16,6144]{1,0:T(8,128)S(1)}, u32[]{:S(2)}, u32[]{:S(2)}) collective-permute-start(f32[16,6144]{1,0:T(8,128)} %convert_reduce_fusion), channel_id=1, source_target_pairs={{0,1},{1,0},{2,3},{3,2},{4,5},{5,4},{6,7},{7,6},{8,9},{9,8},{10,11... | collective-permute-start | bytes 1179656 | tf_op jit(solution)/shard_map/ppermute | solution.py:34
  115.5 0.8 copy-start.1
  115.6 0.9 copy-start.2
  134.1 80.3 %all-gather.7.cloned.1.call-start = ((), (), s32[]{:S(2)}) async-start(), calls=%async_computation.9 | async-start | bytes 7077888 | tf_op jit(solution)/shard_map/all_gather | solution.py:132
  148.9 109.3 %reduce-scatter.3.cloned.1.call-start = ((), (), s32[]{:S(2)}) async-start(), calls=%async_computation.8 | async-start | bytes 7077888 | tf_op jit(solution)/shard_map/reduce_scatter | solution.py:137
  171.7 8.2 %copy-start.8 = (bf16[512,6144]{1,0:T(8,128)(2,1)S(1)}, bf16[512,6144]{1,0:T(8,128)(2,1)}, u32[]{:S(2)}) copy-start(bf16[512,6144]{1,0:T(8,128)(2,1)} %all-gather.5.cloned.1.call-done) | copy-start | bytes 18874372
  171.7 14.7 %slice-start = ((s8[6291456]{0:T(1024)(128)(4,1)}), s8[4194304]{0:T(1024)(128)(4,1)S(1)}, s32[]{:S(2)}) async-start(s8[6291456]{0:T(1024)(128)(4,1)} %bitcast.116), calls=%async_computation.12 | async-start | bytes 8388608
  180.0 6.5 %slice-start.1 = ((s8[6291456]{0:T(1024)(128)(4,1)}), s8[2097152]{0:T(1024)(128)(4,1)S(1)}, s32[]{:S(2)}) async-start(s8[6291456]{0:T(1024)(128)(4,1)} %bitcast.116), calls=%async_computation.13 | async-start | bytes 4194304
  191.8 111.0 %reduce-scatter.5.cloned.1.call-start = ((), (), s32[]{:S(2)}) async-start(), calls=%async_computation.10 | async-start | bytes 7077888 | tf_op jit(solution)/shard_map/reduce_scatter | solution.py:137
  214.5 8.2 %copy-start.7 = (bf16[512,6144]{1,0:T(8,128)(2,1)S(1)}, bf16[512,6144]{1,0:T(8,128)(2,1)}, u32[]{:S(2)}) copy-start(bf16[512,6144]{1,0:T(8,128)(2,1)} %all-gather.7.cloned.1.call-done) | copy-start | bytes 18874372
  214.5 14.6 %slice-start.2 = ((s8[6291456]{0:T(1024)(128)(4,1)}), s8[4194304]{0:T(1024)(128)(4,1)S(1)}, s32[]{:S(2)}) async-start(s8[6291456]{0:T(1024)(128)(4,1)} %bitcast.118), calls=%async_computation.14 | async-start | bytes 8388608
  222.7 6.4 %slice-start.3 = ((s8[6291456]{0:T(1024)(128)(4,1)}), s8[2097152]{0:T(1024)(128)(4,1)S(1)}, s32[]{:S(2)}) async-start(s8[6291456]{0:T(1024)(128)(4,1)} %bitcast.118), calls=%async_computation.15 | async-start | bytes 4194304
  258.1 44.6 %all-to-all-start.2 = ((bf16[8,8,6144]{2,1,0:T(8,128)(2,1)}), bf16[8,8,6144]{2,1,0:T(8,128)(2,1)S(1)}, u32[]{:S(2)}, u32[]{:S(2)}) async-start(bf16[8,8,6144]{2,1,0:T(8,128)(2,1)} %bitcast.107), calls=%async_computation.3 | async-start | bytes 1572864 | tf_op jit(solution)/shard_map/all_to_all | solution.py:139
  302.7 20.7 %all-to-all-start.4 = ((bf16[8,8,6144]{2,1,0:T(8,128)(2,1)}), bf16[8,8,6144]{2,1,0:T(8,128)(2,1)}, u32[]{:S(2)}, u32[]{:S(2)}) async-start(bf16[8,8,6144]{2,1,0:T(8,128)(2,1)} %bitcast.108), calls=%async_computation.6 | async-start | bytes 1572864 | tf_op jit(solution)/shard_map/all_to_all | solution.py:139
  325.8 19.5 %collective-permute-start.1 = (bf16[64,6144]{1,0:T(8,128)(2,1)S(1)}, bf16[64,6144]{1,0:T(8,128)(2,1)}, u32[]{:S(2)}, u32[]{:S(2)}) collective-permute-start(bf16[64,6144]{1,0:T(8,128)(2,1)S(1)} %broadcast_select_fusion), channel_id=1, source_target_pairs={{0,1},{1,0},{2,3},{3,2},{4,5},{5,4},{6,7},{7,6},{8,9},{9,8},{10,11... | collective-permute-start | bytes 2359304 | tf_op jit(solution)/shard_map/ppermute | solution.py:149
Sparse Core Ops, SparseCore 0:
  9.2 29.0 all-gather.8
  134.3 37.4 all-gather.4
  173.4 41.0 all-gather.6
  216.8 41.3 reduce-scatter.2
  260.4 42.2 reduce-scatter.4

commit v4 on v3

--- a/solution.py
+++ b/solution.py
@@ -34,6 +34,38 @@
     other = lax.ppermute(share, "tensor", perm=[(0, 1), (1, 0)])
     low = lax.axis_index("tensor") == 0
     return jnp.concatenate([jnp.where(low, share, other), jnp.where(low, other, share)], axis=0)
+
+
+def ring_reduce_leaf(x):
+    rows, width = x.shape
+    n_leaf = lax.axis_size("leaf")
+    n_z = n_leaf // 2
+    index = lax.axis_index("leaf")
+    core = index % 2
+    z = index // 2
+    block = rows // n_leaf
+    grid = x.reshape(n_z, 2, block, width)
+    mine = jnp.where(core == 0, grid[:, 0], grid[:, 1])
+    other = jnp.where(core == 0, grid[:, 1], grid[:, 0])
+    arrived = lax.ppermute(other, "leaf", perm=[(j, j ^ 1) for j in range(n_leaf)])
+    chip = mine.astype(jnp.float32) + arrived.astype(jnp.float32)
+    half = width // 2
+    east = chip[:, :, :half]
+    west = chip[:, :, half:]
+    fwd = [(a * 2 + b, ((a + 1) % n_z) * 2 + b) for a in range(n_z) for b in range(2)]
+    bwd = [(a * 2 + b, ((a - 1) % n_z) * 2 + b) for a in range(n_z) for b in range(2)]
+
+    def pick(table, at):
+        return lax.dynamic_index_in_dim(table, at % n_z, 0, keepdims=False)
+
+    acc_f = pick(east, z - 1)
+    acc_b = pick(west, z + 1)
+    for step in range(1, n_z):
+        got_f = lax.ppermute(acc_f.astype(jnp.bfloat16), "leaf", perm=fwd)
+        got_b = lax.ppermute(acc_b.astype(jnp.bfloat16), "leaf", perm=bwd)
+        acc_f = got_f.astype(jnp.float32) + pick(east, z - 1 - step)
+        acc_b = got_b.astype(jnp.float32) + pick(west, z + 1 + step)
+    return jnp.concatenate([acc_f, acc_b], axis=1).astype(jnp.bfloat16)
 
 
 def per_device(
@@ -134,7 +166,10 @@
         up_v = jnp.dot(piece, w_up[0], preferred_element_type=jnp.float32)
         hidden = (jax.nn.silu(gate_v) * up_v).astype(jnp.bfloat16)
         down = jnp.dot(hidden, w_down[0], preferred_element_type=jnp.float32).astype(jnp.bfloat16)
-        part_rows = lax.psum_scatter(down, "leaf", scatter_dimension=0, tiled=True)
+        if c == 0:
+            part_rows = ring_reduce_leaf(down)
+        else:
+            part_rows = lax.psum_scatter(down, "leaf", scatter_dimension=0, tiled=True)
         returned.append(
             lax.all_to_all(
                 part_rows.reshape(experts, chunk_slots, width),

time: 359 us -> 368 us (1.025); the launches traced: 358 us -> 363 us
  waiting for transfers between devices: 216 us -> 193 us
  blocking collectives: 31.5 us -> 50.2 us
  other arithmetic: 14.1 us -> 22.9 us
  local copies, waits for them, and re-layouts: 8.8 us -> 13.4 us
  starting transfers between devices: 24.3 us -> 20.3 us
    reduce_scatter x2 -> x1, waiting for transfers between devices: 61.5 us -> 0.01 us  [per_device(): part_rows = lax.psum_scatter(down, 'leaf', scatter_dimension=0, tiled=True)]
    ppermute x0 -> x7, waiting for transfers between devices: none -> 46.1 us  [the longest x3 40.3 us: ring_reduce_leaf(): got_b = lax.ppermute(acc_b.astype(jnp.bfloat16), 'leaf', perm=bwd)]
    all_to_all x0 -> x1, blocking collectives: none -> 18.8 us  [per_device(): lax.all_to_all(part_rows.reshape(experts, chunk_slots, width), 'expert',...]
    all_to_all x2 -> x1, starting transfers between devices: 13.4 us -> 3.55 us  [per_device(): lax.all_to_all(part_rows.reshape(experts, chunk_slots, width), 'expert',...]
    ppermute x0 -> x7, starting transfers between devices: none -> 6.51 us  [the longest x3 4.68 us: ring_reduce_leaf(): got_b = lax.ppermute(acc_b.astype(jnp.bfloat16), 'leaf', perm=bwd)]
    select_n x0 -> x1, other arithmetic: none -> 4.83 us  [ring_reduce_leaf(): other = jnp.where(core == 0, grid[:, 1], grid[:, 0])]
    add x0 -> x1, other arithmetic: none -> 4.43 us  [ring_reduce_leaf(): chip = mine.astype(jnp.float32) + arrived.astype(jnp.float32)]
    ppermute x1, waiting for transfers between devices: 17.9 us -> 13.8 us  [per_device(): other = lax.ppermute(picked, 'tensor', perm=[(0, 1), (1, 0)])]
  transfers between devices with their start and end apart: 10 -> 15, of which waited for: 9 -> 12; matrix products, arithmetic and copies ran while one was open for 12% -> 10% of each run, Pallas kernels for 0% -> 0%
where the time goes in v4:
time: 368 us; the launch traced here: 363 us
  waiting for transfers between devices  193 us (52%)
  blocking collectives  50.2 us (14%)
  matrix products  44.2 us (12%)
  other arithmetic  22.9 us (6%)
  starting transfers between devices  20.3 us (6%)
  between operations  19 us (5%)
  local copies, waits for them, and re-layouts  13.4 us (4%)
    all_to_all x1, waiting for transfers between devices, per_device(): lax.all_to_all(term.reshape(group, share_rows, width), ('expert', 'tensor...  47.3 us
    all_gather x2, waiting for transfers between devices, per_device(): piece = lax.all_gather(arrived, 'leaf', axis=0, tiled=True)  45.4 us
    ppermute x3, waiting for transfers between devices, ring_reduce_leaf(): got_b = lax.ppermute(acc_b.astype(jnp.bfloat16), 'leaf', perm=bwd)  40.3 us
    all_to_all x2, blocking collectives, per_device(): lax.all_to_all(outgoing[:, c * chunk_slots:(c + 1) * chunk_slots], 'exper...  31.5 us
    all_gather x1, waiting for transfers between devices, per_device(): gathered = lax.all_gather(payload, 'leaf', axis=0, tiled=False)  21.3 us
    all_to_all x1, blocking collectives, per_device(): lax.all_to_all(part_rows.reshape(experts, chunk_slots, width), 'expert',...  18.8 us
    dot_general x2, matrix products, per_device(): gate_v = jnp.dot(piece, w_gate[0], preferred_element_type=jnp.float32)  16.4 us
    ppermute x1, waiting for transfers between devices, per_device(): other = lax.ppermute(picked, 'tensor', perm=[(0, 1), (1, 0)])  13.8 us
  transfers between devices with their start and end apart: 15, of which 12 were waited for; matrix products, arithmetic and copies ran while one was open for 10% of the time, Pallas kernels for 0%

profile of v4, /device:TPU:32, one launch (start us, length us, event | category | flops | bytes accessed | tf_op | source)
XLA Modules:
  0.0 362.8 jit_solution(16004888812292174793)
XLA Ops:
  7.3 1.8 pad_maximum_fusion.3
  17.0 21.3 %all-gather.9.cloned.1.call-done = bf16[4160,384]{1,0:T(8,128)(2,1)} async-done(((bf16[520,384]{1,0:T(8,128)(2,1)}), bf16[4160,384]{1,0:T(8,128)(2,1)}) %all-gather.9.cloned.1.call-update) | async-done | bytes 3194896 | tf_op jit(solution)/shard_map/all_gather | solution.py:98
  43.6 1.8 fusion.67
  45.5 2.1 convert_element_type.126
  47.6 6.9 %all-to-all-start = ((bf16[16,16,6144]{2,1,0:T(8,128)(2,1)}), bf16[16,16,6144]{2,1,0:T(8,128)(2,1)S(1)}, u32[]{:S(2)}, u32[]{:S(2)}) async-start(bf16[16,16,6144]{2,1,0:T(8,128)(2,1)} %bitcast.161), calls=%async_computation | async-start | bytes 6291456 | tf_op jit(solution)/shard_map/all_to_all | solution.py:128
  55.0 47.3 %all-to-all-done = bf16[16,16,6144]{2,1,0:T(8,128)(2,1)S(1)} async-done(((bf16[16,16,6144]{2,1,0:T(8,128)(2,1)}), bf16[16,16,6144]{2,1,0:T(8,128)(2,1)S(1)}, u32[]{:S(2)}, u32[]{:S(2)}) %all-to-all-start) | async-done | bytes 3145760 | tf_op jit(solution)/shard_map/all_to_all | solution.py:128
  103.5 2.3 collective-permute-start
  106.2 8.2 %collective-permute-done = f32[16,6144]{1,0:T(8,128)S(1)} collective-permute-done((f32[16,6144]{1,0:T(8,128)}, f32[16,6144]{1,0:T(8,128)S(1)}, u32[]{:S(2)}, u32[]{:S(2)}) %collective-permute-start) | collective-permute-done | bytes 393248 | tf_op jit(solution)/shard_map/ppermute | solution.py:34
  118.0 16.8 %all_to_all.25 = bf16[8,8,6144]{2,1,0:T(8,128)(2,1)} all-to-all(bf16[8,8,6144]{2,1,0:T(8,128)(2,1)S(1)} %get-tuple-element.13), channel_id=1, replica_groups=mesh['leaf'=8,'expert'=8,'tensor'=2] {'expert'}, dimensions={0} | all-to-all | bytes 1572864 | tf_op jit(solution)/shard_map/all_to_all | solution.py:157
  134.8 14.6 %all_to_all.26 = bf16[8,8,6144]{2,1,0:T(8,128)(2,1)} all-to-all(bf16[8,8,6144]{2,1,0:T(8,128)(2,1)S(1)} %get-tuple-element.14), channel_id=1, replica_groups=mesh['leaf'=8,'expert'=8,'tensor'=2] {'expert'}, dimensions={0} | all-to-all | bytes 1572864 | tf_op jit(solution)/shard_map/all_to_all | solution.py:157
  149.7 22.7 %all-gather.5.cloned.1.call-done = bf16[512,6144]{1,0:T(8,128)(2,1)} async-done(((bf16[64,6144]{1,0:T(8,128)(2,1)}), bf16[512,6144]{1,0:T(8,128)(2,1)}) %all-gather.5.cloned.1.call-update) | async-done | bytes 6291472 | tf_op jit(solution)/shard_map/all_gather | solution.py:164
  172.4 8.2 %fusion.8 = f32[512,512]{1,0:T(8,128)S(1)} fusion(bf16[512,6144]{1,0:T(8,128)(2,1)} %all-gather.5.cloned.1.call-done, bf16[1,6144,512]{2,1,0:T(8,128)(2,1)} %param.21), kind=kOutput, calls=%fused_computation.13 | convolution fusion | flops 3221225472 | bytes 13631488 | tf_op jit(solution)/shard_map/dot_general | solution.py:165
  180.7 6.4 %fusion.25 = bf16[512,512]{1,0:T(8,128)(2,1)S(1)} fusion(bf16[512,6144]{1,0:T(8,128)(2,1)S(1)} %copy-done.13, bf16[1,6144,512]{2,1,0:T(8,128)(2,1)} %param.22, f32[512,512]{1,0:T(8,128)S(1)} %fusion.8), kind=kOutput, calls=%fused_computation.31 | convolution fusion | flops 3222798336 | bytes 14155776 | tf_op jit(solution)/shard_map/dot_general | solution.py:166
  187.1 5.3 %convolution_convert_fusion.1 = bf16[512,6144]{1,0:T(8,128)(2,1)} fusion(bf16[512,512]{1,0:T(8,128)(2,1)S(1)} %fusion.25, bf16[1,512,6144]{2,1,0:T(8,128)(2,1)S(1)} %bitcast.175), kind=kOutput, calls=%fused_computation.2 | convolution fusion | flops 3224371200 | bytes 13107200 | tf_op jit(solution)/shard_map/dot_general | solution.py:168
  192.5 22.7 %all-gather.7.cloned.1.call-done = bf16[512,6144]{1,0:T(8,128)(2,1)} async-done(((bf16[64,6144]{1,0:T(8,128)(2,1)}), bf16[512,6144]{1,0:T(8,128)(2,1)}) %all-gather.7.cloned.1.call-update) | async-done | bytes 6291472 | tf_op jit(solution)/shard_map/all_gather | solution.py:164
  215.2 8.1 %fusion.6 = f32[512,512]{1,0:T(8,128)S(1)} fusion(bf16[512,6144]{1,0:T(8,128)(2,1)} %all-gather.7.cloned.1.call-done, bf16[1,6144,512]{2,1,0:T(8,128)(2,1)} %param.21), kind=kOutput, calls=%fused_computation.11 | convolution fusion | flops 3221225472 | bytes 13631488 | tf_op jit(solution)/shard_map/dot_general | solution.py:165
  223.4 6.4 %fusion.22 = bf16[512,512]{1,0:T(8,128)(2,1)S(1)} fusion(bf16[512,6144]{1,0:T(8,128)(2,1)S(1)} %copy-done.14, bf16[1,6144,512]{2,1,0:T(8,128)(2,1)} %param.22, f32[512,512]{1,0:T(8,128)S(1)} %fusion.6), kind=kOutput, calls=%fused_computation.30 | convolution fusion | flops 3222798336 | bytes 14155776 | tf_op jit(solution)/shard_map/dot_general | solution.py:166
  229.8 5.4 %convolution_convert_fusion = bf16[512,6144]{1,0:T(8,128)(2,1)} fusion(bf16[512,512]{1,0:T(8,128)(2,1)S(1)} %fusion.22, bf16[1,512,6144]{2,1,0:T(8,128)(2,1)S(1)} %bitcast.177), kind=kOutput, calls=%fused_computation.1 | convolution fusion | flops 3224371200 | bytes 13107200 | tf_op jit(solution)/shard_map/dot_general | solution.py:168
  235.2 4.8 %fusion.10 = bf16[4,64,6144]{2,1,0:T(8,128)(2,1)} fusion(pred[]{:T(512)S(6)} %eq.98, bf16[4,2,64,6144]{3,2,1,0:T(8,128)(2,1)} %bitcast.159), kind=kLoop, calls=%fused_computation.17 | loop fusion | flops 1572864 | bytes 9437185 | tf_op jit(solution)/shard_map/jit(_where)/select_n | solution.py:49
  240.3 5.6 %collective-permute-done.1 = bf16[4,64,6144]{2,1,0:T(8,128)(2,1)S(1)} collective-permute-done((bf16[4,64,6144]{2,1,0:T(8,128)(2,1)}, bf16[4,64,6144]{2,1,0:T(8,128)(2,1)S(1)}, u32[]{:S(2)}, u32[]{:S(2)}) %collective-permute-start.1) | collective-permute-done | bytes 3145760 | tf_op jit(solution)/shard_map/ppermute | solution.py:50
  245.9 4.4 %convert_add_fusion = f32[4,64,6144]{2,1,0:T(8,128)S(1)} fusion(bf16[4,64,6144]{2,1,0:T(8,128)(2,1)S(1)} %collective-permute-done.1, pred[]{:T(512)S(6)} %eq.98, bf16[4,2,64,6144]{3,2,1,0:T(8,128)(2,1)} %bitcast.160), kind=kLoop, calls=%fused_computation.4 | loop fusion | flops 6291456 | bytes 15728641 | tf_op jit(solution)/shard_map/add | solution.py:51
  250.9 1.7 copy-done.1
  253.4 1.5 collective-permute-start.5
  255.6 14.0 %collective-permute-done.5 = bf16[64,3072]{1,0:T(8,128)(2,1)} collective-permute-done((bf16[64,3072]{1,0:T(8,128)(2,1)}, bf16[64,3072]{1,0:T(8,128)(2,1)}, u32[]{:S(2)}, u32[]{:S(2)}) %collective-permute-start.5) | collective-permute-done | bytes 393248 | tf_op jit(solution)/shard_map/ppermute | solution.py:65
  270.9 1.6 collective-permute-start.6
  273.1 13.4 %collective-permute-done.6 = bf16[64,3072]{1,0:T(8,128)(2,1)S(1)} collective-permute-done((bf16[64,3072]{1,0:T(8,128)(2,1)S(1)}, bf16[64,3072]{1,0:T(8,128)(2,1)S(1)}, u32[]{:S(2)}, u32[]{:S(2)}) %collective-permute-start.6) | collective-permute-done | bytes 393248 | tf_op jit(solution)/shard_map/ppermute | solution.py:65
  286.6 1.6 collective-permute-start.7
  288.8 13.0 %collective-permute-done.7 = bf16[64,3072]{1,0:T(8,128)(2,1)S(1)} collective-permute-done((bf16[64,3072]{1,0:T(8,128)(2,1)S(1)}, bf16[64,3072]{1,0:T(8,128)(2,1)S(1)}, u32[]{:S(2)}, u32[]{:S(2)}) %collective-permute-start.7) | collective-permute-done | bytes 393248 | tf_op jit(solution)/shard_map/ppermute | solution.py:65
  302.0 18.8 %all_to_all.27 = bf16[8,8,6144]{2,1,0:T(8,128)(2,1)S(1)} all-to-all(bf16[8,8,6144]{2,1,0:T(8,128)(2,1)S(1)} %pad_maximum_fusion.2), channel_id=1, replica_groups=mesh['leaf'=8,'expert'=8,'tensor'=2] {'expert'}, dimensions={0} | all-to-all | bytes 1572864 | tf_op jit(solution)/shard_map/all_to_all | solution.py:174
  320.8 3.5 all-to-all-start.4
  324.5 10.6 %all-to-all-done.4 = bf16[8,8,6144]{2,1,0:T(8,128)(2,1)S(1)} async-done(((bf16[8,8,6144]{2,1,0:T(8,128)(2,1)}), bf16[8,8,6144]{2,1,0:T(8,128)(2,1)S(1)}, u32[]{:S(2)}, u32[]{:S(2)}) %all-to-all-start.4) | async-done | bytes 786464 | tf_op jit(solution)/shard_map/all_to_all | solution.py:174
  337.4 13.8 %collective-permute-done.8 = bf16[64,6144]{1,0:T(8,128)(2,1)} collective-permute-done((bf16[64,6144]{1,0:T(8,128)(2,1)S(1)}, bf16[64,6144]{1,0:T(8,128)(2,1)}, u32[]{:S(2)}, u32[]{:S(2)}) %collective-permute-start.8) | collective-permute-done | bytes 786464 | tf_op jit(solution)/shard_map/ppermute | solution.py:184
  (121 shorter events, 27.0 us)
Async XLA Ops:
  6.5 330.6 %copy-start = (bf16[6144,8]{0,1:T(8,128)(2,1)S(1)}, bf16[6144,8]{0,1:T(8,128)(2,1)}, u32[]{:S(2)}) copy-start(bf16[6144,8]{0,1:T(8,128)(2,1)} %param.19) | copy-start | bytes 294916
  6.5 34.4 %copy-start.15 = (f32[3,16]{1,0:T(4,128)S(1)}, f32[3,16]{1,0:T(4,128)}, u32[]{:S(2)}) copy-start(f32[3,16]{1,0:T(4,128)} %param.16) | copy-start | bytes 580
  6.5 31.8 %all-gather.9.cloned.1.call-start = ((), (), s32[]{:S(2)}) async-start(), calls=%async_computation.9 | async-start | bytes 3594240 | tf_op jit(solution)/shard_map/all_gather | solution.py:98
  41.3 2.4 copy-start.7
  43.6 1.8 copy-start.10
  47.6 7.0 %copy-start.12 = (s32[32,2]{0,1:T(2,128)S(1)}, s32[32,2]{0,1:T(2,128)}, u32[]{:S(2)}) copy-start(s32[32,2]{0,1:T(2,128)} %param.20) | copy-start | bytes 772
  47.6 54.7 %all-to-all-start = ((bf16[16,16,6144]{2,1,0:T(8,128)(2,1)}), bf16[16,16,6144]{2,1,0:T(8,128)(2,1)S(1)}, u32[]{:S(2)}, u32[]{:S(2)}) async-start(bf16[16,16,6144]{2,1,0:T(8,128)(2,1)} %bitcast.161), calls=%async_computation | async-start | bytes 6291456 | tf_op jit(solution)/shard_map/all_to_all | solution.py:128
  54.5 61.8 %copy-start.11 = (f32[6144]{0:T(1024)S(1)}, f32[6144]{0:T(1024)}, u32[]{:S(2)}) copy-start(f32[6144]{0:T(1024)} %param.18) | copy-start | bytes 73732
  54.6 117.8 %all-gather.5.cloned.1.call-start = ((), (), s32[]{:S(2)}) async-start(), calls=%async_computation.6 | async-start | bytes 7077888 | tf_op jit(solution)/shard_map/all_gather | solution.py:164
  103.5 11.0 %collective-permute-start = (f32[16,6144]{1,0:T(8,128)}, f32[16,6144]{1,0:T(8,128)S(1)}, u32[]{:S(2)}, u32[]{:S(2)}) collective-permute-start(f32[16,6144]{1,0:T(8,128)} %convert_reduce_fusion), channel_id=1, source_target_pairs={{0,1},{1,0},{2,3},{3,2},{4,5},{5,4},{6,7},{7,6},{8,9},{9,8},{10,11... | collective-permute-start | bytes 1179656 | tf_op jit(solution)/shard_map/ppermute | solution.py:34
  134.8 80.4 %all-gather.7.cloned.1.call-start = ((), (), s32[]{:S(2)}) async-start(), calls=%async_computation.7 | async-start | bytes 7077888 | tf_op jit(solution)/shard_map/all_gather | solution.py:164
  149.5 171.3 %reduce-scatter.2.cloned.1.call-start = ((), (), s32[]{:S(2)}) async-start(), calls=%async_computation.8 | async-start | bytes 7077888 | tf_op jit(solution)/shard_map/reduce_scatter | solution.py:172
  172.4 8.3 %copy-start.13 = (bf16[512,6144]{1,0:T(8,128)(2,1)S(1)}, bf16[512,6144]{1,0:T(8,128)(2,1)}, u32[]{:S(2)}) copy-start(bf16[512,6144]{1,0:T(8,128)(2,1)} %all-gather.5.cloned.1.call-done) | copy-start | bytes 18874372
  172.4 14.7 %slice-start = ((s8[6291456]{0:T(1024)(128)(4,1)}), s8[4194304]{0:T(1024)(128)(4,1)S(1)}, s32[]{:S(2)}) async-start(s8[6291456]{0:T(1024)(128)(4,1)} %bitcast.174), calls=%async_computation.10 | async-start | bytes 8388608
  180.7 6.5 %slice-start.1 = ((s8[6291456]{0:T(1024)(128)(4,1)}), s8[2097152]{0:T(1024)(128)(4,1)S(1)}, s32[]{:S(2)}) async-start(s8[6291456]{0:T(1024)(128)(4,1)} %bitcast.174), calls=%async_computation.11 | async-start | bytes 4194304
  215.2 8.2 %copy-start.14 = (bf16[512,6144]{1,0:T(8,128)(2,1)S(1)}, bf16[512,6144]{1,0:T(8,128)(2,1)}, u32[]{:S(2)}) copy-start(bf16[512,6144]{1,0:T(8,128)(2,1)} %all-gather.7.cloned.1.call-done) | copy-start | bytes 18874372
  215.2 14.6 %slice-start.2 = ((s8[6291456]{0:T(1024)(128)(4,1)}), s8[4194304]{0:T(1024)(128)(4,1)S(1)}, s32[]{:S(2)}) async-start(s8[6291456]{0:T(1024)(128)(4,1)} %bitcast.176), calls=%async_computation.12 | async-start | bytes 8388608
  223.4 6.5 %slice-start.3 = ((s8[6291456]{0:T(1024)(128)(4,1)}), s8[2097152]{0:T(1024)(128)(4,1)S(1)}, s32[]{:S(2)}) async-start(s8[6291456]{0:T(1024)(128)(4,1)} %bitcast.176), calls=%async_computation.13 | async-start | bytes 4194304
  240.0 5.9 %collective-permute-start.1 = (bf16[4,64,6144]{2,1,0:T(8,128)(2,1)}, bf16[4,64,6144]{2,1,0:T(8,128)(2,1)S(1)}, u32[]{:S(2)}, u32[]{:S(2)}) collective-permute-start(bf16[4,64,6144]{2,1,0:T(8,128)(2,1)} %fusion.10), channel_id=1, source_target_pairs={{0,16},{16,0},{32,48},{48,32},{64,80},{80,64},{96,112},{112,96},{1... | collective-permute-start | bytes 9437192 | tf_op jit(solution)/shard_map/ppermute | solution.py:50
  250.9 1.7 copy-start.1
  253.4 16.1 %collective-permute-start.5 = (bf16[64,3072]{1,0:T(8,128)(2,1)}, bf16[64,3072]{1,0:T(8,128)(2,1)}, u32[]{:S(2)}, u32[]{:S(2)}) collective-permute-start(bf16[64,3072]{1,0:T(8,128)(2,1)} %fusion.50), channel_id=1, source_target_pairs={{0,96},{16,112},{32,0},{48,16},{64,32},{80,48},{96,64},{112,80},{1... | collective-permute-start | bytes 1179656 | tf_op jit(solution)/shard_map/ppermute | solution.py:65
  254.9 31.6 %copy-start.2 = (f32[4,64,3072]{2,1,0:T(8,128)S(1)}, f32[4,64,3072]{2,1,0:T(8,128)}, u32[]{:S(2)}) copy-start(f32[4,64,3072]{2,1,0:T(8,128)} %copy-done.1) | copy-start | bytes 9437188
  254.9 17.6 %collective-permute-start.2 = (bf16[64,3072]{1,0:T(8,128)(2,1)S(1)}, bf16[64,3072]{1,0:T(8,128)(2,1)S(1)}, u32[]{:S(2)}, u32[]{:S(2)}) collective-permute-start(bf16[64,3072]{1,0:T(8,128)(2,1)S(1)} %fusion.49), channel_id=1, source_target_pairs={{0,32},{16,48},{32,64},{48,80},{64,96},{80,112},{96,0},{112,16},{1... | collective-permute-start | bytes 1179656 | tf_op jit(solution)/shard_map/ppermute | solution.py:64
  270.9 15.6 %collective-permute-start.6 = (bf16[64,3072]{1,0:T(8,128)(2,1)S(1)}, bf16[64,3072]{1,0:T(8,128)(2,1)S(1)}, u32[]{:S(2)}, u32[]{:S(2)}) collective-permute-start(bf16[64,3072]{1,0:T(8,128)(2,1)S(1)} %fusion.44), channel_id=1, source_target_pairs={{0,96},{16,112},{32,0},{48,16},{64,32},{80,48},{96,64},{112,80},{1... | collective-permute-start | bytes 1179656 | tf_op jit(solution)/shard_map/ppermute | solution.py:65
  272.6 15.8 %collective-permute-start.3 = (bf16[64,3072]{1,0:T(8,128)(2,1)S(1)}, bf16[64,3072]{1,0:T(8,128)(2,1)S(1)}, u32[]{:S(2)}, u32[]{:S(2)}) collective-permute-start(bf16[64,3072]{1,0:T(8,128)(2,1)S(1)} %fusion.47), channel_id=1, source_target_pairs={{0,32},{16,48},{32,64},{48,80},{64,96},{80,112},{96,0},{112,16},{1... | collective-permute-start | bytes 1179656 | tf_op jit(solution)/shard_map/ppermute | solution.py:64
  286.6 15.2 %collective-permute-start.7 = (bf16[64,3072]{1,0:T(8,128)(2,1)S(1)}, bf16[64,3072]{1,0:T(8,128)(2,1)S(1)}, u32[]{:S(2)}, u32[]{:S(2)}) collective-permute-start(bf16[64,3072]{1,0:T(8,128)(2,1)S(1)} %fusion.43), channel_id=1, source_target_pairs={{0,96},{16,112},{32,0},{48,16},{64,32},{80,48},{96,64},{112,80},{1... | collective-permute-start | bytes 1179656 | tf_op jit(solution)/shard_map/ppermute | solution.py:65
  288.4 13.4 %collective-permute-start.4 = (bf16[64,3072]{1,0:T(8,128)(2,1)S(1)}, bf16[64,3072]{1,0:T(8,128)(2,1)S(1)}, u32[]{:S(2)}, u32[]{:S(2)}) collective-permute-start(bf16[64,3072]{1,0:T(8,128)(2,1)S(1)} %fusion.46), channel_id=1, source_target_pairs={{0,32},{16,48},{32,64},{48,80},{64,96},{80,112},{96,0},{112,16},{1... | collective-permute-start | bytes 1179656 | tf_op jit(solution)/shard_map/ppermute | solution.py:64
  320.8 14.3 %all-to-all-start.4 = ((bf16[8,8,6144]{2,1,0:T(8,128)(2,1)}), bf16[8,8,6144]{2,1,0:T(8,128)(2,1)S(1)}, u32[]{:S(2)}, u32[]{:S(2)}) async-start(bf16[8,8,6144]{2,1,0:T(8,128)(2,1)} %bitcast.166), calls=%async_computation.5 | async-start | bytes 1572864 | tf_op jit(solution)/shard_map/all_to_all | solution.py:174
  335.3 1.9 copy-start.9
  336.4 14.8 %collective-permute-start.8 = (bf16[64,6144]{1,0:T(8,128)(2,1)S(1)}, bf16[64,6144]{1,0:T(8,128)(2,1)}, u32[]{:S(2)}, u32[]{:S(2)}) collective-permute-start(bf16[64,6144]{1,0:T(8,128)(2,1)S(1)} %broadcast_select_fusion), channel_id=1, source_target_pairs={{0,1},{1,0},{2,3},{3,2},{4,5},{5,4},{6,7},{7,6},{8,9},{9,8},{10,11... | collective-permute-start | bytes 2359304 | tf_op jit(solution)/shard_map/ppermute | solution.py:184
  353.6 1.2 copy-start.4
  353.6 1.2 copy-start.6
  (3 other events, 2.3 us)
Sparse Core Ops, SparseCore 0:
  9.2 29.0 all-gather.8
  134.9 37.4 all-gather.4
  174.1 41.0 all-gather.6
  235.3 65.1 reduce-scatter.1

commit v5 on v3

--- a/solution.py
+++ b/solution.py
@@ -146,10 +146,10 @@
         )
     back = jnp.concatenate(returned, axis=1).reshape(-1, width)
     picked = jnp.take(back, target, axis=0)
-    other = lax.ppermute(picked, "tensor", perm=[(0, 1), (1, 0)])
-    expert_out = (picked.astype(jnp.float32) + other.astype(jnp.float32)).astype(jnp.bfloat16)
-    picked = expert_out.astype(jnp.float32).reshape(tok_count, 2, width)
-    mixed = gates[:, 0:1] * picked[:, 0] + gates[:, 1:2] * picked[:, 1]
+    picked = picked.astype(jnp.float32).reshape(tok_count, 2, width)
+    own_mix = (gates[:, 0:1] * picked[:, 0] + gates[:, 1:2] * picked[:, 1]).astype(jnp.bfloat16)
+    other_mix = lax.ppermute(own_mix, "tensor", perm=[(0, 1), (1, 0)])
+    mixed = own_mix.astype(jnp.float32) + other_mix.astype(jnp.float32)
     return merged + mixed
 
 

time: 359 us -> 345 us (0.961)
  waiting for transfers between devices: 216 us -> 207 us
    ppermute x1, waiting for transfers between devices: 17.9 us -> 9.7 us  [per_device(): other_mix = lax.ppermute(own_mix, 'tensor', perm=[(0, 1), (1, 0)])]
  transfers between devices with their start and end apart: 10 -> 10, of which waited for: 9 -> 9; matrix products, arithmetic and copies ran while one was open for 12% -> 13% of each run, Pallas kernels for 0% -> 0%
where the time goes in v5:
time: 345 us
  waiting for transfers between devices  207 us (60%)
  matrix products  45.2 us (13%)
  blocking collectives  31.5 us (9%)
  starting transfers between devices  24.1 us (7%)
  between operations  19 us (6%)
  other arithmetic  11.9 us (3%)
  local copies, waits for them, and re-layouts  6.61 us (2%)
    reduce_scatter x2, waiting for transfers between devices, per_device(): part_rows = lax.psum_scatter(down, 'leaf', scatter_dimension=0, tiled=True)  61.2 us
    all_to_all x1, waiting for transfers between devices, per_device(): lax.all_to_all(term.reshape(group, share_rows, width), ('expert', 'tensor...  47.3 us
    all_gather x2, waiting for transfers between devices, per_device(): piece = lax.all_gather(arrived, 'leaf', axis=0, tiled=True)  45.2 us
    all_to_all x2, blocking collectives, per_device(): lax.all_to_all(outgoing[:, c * chunk_slots:(c + 1) * chunk_slots], 'exper...  31.5 us
    all_gather x1, waiting for transfers between devices, per_device(): gathered = lax.all_gather(payload, 'leaf', axis=0, tiled=False)  21.2 us
    dot_general x2, matrix products, per_device(): gate_v = jnp.dot(piece, w_gate[0], preferred_element_type=jnp.float32)  16.4 us
    all_to_all x2, waiting for transfers between devices, per_device(): lax.all_to_all(part_rows.reshape(experts, chunk_slots, width), 'expert',...  13.6 us
    all_to_all x2, starting transfers between devices, per_device(): lax.all_to_all(part_rows.reshape(experts, chunk_slots, width), 'expert',...  13.4 us
  transfers between devices with their start and end apart: 10, of which 9 were waited for; matrix products, arithmetic and copies ran while one was open for 13% of the time, Pallas kernels for 0%

profile of v5, /device:TPU:32, one launch (start us, length us, event | category | flops | bytes accessed | tf_op | source)
XLA Modules:
  0.0 344.7 jit_solution(5772840030772444562)
XLA Ops:
  7.3 1.8 pad_maximum_fusion.2
  16.0 1.1 copy.65
  17.1 21.2 %all-gather.9.cloned.1.call-done = bf16[4160,384]{1,0:T(8,128)(2,1)} async-done(((bf16[520,384]{1,0:T(8,128)(2,1)}), bf16[4160,384]{1,0:T(8,128)(2,1)}) %all-gather.9.cloned.1.call-update) | async-done | bytes 3194896 | tf_op jit(solution)/shard_map/all_gather | solution.py:66
  39.1 1.1 constant_dynamic-slice_fusion.1
  40.9 1.1 convolution_bitcast_fusion
  43.7 1.8 fusion.54
  45.6 2.1 convert_element_type.76
  47.7 6.9 %all-to-all-start = ((bf16[16,16,6144]{2,1,0:T(8,128)(2,1)}), bf16[16,16,6144]{2,1,0:T(8,128)(2,1)S(1)}, u32[]{:S(2)}, u32[]{:S(2)}) async-start(bf16[16,16,6144]{2,1,0:T(8,128)(2,1)} %bitcast.106), calls=%async_computation | async-start | bytes 6291456 | tf_op jit(solution)/shard_map/all_to_all | solution.py:96
  55.0 47.3 %all-to-all-done = bf16[16,16,6144]{2,1,0:T(8,128)(2,1)S(1)} async-done(((bf16[16,16,6144]{2,1,0:T(8,128)(2,1)}), bf16[16,16,6144]{2,1,0:T(8,128)(2,1)S(1)}, u32[]{:S(2)}, u32[]{:S(2)}) %all-to-all-start) | async-done | bytes 3145760 | tf_op jit(solution)/shard_map/all_to_all | solution.py:96
  102.4 1.2 convert_reduce_fusion
  103.5 2.3 collective-permute-start
  106.3 8.2 %collective-permute-done = f32[16,6144]{1,0:T(8,128)S(1)} collective-permute-done((f32[16,6144]{1,0:T(8,128)}, f32[16,6144]{1,0:T(8,128)S(1)}, u32[]{:S(2)}, u32[]{:S(2)}) %collective-permute-start) | collective-permute-done | bytes 393248 | tf_op jit(solution)/shard_map/ppermute | solution.py:34
  114.5 1.0 broadcast_select_fusion.1
  116.6 16.8 %all_to_all.25 = bf16[8,8,6144]{2,1,0:T(8,128)(2,1)} all-to-all(bf16[8,8,6144]{2,1,0:T(8,128)(2,1)S(1)} %get-tuple-element.11), channel_id=1, replica_groups=mesh['leaf'=8,'expert'=8,'tensor'=2] {'expert'}, dimensions={0} | all-to-all | bytes 1572864 | tf_op jit(solution)/shard_map/all_to_all | solution.py:125
  133.5 14.6 %all_to_all.26 = bf16[8,8,6144]{2,1,0:T(8,128)(2,1)} all-to-all(bf16[8,8,6144]{2,1,0:T(8,128)(2,1)S(1)} %get-tuple-element.12), channel_id=1, replica_groups=mesh['leaf'=8,'expert'=8,'tensor'=2] {'expert'}, dimensions={0} | all-to-all | bytes 1572864 | tf_op jit(solution)/shard_map/all_to_all | solution.py:125
  148.4 22.6 %all-gather.5.cloned.1.call-done = bf16[512,6144]{1,0:T(8,128)(2,1)} async-done(((bf16[64,6144]{1,0:T(8,128)(2,1)}), bf16[512,6144]{1,0:T(8,128)(2,1)}) %all-gather.5.cloned.1.call-update) | async-done | bytes 6291472 | tf_op jit(solution)/shard_map/all_gather | solution.py:132
  171.0 8.2 %fusion.8 = f32[512,512]{1,0:T(8,128)S(1)} fusion(bf16[512,6144]{1,0:T(8,128)(2,1)} %all-gather.5.cloned.1.call-done, bf16[1,6144,512]{2,1,0:T(8,128)(2,1)} %param.21), kind=kOutput, calls=%fused_computation.12 | convolution fusion | flops 3221225472 | bytes 13631488 | tf_op jit(solution)/shard_map/dot_general | solution.py:133
  179.3 6.4 %fusion.23 = bf16[512,512]{1,0:T(8,128)(2,1)S(1)} fusion(bf16[512,6144]{1,0:T(8,128)(2,1)S(1)} %copy-done.6, bf16[1,6144,512]{2,1,0:T(8,128)(2,1)} %param.22, f32[512,512]{1,0:T(8,128)S(1)} %fusion.8), kind=kOutput, calls=%fused_computation.25 | convolution fusion | flops 3222798336 | bytes 14155776 | tf_op jit(solution)/shard_map/dot_general | solution.py:134
  185.8 5.4 %convolution_convert_fusion.1 = bf16[512,6144]{1,0:T(8,128)(2,1)} fusion(bf16[512,512]{1,0:T(8,128)(2,1)S(1)} %fusion.23, bf16[1,512,6144]{2,1,0:T(8,128)(2,1)S(1)} %bitcast.121), kind=kOutput, calls=%fused_computation.2 | convolution fusion | flops 3224371200 | bytes 13107200 | tf_op jit(solution)/shard_map/dot_general | solution.py:136
  191.2 22.6 %all-gather.7.cloned.1.call-done = bf16[512,6144]{1,0:T(8,128)(2,1)} async-done(((bf16[64,6144]{1,0:T(8,128)(2,1)}), bf16[512,6144]{1,0:T(8,128)(2,1)}) %all-gather.7.cloned.1.call-update) | async-done | bytes 6291472 | tf_op jit(solution)/shard_map/all_gather | solution.py:132
  213.8 8.2 %fusion.6 = f32[512,512]{1,0:T(8,128)S(1)} fusion(bf16[512,6144]{1,0:T(8,128)(2,1)} %all-gather.7.cloned.1.call-done, bf16[1,6144,512]{2,1,0:T(8,128)(2,1)} %param.21), kind=kOutput, calls=%fused_computation.10 | convolution fusion | flops 3221225472 | bytes 13631488 | tf_op jit(solution)/shard_map/dot_general | solution.py:133
  222.0 6.4 %fusion.20 = bf16[512,512]{1,0:T(8,128)(2,1)S(1)} fusion(bf16[512,6144]{1,0:T(8,128)(2,1)S(1)} %copy-done.5, bf16[1,6144,512]{2,1,0:T(8,128)(2,1)} %param.22, f32[512,512]{1,0:T(8,128)S(1)} %fusion.6), kind=kOutput, calls=%fused_computation.24 | convolution fusion | flops 3222798336 | bytes 14155776 | tf_op jit(solution)/shard_map/dot_general | solution.py:134
  228.5 5.4 %convolution_convert_fusion = bf16[512,6144]{1,0:T(8,128)(2,1)} fusion(bf16[512,512]{1,0:T(8,128)(2,1)S(1)} %fusion.20, bf16[1,512,6144]{2,1,0:T(8,128)(2,1)S(1)} %bitcast.123), kind=kOutput, calls=%fused_computation.1 | convolution fusion | flops 3224371200 | bytes 13107200 | tf_op jit(solution)/shard_map/dot_general | solution.py:136
  233.9 23.5 %reduce-scatter.3.cloned.1.call-done = bf16[64,6144]{1,0:T(8,128)(2,1)} async-done(((bf16[512,6144]{1,0:T(8,128)(2,1)}), bf16[64,6144]{1,0:T(8,128)(2,1)}) %reduce-scatter.3.cloned.1.call-update) | async-done | bytes 786448 | tf_op jit(solution)/shard_map/reduce_scatter | solution.py:137
  257.5 6.7 %all-to-all-start.2 = ((bf16[8,8,6144]{2,1,0:T(8,128)(2,1)}), bf16[8,8,6144]{2,1,0:T(8,128)(2,1)S(1)}, u32[]{:S(2)}, u32[]{:S(2)}) async-start(bf16[8,8,6144]{2,1,0:T(8,128)(2,1)} %bitcast.112), calls=%async_computation.3 | async-start | bytes 1572864 | tf_op jit(solution)/shard_map/all_to_all | solution.py:139
  264.4 37.6 %reduce-scatter.5.cloned.1.call-done = bf16[64,6144]{1,0:T(8,128)(2,1)} async-done(((bf16[512,6144]{1,0:T(8,128)(2,1)}), bf16[64,6144]{1,0:T(8,128)(2,1)}) %reduce-scatter.5.cloned.1.call-update) | async-done | bytes 786448 | tf_op jit(solution)/shard_map/reduce_scatter | solution.py:137
  302.0 6.7 %all-to-all-start.4 = ((bf16[8,8,6144]{2,1,0:T(8,128)(2,1)}), bf16[8,8,6144]{2,1,0:T(8,128)(2,1)}, u32[]{:S(2)}, u32[]{:S(2)}) async-start(bf16[8,8,6144]{2,1,0:T(8,128)(2,1)} %bitcast.111), calls=%async_computation.6 | async-start | bytes 1572864 | tf_op jit(solution)/shard_map/all_to_all | solution.py:139
  309.1 13.6 %all-to-all-done.4 = bf16[8,8,6144]{2,1,0:T(8,128)(2,1)} async-done(((bf16[8,8,6144]{2,1,0:T(8,128)(2,1)}), bf16[8,8,6144]{2,1,0:T(8,128)(2,1)}, u32[]{:S(2)}, u32[]{:S(2)}) %all-to-all-start.4) | async-done | bytes 786464 | tf_op jit(solution)/shard_map/all_to_all | solution.py:139
  322.7 1.2 pad_maximum_fusion
  326.2 1.1 collective-permute-start.1
  327.2 9.7 %collective-permute-done.1 = bf16[32,6144]{1,0:T(8,128)(2,1)S(1)} collective-permute-done((bf16[32,6144]{1,0:T(8,128)(2,1)S(1)}, bf16[32,6144]{1,0:T(8,128)(2,1)S(1)}, u32[]{:S(2)}, u32[]{:S(2)}) %collective-permute-start.1) | collective-permute-done | bytes 393248 | tf_op jit(solution)/shard_map/ppermute | solution.py:151
  336.9 1.2 add_add_fusion
  (81 shorter events, 10.4 us)
Async XLA Ops:
  6.5 302.2 %copy-start = (bf16[6144,8]{0,1:T(8,128)(2,1)S(1)}, bf16[6144,8]{0,1:T(8,128)(2,1)}, u32[]{:S(2)}) copy-start(bf16[6144,8]{0,1:T(8,128)(2,1)} %param.19) | copy-start | bytes 294916
  6.5 31.7 %all-gather.9.cloned.1.call-start = ((), (), s32[]{:S(2)}) async-start(), calls=%async_computation.11 | async-start | bytes 3594240 | tf_op jit(solution)/shard_map/all_gather | solution.py:66
  40.8 2.9 copy-start.1
  43.6 1.8 copy-start.2
  45.6 9.1 %copy-start.4 = (s32[32,2]{0,1:T(2,128)S(1)}, s32[32,2]{0,1:T(2,128)}, u32[]{:S(2)}) copy-start(s32[32,2]{0,1:T(2,128)} %param.20) | copy-start | bytes 772
  47.7 68.1 %copy-start.3 = (f32[6144]{0:T(1024)S(1)}, f32[6144]{0:T(1024)}, u32[]{:S(2)}) copy-start(f32[6144]{0:T(1024)} %param.18) | copy-start | bytes 73732
  47.7 54.7 %all-to-all-start = ((bf16[16,16,6144]{2,1,0:T(8,128)(2,1)}), bf16[16,16,6144]{2,1,0:T(8,128)(2,1)S(1)}, u32[]{:S(2)}, u32[]{:S(2)}) async-start(bf16[16,16,6144]{2,1,0:T(8,128)(2,1)} %bitcast.106), calls=%async_computation | async-start | bytes 6291456 | tf_op jit(solution)/shard_map/all_to_all | solution.py:96
  54.6 116.4 %all-gather.5.cloned.1.call-start = ((), (), s32[]{:S(2)}) async-start(), calls=%async_computation.7 | async-start | bytes 7077888 | tf_op jit(solution)/shard_map/all_gather | solution.py:132
  103.5 11.0 %collective-permute-start = (f32[16,6144]{1,0:T(8,128)}, f32[16,6144]{1,0:T(8,128)S(1)}, u32[]{:S(2)}, u32[]{:S(2)}) collective-permute-start(f32[16,6144]{1,0:T(8,128)} %convert_reduce_fusion), channel_id=1, source_target_pairs={{0,1},{1,0},{2,3},{3,2},{4,5},{5,4},{6,7},{7,6},{8,9},{9,8},{10,11... | collective-permute-start | bytes 1179656 | tf_op jit(solution)/shard_map/ppermute | solution.py:34
  133.5 80.3 %all-gather.7.cloned.1.call-start = ((), (), s32[]{:S(2)}) async-start(), calls=%async_computation.9 | async-start | bytes 7077888 | tf_op jit(solution)/shard_map/all_gather | solution.py:132
  148.2 109.3 %reduce-scatter.3.cloned.1.call-start = ((), (), s32[]{:S(2)}) async-start(), calls=%async_computation.8 | async-start | bytes 7077888 | tf_op jit(solution)/shard_map/reduce_scatter | solution.py:137
  171.0 8.3 %copy-start.6 = (bf16[512,6144]{1,0:T(8,128)(2,1)S(1)}, bf16[512,6144]{1,0:T(8,128)(2,1)}, u32[]{:S(2)}) copy-start(bf16[512,6144]{1,0:T(8,128)(2,1)} %all-gather.5.cloned.1.call-done) | copy-start | bytes 18874372
  171.0 14.7 %slice-start = ((s8[6291456]{0:T(1024)(128)(4,1)}), s8[4194304]{0:T(1024)(128)(4,1)S(1)}, s32[]{:S(2)}) async-start(s8[6291456]{0:T(1024)(128)(4,1)} %bitcast.120), calls=%async_computation.12 | async-start | bytes 8388608
  179.3 6.5 %slice-start.1 = ((s8[6291456]{0:T(1024)(128)(4,1)}), s8[2097152]{0:T(1024)(128)(4,1)S(1)}, s32[]{:S(2)}) async-start(s8[6291456]{0:T(1024)(128)(4,1)} %bitcast.120), calls=%async_computation.13 | async-start | bytes 4194304
  191.2 110.8 %reduce-scatter.5.cloned.1.call-start = ((), (), s32[]{:S(2)}) async-start(), calls=%async_computation.10 | async-start | bytes 7077888 | tf_op jit(solution)/shard_map/reduce_scatter | solution.py:137
  213.8 8.2 %copy-start.5 = (bf16[512,6144]{1,0:T(8,128)(2,1)S(1)}, bf16[512,6144]{1,0:T(8,128)(2,1)}, u32[]{:S(2)}) copy-start(bf16[512,6144]{1,0:T(8,128)(2,1)} %all-gather.7.cloned.1.call-done) | copy-start | bytes 18874372
  213.8 14.6 %slice-start.2 = ((s8[6291456]{0:T(1024)(128)(4,1)}), s8[4194304]{0:T(1024)(128)(4,1)S(1)}, s32[]{:S(2)}) async-start(s8[6291456]{0:T(1024)(128)(4,1)} %bitcast.122), calls=%async_computation.14 | async-start | bytes 8388608
  222.0 6.5 %slice-start.3 = ((s8[6291456]{0:T(1024)(128)(4,1)}), s8[2097152]{0:T(1024)(128)(4,1)S(1)}, s32[]{:S(2)}) async-start(s8[6291456]{0:T(1024)(128)(4,1)} %bitcast.122), calls=%async_computation.15 | async-start | bytes 4194304
  257.5 44.6 %all-to-all-start.2 = ((bf16[8,8,6144]{2,1,0:T(8,128)(2,1)}), bf16[8,8,6144]{2,1,0:T(8,128)(2,1)S(1)}, u32[]{:S(2)}, u32[]{:S(2)}) async-start(bf16[8,8,6144]{2,1,0:T(8,128)(2,1)} %bitcast.112), calls=%async_computation.3 | async-start | bytes 1572864 | tf_op jit(solution)/shard_map/all_to_all | solution.py:139
  302.0 20.7 %all-to-all-start.4 = ((bf16[8,8,6144]{2,1,0:T(8,128)(2,1)}), bf16[8,8,6144]{2,1,0:T(8,128)(2,1)}, u32[]{:S(2)}, u32[]{:S(2)}) async-start(bf16[8,8,6144]{2,1,0:T(8,128)(2,1)} %bitcast.111), calls=%async_computation.6 | async-start | bytes 1572864 | tf_op jit(solution)/shard_map/all_to_all | solution.py:139
  326.2 10.8 %collective-permute-start.1 = (bf16[32,6144]{1,0:T(8,128)(2,1)S(1)}, bf16[32,6144]{1,0:T(8,128)(2,1)S(1)}, u32[]{:S(2)}, u32[]{:S(2)}) collective-permute-start(bf16[32,6144]{1,0:T(8,128)(2,1)S(1)} %fusion.37), channel_id=1, source_target_pairs={{0,1},{1,0},{2,3},{3,2},{4,5},{5,4},{6,7},{7,6},{8,9},{9,8},{10,11... | collective-permute-start | bytes 1179656 | tf_op jit(solution)/shard_map/ppermute | solution.py:151
Sparse Core Ops, SparseCore 0:
  9.2 29.0 all-gather.8
  133.6 37.3 all-gather.4
  172.7 41.0 all-gather.6
  216.1 41.3 reduce-scatter.2
  259.7 42.2 reduce-scatter.4

commit v6 on v5

--- a/solution.py
+++ b/solution.py
@@ -97,9 +97,8 @@
         term.reshape(group, share_rows, width), ("expert", "tensor"), 0, 0, tiled=True
     )
     share = jnp.sum(arrived_terms.astype(jnp.float32), axis=0)
-    merged = pair_gather(share)
-    mean_square = jnp.mean(merged * merged, axis=-1, keepdims=True)
-    normed = (merged * lax.rsqrt(mean_square + 1e-05) * norm_gain).astype(jnp.bfloat16)
+    mean_square = jnp.mean(share * share, axis=-1, keepdims=True)
+    normed = pair_gather((share * lax.rsqrt(mean_square + 1e-05) * norm_gain).astype(jnp.bfloat16))
     logits = jnp.dot(normed, router, preferred_element_type=jnp.float32)
     experts = router.shape[1]
     tok_count = routes.shape[0]
@@ -130,6 +129,11 @@
             tiled=True,
         ).reshape(-1, width)
         piece = lax.all_gather(arrived, "leaf", axis=0, tiled=True)
+        if c == 0:
+            piece, share = lax.optimization_barrier((piece, share))
+            other_share = lax.ppermute(share, "tensor", perm=[(0, 1), (1, 0)])
+        else:
+            piece, other_share = lax.optimization_barrier((piece, other_share))
         gate_v = jnp.dot(piece, w_gate[0], preferred_element_type=jnp.float32)
         up_v = jnp.dot(piece, w_up[0], preferred_element_type=jnp.float32)
         hidden = (jax.nn.silu(gate_v) * up_v).astype(jnp.bfloat16)
@@ -145,6 +149,10 @@
             )
         )
     back = jnp.concatenate(returned, axis=1).reshape(-1, width)
+    low = lax.axis_index("tensor") == 0
+    merged = jnp.concatenate(
+        [jnp.where(low, share, other_share), jnp.where(low, other_share, share)], axis=0
+    )
     picked = jnp.take(back, target, axis=0)
     picked = picked.astype(jnp.float32).reshape(tok_count, 2, width)
     own_mix = (gates[:, 0:1] * picked[:, 0] + gates[:, 1:2] * picked[:, 1]).astype(jnp.bfloat16)

time: 345 us -> 341 us (0.988)
  waiting for transfers between devices: 207 us -> 201 us
    ppermute x1, waiting for transfers between devices: 8.18 us -> 4.13 us  [pair_gather(): other = lax.ppermute(share, 'tensor', perm=[(0, 1), (1, 0)])]
  transfers between devices with their start and end apart: 10 -> 11, of which waited for: 9 -> 9; matrix products, arithmetic and copies ran while one was open for 13% -> 13% of each run, Pallas kernels for 0% -> 0%
where the time goes in v6:
time: 341 us; the launch traced here: 340 us
  waiting for transfers between devices  201 us (59%)
  matrix products  43.8 us (13%)
  blocking collectives  31.5 us (9%)
  starting transfers between devices  25.7 us (8%)
  between operations  18.6 us (5%)
  other arithmetic  11.2 us (3%)
  local copies, waits for them, and re-layouts  8.08 us (2%)
    reduce_scatter x2, waiting for transfers between devices, per_device(): part_rows = lax.psum_scatter(down, 'leaf', scatter_dimension=0, tiled=True)  62.5 us
    all_to_all x1, waiting for transfers between devices, per_device(): lax.all_to_all(term.reshape(group, share_rows, width), ('expert', 'tensor...  46.9 us
    all_gather x2, waiting for transfers between devices, per_device(): piece = lax.all_gather(arrived, 'leaf', axis=0, tiled=True)  43 us
    all_to_all x2, blocking collectives, per_device(): lax.all_to_all(outgoing[:, c * chunk_slots:(c + 1) * chunk_slots], 'exper...  31.5 us
    all_gather x1, waiting for transfers between devices, per_device(): gathered = lax.all_gather(payload, 'leaf', axis=0, tiled=False)  21.6 us
    dot_general x2, matrix products, per_device(): up_v = jnp.dot(piece, w_up[0], preferred_element_type=jnp.float32)  14 us
    dot_general x2, matrix products, per_device(): gate_v = jnp.dot(piece, w_gate[0], preferred_element_type=jnp.float32)  14 us
    all_to_all x2, waiting for transfers between devices, per_device(): lax.all_to_all(part_rows.reshape(experts, chunk_slots, width), 'expert',...  13.6 us
  transfers between devices with their start and end apart: 11, of which 9 were waited for; matrix products, arithmetic and copies ran while one was open for 13% of the time, Pallas kernels for 0%

profile of v6, /device:TPU:32, one launch (start us, length us, event | category | flops | bytes accessed | tf_op | source)
XLA Modules:
  0.0 340.3 jit_solution(3593245061587514400)
XLA Ops:
  7.3 1.8 pad_maximum_fusion.1
  15.6 1.1 copy.67
  16.7 21.6 %all-gather.9.cloned.1.call-done = bf16[4160,384]{1,0:T(8,128)(2,1)} async-done(((bf16[520,384]{1,0:T(8,128)(2,1)}), bf16[4160,384]{1,0:T(8,128)(2,1)}) %all-gather.9.cloned.1.call-update) | async-done | bytes 3194896 | tf_op jit(solution)/shard_map/all_gather | solution.py:66
  39.1 1.1 constant_dynamic-slice_fusion.1
  40.9 1.1 convolution_bitcast_fusion
  43.7 1.8 fusion.53
  45.6 2.1 convert_element_type.78
  47.7 6.9 %all-to-all-start = ((bf16[16,16,6144]{2,1,0:T(8,128)(2,1)}), bf16[16,16,6144]{2,1,0:T(8,128)(2,1)S(1)}, u32[]{:S(2)}, u32[]{:S(2)}) async-start(bf16[16,16,6144]{2,1,0:T(8,128)(2,1)} %bitcast.99), calls=%async_computation | async-start | bytes 6291456 | tf_op jit(solution)/shard_map/all_to_all | solution.py:96
  55.4 46.9 %all-to-all-done = bf16[16,16,6144]{2,1,0:T(8,128)(2,1)S(1)} async-done(((bf16[16,16,6144]{2,1,0:T(8,128)(2,1)}), bf16[16,16,6144]{2,1,0:T(8,128)(2,1)S(1)}, u32[]{:S(2)}, u32[]{:S(2)}) %all-to-all-start) | async-done | bytes 3145760 | tf_op jit(solution)/shard_map/all_to_all | solution.py:96
  103.7 2.4 collective-permute-start
  106.2 4.1 %collective-permute-done = bf16[16,6144]{1,0:T(8,128)(2,1)S(1)} collective-permute-done((bf16[16,6144]{1,0:T(8,128)(2,1)S(1)}, bf16[16,6144]{1,0:T(8,128)(2,1)S(1)}, u32[]{:S(2)}, u32[]{:S(2)}) %collective-permute-start) | collective-permute-done | bytes 196640 | tf_op jit(solution)/shard_map/ppermute | solution.py:34
  110.3 1.2 broadcast_select_fusion.3
  112.2 16.8 %all_to_all.25 = bf16[8,8,6144]{2,1,0:T(8,128)(2,1)} all-to-all(bf16[8,8,6144]{2,1,0:T(8,128)(2,1)S(1)} %get-tuple-element.19), channel_id=1, replica_groups=mesh['leaf'=8,'expert'=8,'tensor'=2] {'expert'}, dimensions={0} | all-to-all | bytes 1572864 | tf_op jit(solution)/shard_map/all_to_all | solution.py:124
  129.1 14.6 %all_to_all.26 = bf16[8,8,6144]{2,1,0:T(8,128)(2,1)} all-to-all(bf16[8,8,6144]{2,1,0:T(8,128)(2,1)S(1)} %get-tuple-element.20), channel_id=1, replica_groups=mesh['leaf'=8,'expert'=8,'tensor'=2] {'expert'}, dimensions={0} | all-to-all | bytes 1572864 | tf_op jit(solution)/shard_map/all_to_all | solution.py:124
  143.9 22.8 %all-gather.5.cloned.1.call-done = bf16[512,6144]{1,0:T(8,128)(2,1)} async-done(((bf16[64,6144]{1,0:T(8,128)(2,1)}), bf16[512,6144]{1,0:T(8,128)(2,1)}) %all-gather.5.cloned.1.call-update) | async-done | bytes 6291472 | tf_op jit(solution)/shard_map/all_gather | solution.py:131
  166.7 8.2 %fusion.8 = f32[512,512]{1,0:T(8,128)S(1)} fusion(bf16[512,6144]{1,0:T(8,128)(2,1)} %all-gather.5.cloned.1.call-done, bf16[1,6144,512]{2,1,0:T(8,128)(2,1)} %param.21), kind=kOutput, calls=%fused_computation.12 | convolution fusion | flops 3221225472 | bytes 13631488 | tf_op jit(solution)/shard_map/dot_general | solution.py:137
  175.0 6.4 %fusion.17 = bf16[512,512]{1,0:T(8,128)(2,1)S(1)} fusion(bf16[512,6144]{1,0:T(8,128)(2,1)S(1)} %copy-done.8, bf16[1,6144,512]{2,1,0:T(8,128)(2,1)} %param.22, f32[512,512]{1,0:T(8,128)S(1)} %fusion.8), kind=kOutput, calls=%fused_computation.23 | convolution fusion | flops 3222798336 | bytes 14155776 | tf_op jit(solution)/shard_map/dot_general | solution.py:138
  181.5 5.4 %convolution_convert_fusion.1 = bf16[512,6144]{1,0:T(8,128)(2,1)} fusion(bf16[512,512]{1,0:T(8,128)(2,1)S(1)} %fusion.17, bf16[1,512,6144]{2,1,0:T(8,128)(2,1)S(1)} %bitcast.114), kind=kOutput, calls=%fused_computation.2 | convolution fusion | flops 3224371200 | bytes 13107200 | tf_op jit(solution)/shard_map/dot_general | solution.py:140
  187.8 1.5 collective-permute-start.1
  189.3 20.2 %all-gather.7.cloned.1.call-done = bf16[512,6144]{1,0:T(8,128)(2,1)} async-done(((bf16[64,6144]{1,0:T(8,128)(2,1)}), bf16[512,6144]{1,0:T(8,128)(2,1)}) %all-gather.7.cloned.1.call-update) | async-done | bytes 6291472 | tf_op jit(solution)/shard_map/all_gather | solution.py:131
  209.5 7.6 %fusion.2 = f32[512,512]{1,0:T(8,128)S(1)} fusion(bf16[512,6144]{1,0:T(8,128)(2,1)} %all-gather.7.cloned.1.call-done, bf16[1,6144,512]{2,1,0:T(8,128)(2,1)} %param.22), kind=kOutput, calls=%fused_computation.6 | convolution fusion | flops 3221225472 | bytes 13631488 | tf_op jit(solution)/shard_map/dot_general | solution.py:138
  217.2 5.7 %fusion.6 = f32[512,512]{1,0:T(8,128)S(1)} fusion(bf16[512,6144]{1,0:T(8,128)(2,1)S(1)} %copy-done.7, bf16[1,6144,512]{2,1,0:T(8,128)(2,1)} %param.21), kind=kOutput, calls=%fused_computation.10 | convolution fusion | flops 3221225472 | bytes 13631488 | tf_op jit(solution)/shard_map/dot_general | solution.py:137
  222.9 5.4 %convolution_convert_fusion = bf16[512,6144]{1,0:T(8,128)(2,1)} fusion(bf16[1,512,6144]{2,1,0:T(8,128)(2,1)S(1)} %bitcast.116, f32[512,512]{1,0:T(8,128)S(1)} %fusion.2, f32[512,512]{1,0:T(8,128)S(1)} %fusion.6), kind=kOutput, calls=%fused_computation.1 | convolution fusion | flops 3225944064 | bytes 14680064 | tf_op jit(solution)/shard_map/dot_general | solution.py:140
  228.3 24.8 %reduce-scatter.3.cloned.1.call-done = bf16[64,6144]{1,0:T(8,128)(2,1)} async-done(((bf16[512,6144]{1,0:T(8,128)(2,1)}), bf16[64,6144]{1,0:T(8,128)(2,1)}) %reduce-scatter.3.cloned.1.call-update) | async-done | bytes 786448 | tf_op jit(solution)/shard_map/reduce_scatter | solution.py:141
  253.2 6.7 %all-to-all-start.3 = ((bf16[8,8,6144]{2,1,0:T(8,128)(2,1)}), bf16[8,8,6144]{2,1,0:T(8,128)(2,1)S(1)}, u32[]{:S(2)}, u32[]{:S(2)}) async-start(bf16[8,8,6144]{2,1,0:T(8,128)(2,1)} %bitcast.104), calls=%async_computation.4 | async-start | bytes 1572864 | tf_op jit(solution)/shard_map/all_to_all | solution.py:143
  260.1 37.6 %reduce-scatter.5.cloned.1.call-done = bf16[64,6144]{1,0:T(8,128)(2,1)} async-done(((bf16[512,6144]{1,0:T(8,128)(2,1)}), bf16[64,6144]{1,0:T(8,128)(2,1)}) %reduce-scatter.5.cloned.1.call-update) | async-done | bytes 786448 | tf_op jit(solution)/shard_map/reduce_scatter | solution.py:141
  297.8 6.7 %all-to-all-start.4 = ((bf16[8,8,6144]{2,1,0:T(8,128)(2,1)}), bf16[8,8,6144]{2,1,0:T(8,128)(2,1)}, u32[]{:S(2)}, u32[]{:S(2)}) async-start(bf16[8,8,6144]{2,1,0:T(8,128)(2,1)} %bitcast.105), calls=%async_computation.6 | async-start | bytes 1572864 | tf_op jit(solution)/shard_map/all_to_all | solution.py:143
  304.8 13.6 %all-to-all-done.4 = bf16[8,8,6144]{2,1,0:T(8,128)(2,1)} async-done(((bf16[8,8,6144]{2,1,0:T(8,128)(2,1)}), bf16[8,8,6144]{2,1,0:T(8,128)(2,1)}, u32[]{:S(2)}, u32[]{:S(2)}) %all-to-all-start.4) | async-done | bytes 786464 | tf_op jit(solution)/shard_map/all_to_all | solution.py:143
  318.4 1.2 pad_maximum_fusion
  321.9 1.1 collective-permute-start.2
  323.0 9.6 %collective-permute-done.2 = bf16[32,6144]{1,0:T(8,128)(2,1)S(1)} collective-permute-done((bf16[32,6144]{1,0:T(8,128)(2,1)S(1)}, bf16[32,6144]{1,0:T(8,128)(2,1)S(1)}, u32[]{:S(2)}, u32[]{:S(2)}) %collective-permute-start.2) | collective-permute-done | bytes 393248 | tf_op jit(solution)/shard_map/ppermute | solution.py:159
  332.7 1.1 maximum_add_fusion
  (88 shorter events, 12.3 us)
Async XLA Ops:
  6.5 297.9 %copy-start = (bf16[6144,8]{0,1:T(8,128)(2,1)S(1)}, bf16[6144,8]{0,1:T(8,128)(2,1)}, u32[]{:S(2)}) copy-start(bf16[6144,8]{0,1:T(8,128)(2,1)} %param.19) | copy-start | bytes 294916
  6.5 31.7 %all-gather.9.cloned.1.call-start = ((), (), s32[]{:S(2)}) async-start(), calls=%async_computation.11 | async-start | bytes 3594240 | tf_op jit(solution)/shard_map/all_gather | solution.py:66
  40.8 2.9 copy-start.3
  43.6 1.8 copy-start.4
  45.6 9.1 %copy-start.6 = (s32[32,2]{0,1:T(2,128)S(1)}, s32[32,2]{0,1:T(2,128)}, u32[]{:S(2)}) copy-start(s32[32,2]{0,1:T(2,128)} %param.20) | copy-start | bytes 772
  47.7 55.9 %copy-start.5 = (f32[6144]{0:T(1024)S(1)}, f32[6144]{0:T(1024)}, u32[]{:S(2)}) copy-start(f32[6144]{0:T(1024)} %param.18) | copy-start | bytes 73732
  47.7 54.7 %all-to-all-start = ((bf16[16,16,6144]{2,1,0:T(8,128)(2,1)}), bf16[16,16,6144]{2,1,0:T(8,128)(2,1)S(1)}, u32[]{:S(2)}, u32[]{:S(2)}) async-start(bf16[16,16,6144]{2,1,0:T(8,128)(2,1)} %bitcast.99), calls=%async_computation | async-start | bytes 6291456 | tf_op jit(solution)/shard_map/all_to_all | solution.py:96
  54.6 112.1 %all-gather.5.cloned.1.call-start = ((), (), s32[]{:S(2)}) async-start(), calls=%async_computation.7 | async-start | bytes 7077888 | tf_op jit(solution)/shard_map/all_gather | solution.py:131
  102.8 0.7 copy-start.1
  103.7 6.6 %collective-permute-start = (bf16[16,6144]{1,0:T(8,128)(2,1)S(1)}, bf16[16,6144]{1,0:T(8,128)(2,1)S(1)}, u32[]{:S(2)}, u32[]{:S(2)}) collective-permute-start(bf16[16,6144]{1,0:T(8,128)(2,1)S(1)} %multiply_convert_fusion.2), channel_id=1, source_target_pairs={{0,1},{1,0},{2,3},{3,2},{4,5},{5,4},{6,7},{7,6},{8,9},{9,8},{10,11... | collective-permute-start | bytes 589832 | tf_op jit(solution)/shard_map/ppermute | solution.py:34
  129.0 80.5 %all-gather.7.cloned.1.call-start = ((), (), s32[]{:S(2)}) async-start(), calls=%async_computation.8 | async-start | bytes 7077888 | tf_op jit(solution)/shard_map/all_gather | solution.py:131
  143.7 109.5 %reduce-scatter.3.cloned.1.call-start = ((), (), s32[]{:S(2)}) async-start(), calls=%async_computation.9 | async-start | bytes 7077888 | tf_op jit(solution)/shard_map/reduce_scatter | solution.py:141
  166.7 8.2 %copy-start.8 = (bf16[512,6144]{1,0:T(8,128)(2,1)S(1)}, bf16[512,6144]{1,0:T(8,128)(2,1)}, u32[]{:S(2)}) copy-start(bf16[512,6144]{1,0:T(8,128)(2,1)} %all-gather.5.cloned.1.call-done) | copy-start | bytes 18874372
  166.7 14.7 %slice-start = ((s8[6291456]{0:T(1024)(128)(4,1)}), s8[4194304]{0:T(1024)(128)(4,1)S(1)}, s32[]{:S(2)}) async-start(s8[6291456]{0:T(1024)(128)(4,1)} %bitcast.113), calls=%async_computation.12 | async-start | bytes 8388608
  175.0 6.5 %slice-start.1 = ((s8[6291456]{0:T(1024)(128)(4,1)}), s8[2097152]{0:T(1024)(128)(4,1)S(1)}, s32[]{:S(2)}) async-start(s8[6291456]{0:T(1024)(128)(4,1)} %bitcast.113), calls=%async_computation.13 | async-start | bytes 4194304
  186.8 1.0 copy-start.2
  186.9 110.9 %reduce-scatter.5.cloned.1.call-start = ((), (), s32[]{:S(2)}) async-start(), calls=%async_computation.10 | async-start | bytes 7077888 | tf_op jit(solution)/shard_map/reduce_scatter | solution.py:141
  187.8 21.7 %collective-permute-start.1 = (f32[16,6144]{1,0:T(8,128)S(1)}, f32[16,6144]{1,0:T(8,128)S(1)}, u32[]{:S(2)}, u32[]{:S(2)}) collective-permute-start(f32[16,6144]{1,0:T(8,128)S(1)} %copy-done.2), channel_id=1, source_target_pairs={{0,1},{1,0},{2,3},{3,2},{4,5},{5,4},{6,7},{7,6},{8,9},{9,8},{10,11... | collective-permute-start | bytes 1179656 | tf_op jit(solution)/shard_map/ppermute | solution.py:134
  209.5 7.6 %copy-start.7 = (bf16[512,6144]{1,0:T(8,128)(2,1)S(1)}, bf16[512,6144]{1,0:T(8,128)(2,1)}, u32[]{:S(2)}) copy-start(bf16[512,6144]{1,0:T(8,128)(2,1)} %all-gather.7.cloned.1.call-done) | copy-start | bytes 18874372
  209.5 13.4 %slice-start.2 = ((s8[6291456]{0:T(1024)(128)(4,1)}), s8[4194304]{0:T(1024)(128)(4,1)S(1)}, s32[]{:S(2)}) async-start(s8[6291456]{0:T(1024)(128)(4,1)} %bitcast.115), calls=%async_computation.14 | async-start | bytes 8388608
  217.1 5.8 %slice-start.3 = ((s8[6291456]{0:T(1024)(128)(4,1)}), s8[2097152]{0:T(1024)(128)(4,1)S(1)}, s32[]{:S(2)}) async-start(s8[6291456]{0:T(1024)(128)(4,1)} %bitcast.115), calls=%async_computation.15 | async-start | bytes 4194304
  253.2 44.6 %all-to-all-start.3 = ((bf16[8,8,6144]{2,1,0:T(8,128)(2,1)}), bf16[8,8,6144]{2,1,0:T(8,128)(2,1)S(1)}, u32[]{:S(2)}, u32[]{:S(2)}) async-start(bf16[8,8,6144]{2,1,0:T(8,128)(2,1)} %bitcast.104), calls=%async_computation.4 | async-start | bytes 1572864 | tf_op jit(solution)/shard_map/all_to_all | solution.py:143
  297.8 20.7 %all-to-all-start.4 = ((bf16[8,8,6144]{2,1,0:T(8,128)(2,1)}), bf16[8,8,6144]{2,1,0:T(8,128)(2,1)}, u32[]{:S(2)}, u32[]{:S(2)}) async-start(bf16[8,8,6144]{2,1,0:T(8,128)(2,1)} %bitcast.105), calls=%async_computation.6 | async-start | bytes 1572864 | tf_op jit(solution)/shard_map/all_to_all | solution.py:143
  321.9 10.8 %collective-permute-start.2 = (bf16[32,6144]{1,0:T(8,128)(2,1)S(1)}, bf16[32,6144]{1,0:T(8,128)(2,1)S(1)}, u32[]{:S(2)}, u32[]{:S(2)}) collective-permute-start(bf16[32,6144]{1,0:T(8,128)(2,1)S(1)} %fusion.31), channel_id=1, source_target_pairs={{0,1},{1,0},{2,3},{3,2},{4,5},{5,4},{6,7},{7,6},{8,9},{9,8},{10,11... | collective-permute-start | bytes 1179656 | tf_op jit(solution)/shard_map/ppermute | solution.py:159
Sparse Core Ops, SparseCore 0:
  9.2 29.0 all-gather.8
  129.1 37.5 all-gather.4
  168.4 41.0 all-gather.6
  211.8 41.3 reduce-scatter.2
  255.4 42.2 reduce-scatter.4

commit v7 on v6

--- a/solution.py
+++ b/solution.py
@@ -91,12 +91,17 @@
         jnp.float32
     )
     term = lax.dynamic_update_slice(term, own_cols, (0, offset)).astype(jnp.bfloat16)
-    group = lax.axis_size(("expert", "tensor"))
-    share_rows = local_rows // group
+    group = lax.axis_size("expert")
+    group_rows = local_rows // group
     arrived_terms = lax.all_to_all(
-        term.reshape(group, share_rows, width), ("expert", "tensor"), 0, 0, tiled=True
+        term.reshape(group, group_rows, width), "expert", 0, 0, tiled=True
     )
-    share = jnp.sum(arrived_terms.astype(jnp.float32), axis=0)
+    pair_sum = jnp.sum(arrived_terms.astype(jnp.float32), axis=0)
+    half = group_rows // 2
+    low = lax.axis_index("tensor") == 0
+    mine = jnp.where(low, pair_sum[:half], pair_sum[half:])
+    theirs = jnp.where(low, pair_sum[half:], pair_sum[:half])
+    share = mine + lax.ppermute(theirs, "tensor", perm=[(0, 1), (1, 0)])
     mean_square = jnp.mean(share * share, axis=-1, keepdims=True)
     normed = pair_gather((share * lax.rsqrt(mean_square + 1e-05) * norm_gain).astype(jnp.bfloat16))
     logits = jnp.dot(normed, router, preferred_element_type=jnp.float32)

time: 341 us -> 342 us (level)
    ppermute x0 -> x1, waiting for transfers between devices: none -> 9.04 us  [per_device(): share = mine + lax.ppermute(theirs, 'tensor', perm=[(0, 1), (1, 0)])]
    all_to_all x1, waiting for transfers between devices: 46.9 us -> 38 us  [per_device(): lax.all_to_all(term.reshape(group, group_rows, width), 'expert', 0, 0, ti...]
  transfers between devices with their start and end apart: 11 -> 12, of which waited for: 9 -> 10; matrix products, arithmetic and copies ran while one was open for 13% -> 13% of each run, Pallas kernels for 0% -> 0%
where the time goes in v7:
time: 342 us
  waiting for transfers between devices  202 us (59%)
  matrix products  44.4 us (13%)
  blocking collectives  33 us (10%)
  starting transfers between devices  24.5 us (7%)
  between operations  18.7 us (5%)
  other arithmetic  11.3 us (3%)
  local copies, waits for them, and re-layouts  7.47 us (2%)
    reduce_scatter x2, waiting for transfers between devices, per_device(): part_rows = lax.psum_scatter(down, 'leaf', scatter_dimension=0, tiled=True)  62 us
    all_gather x2, waiting for transfers between devices, per_device(): piece = lax.all_gather(arrived, 'leaf', axis=0, tiled=True)  43.3 us
    all_to_all x1, waiting for transfers between devices, per_device(): lax.all_to_all(term.reshape(group, group_rows, width), 'expert', 0, 0, ti...  38 us
    all_to_all x2, blocking collectives, per_device(): lax.all_to_all(outgoing[:, c * chunk_slots:(c + 1) * chunk_slots], 'exper...  33 us
    all_gather x1, waiting for transfers between devices, per_device(): gathered = lax.all_gather(payload, 'leaf', axis=0, tiled=False)  21.5 us
    dot_general x2, matrix products, per_device(): up_v = jnp.dot(piece, w_up[0], preferred_element_type=jnp.float32)  14.5 us
    dot_general x2, matrix products, per_device(): gate_v = jnp.dot(piece, w_gate[0], preferred_element_type=jnp.float32)  14 us
    all_to_all x2, waiting for transfers between devices, per_device(): lax.all_to_all(part_rows.reshape(experts, chunk_slots, width), 'expert',...  13.6 us
  transfers between devices with their start and end apart: 12, of which 10 were waited for; matrix products, arithmetic and copies ran while one was open for 13% of the time, Pallas kernels for 0%

profile of v7, /device:TPU:32, one launch (start us, length us, event | category | flops | bytes accessed | tf_op | source)
XLA Modules:
  0.0 341.6 jit_solution(15646207288232733969)
XLA Ops:
  7.3 1.8 pad_maximum_fusion.1
  15.7 1.1 copy.67
  16.7 21.5 %all-gather.9.cloned.1.call-done = bf16[4160,384]{1,0:T(8,128)(2,1)} async-done(((bf16[520,384]{1,0:T(8,128)(2,1)}), bf16[4160,384]{1,0:T(8,128)(2,1)}) %all-gather.9.cloned.1.call-update) | async-done | bytes 3194896 | tf_op jit(solution)/shard_map/all_gather | solution.py:66
  39.1 1.1 constant_dynamic-slice_fusion.1
  40.9 1.1 convolution_bitcast_fusion
  43.7 1.8 fusion.53
  45.6 2.1 convert_element_type.78
  47.6 6.8 %all-to-all-start = ((bf16[8,32,6144]{2,1,0:T(8,128)(2,1)}), bf16[8,32,6144]{2,1,0:T(8,128)(2,1)S(1)}, u32[]{:S(2)}, u32[]{:S(2)}) async-start(bf16[8,32,6144]{2,1,0:T(8,128)(2,1)} %bitcast.99), calls=%async_computation | async-start | bytes 6291456 | tf_op jit(solution)/shard_map/all_to_all | solution.py:96
  54.5 38.0 %all-to-all-done = bf16[8,32,6144]{2,1,0:T(8,128)(2,1)S(1)} async-done(((bf16[8,32,6144]{2,1,0:T(8,128)(2,1)}), bf16[8,32,6144]{2,1,0:T(8,128)(2,1)S(1)}, u32[]{:S(2)}, u32[]{:S(2)}) %all-to-all-start) | async-done | bytes 3145760 | tf_op jit(solution)/shard_map/all_to_all | solution.py:96
  95.3 9.0 %collective-permute-done = f32[16,6144]{1,0:T(8,128)S(1)} collective-permute-done((f32[16,6144]{1,0:T(8,128)S(1)}, f32[16,6144]{1,0:T(8,128)S(1)}, u32[]{:S(2)}, u32[]{:S(2)}) %collective-permute-start) | collective-permute-done | bytes 393248 | tf_op jit(solution)/shard_map/ppermute | solution.py:104
  104.4 1.3 multiply_reduce_fusion
  106.5 5.0 %collective-permute-done.1 = bf16[16,6144]{1,0:T(8,128)(2,1)S(1)} collective-permute-done((bf16[16,6144]{1,0:T(8,128)(2,1)S(1)}, bf16[16,6144]{1,0:T(8,128)(2,1)S(1)}, u32[]{:S(2)}, u32[]{:S(2)}) %collective-permute-start.1) | collective-permute-done | bytes 196640 | tf_op jit(solution)/shard_map/ppermute | solution.py:34
  112.4 18.4 %all_to_all.25 = bf16[8,8,6144]{2,1,0:T(8,128)(2,1)} all-to-all(bf16[8,8,6144]{2,1,0:T(8,128)(2,1)S(1)} %get-tuple-element.21), channel_id=1, replica_groups=mesh['leaf'=8,'expert'=8,'tensor'=2] {'expert'}, dimensions={0} | all-to-all | bytes 1572864 | tf_op jit(solution)/shard_map/all_to_all | solution.py:129
  130.9 14.6 %all_to_all.26 = bf16[8,8,6144]{2,1,0:T(8,128)(2,1)} all-to-all(bf16[8,8,6144]{2,1,0:T(8,128)(2,1)S(1)} %get-tuple-element.22), channel_id=1, replica_groups=mesh['leaf'=8,'expert'=8,'tensor'=2] {'expert'}, dimensions={0} | all-to-all | bytes 1572864 | tf_op jit(solution)/shard_map/all_to_all | solution.py:129
  145.8 22.3 %all-gather.5.cloned.1.call-done = bf16[512,6144]{1,0:T(8,128)(2,1)} async-done(((bf16[64,6144]{1,0:T(8,128)(2,1)}), bf16[512,6144]{1,0:T(8,128)(2,1)}) %all-gather.5.cloned.1.call-update) | async-done | bytes 6291472 | tf_op jit(solution)/shard_map/all_gather | solution.py:136
  168.1 8.2 %fusion.8 = f32[512,512]{1,0:T(8,128)S(1)} fusion(bf16[512,6144]{1,0:T(8,128)(2,1)} %all-gather.5.cloned.1.call-done, bf16[1,6144,512]{2,1,0:T(8,128)(2,1)} %param.21), kind=kOutput, calls=%fused_computation.12 | convolution fusion | flops 3221225472 | bytes 13631488 | tf_op jit(solution)/shard_map/dot_general | solution.py:142
  176.3 6.4 %fusion.17 = bf16[512,512]{1,0:T(8,128)(2,1)S(1)} fusion(bf16[512,6144]{1,0:T(8,128)(2,1)S(1)} %copy-done.9, bf16[1,6144,512]{2,1,0:T(8,128)(2,1)} %param.22, f32[512,512]{1,0:T(8,128)S(1)} %fusion.8), kind=kOutput, calls=%fused_computation.23 | convolution fusion | flops 3222798336 | bytes 14155776 | tf_op jit(solution)/shard_map/dot_general | solution.py:143
  182.8 5.5 %convolution_convert_fusion.1 = bf16[512,6144]{1,0:T(8,128)(2,1)} fusion(bf16[512,512]{1,0:T(8,128)(2,1)S(1)} %fusion.17, bf16[1,512,6144]{2,1,0:T(8,128)(2,1)S(1)} %bitcast.114), kind=kOutput, calls=%fused_computation.2 | convolution fusion | flops 3224371200 | bytes 13107200 | tf_op jit(solution)/shard_map/dot_general | solution.py:145
  188.3 1.5 collective-permute-start.2
  189.9 21.0 %all-gather.7.cloned.1.call-done = bf16[512,6144]{1,0:T(8,128)(2,1)} async-done(((bf16[64,6144]{1,0:T(8,128)(2,1)}), bf16[512,6144]{1,0:T(8,128)(2,1)}) %all-gather.7.cloned.1.call-update) | async-done | bytes 6291472 | tf_op jit(solution)/shard_map/all_gather | solution.py:136
  210.9 8.1 %fusion.2 = f32[512,512]{1,0:T(8,128)S(1)} fusion(bf16[512,6144]{1,0:T(8,128)(2,1)} %all-gather.7.cloned.1.call-done, bf16[1,6144,512]{2,1,0:T(8,128)(2,1)} %param.22), kind=kOutput, calls=%fused_computation.6 | convolution fusion | flops 3221225472 | bytes 13631488 | tf_op jit(solution)/shard_map/dot_general | solution.py:143
  219.0 5.7 %fusion.6 = f32[512,512]{1,0:T(8,128)S(1)} fusion(bf16[512,6144]{1,0:T(8,128)(2,1)S(1)} %copy-done.8, bf16[1,6144,512]{2,1,0:T(8,128)(2,1)} %param.21), kind=kOutput, calls=%fused_computation.10 | convolution fusion | flops 3221225472 | bytes 13631488 | tf_op jit(solution)/shard_map/dot_general | solution.py:142
  224.8 5.3 %convolution_convert_fusion = bf16[512,6144]{1,0:T(8,128)(2,1)} fusion(bf16[1,512,6144]{2,1,0:T(8,128)(2,1)S(1)} %bitcast.116, f32[512,512]{1,0:T(8,128)S(1)} %fusion.2, f32[512,512]{1,0:T(8,128)S(1)} %fusion.6), kind=kOutput, calls=%fused_computation.1 | convolution fusion | flops 3225944064 | bytes 14680064 | tf_op jit(solution)/shard_map/dot_general | solution.py:145
  230.1 24.4 %reduce-scatter.3.cloned.1.call-done = bf16[64,6144]{1,0:T(8,128)(2,1)} async-done(((bf16[512,6144]{1,0:T(8,128)(2,1)}), bf16[64,6144]{1,0:T(8,128)(2,1)}) %reduce-scatter.3.cloned.1.call-update) | async-done | bytes 786448 | tf_op jit(solution)/shard_map/reduce_scatter | solution.py:146
  254.5 6.7 %all-to-all-start.3 = ((bf16[8,8,6144]{2,1,0:T(8,128)(2,1)}), bf16[8,8,6144]{2,1,0:T(8,128)(2,1)S(1)}, u32[]{:S(2)}, u32[]{:S(2)}) async-start(bf16[8,8,6144]{2,1,0:T(8,128)(2,1)} %bitcast.104), calls=%async_computation.4 | async-start | bytes 1572864 | tf_op jit(solution)/shard_map/all_to_all | solution.py:148
  261.4 37.6 %reduce-scatter.5.cloned.1.call-done = bf16[64,6144]{1,0:T(8,128)(2,1)} async-done(((bf16[512,6144]{1,0:T(8,128)(2,1)}), bf16[64,6144]{1,0:T(8,128)(2,1)}) %reduce-scatter.5.cloned.1.call-update) | async-done | bytes 786448 | tf_op jit(solution)/shard_map/reduce_scatter | solution.py:146
  299.1 6.7 %all-to-all-start.4 = ((bf16[8,8,6144]{2,1,0:T(8,128)(2,1)}), bf16[8,8,6144]{2,1,0:T(8,128)(2,1)}, u32[]{:S(2)}, u32[]{:S(2)}) async-start(bf16[8,8,6144]{2,1,0:T(8,128)(2,1)} %bitcast.105), calls=%async_computation.6 | async-start | bytes 1572864 | tf_op jit(solution)/shard_map/all_to_all | solution.py:148
  306.1 13.6 %all-to-all-done.4 = bf16[8,8,6144]{2,1,0:T(8,128)(2,1)} async-done(((bf16[8,8,6144]{2,1,0:T(8,128)(2,1)}), bf16[8,8,6144]{2,1,0:T(8,128)(2,1)}, u32[]{:S(2)}, u32[]{:S(2)}) %all-to-all-start.4) | async-done | bytes 786464 | tf_op jit(solution)/shard_map/all_to_all | solution.py:148
  319.7 1.2 pad_maximum_fusion
  323.2 1.1 collective-permute-start.3
  324.3 9.6 %collective-permute-done.3 = bf16[32,6144]{1,0:T(8,128)(2,1)S(1)} collective-permute-done((bf16[32,6144]{1,0:T(8,128)(2,1)S(1)}, bf16[32,6144]{1,0:T(8,128)(2,1)S(1)}, u32[]{:S(2)}, u32[]{:S(2)}) %collective-permute-start.3) | collective-permute-done | bytes 393248 | tf_op jit(solution)/shard_map/ppermute | solution.py:164
  334.0 1.1 maximum_add_fusion
  (93 shorter events, 13.0 us)
Async XLA Ops:
  6.5 299.2 %copy-start = (bf16[6144,8]{0,1:T(8,128)(2,1)S(1)}, bf16[6144,8]{0,1:T(8,128)(2,1)}, u32[]{:S(2)}) copy-start(bf16[6144,8]{0,1:T(8,128)(2,1)} %param.19) | copy-start | bytes 294916
  6.5 31.7 %all-gather.9.cloned.1.call-start = ((), (), s32[]{:S(2)}) async-start(), calls=%async_computation.11 | async-start | bytes 3594240 | tf_op jit(solution)/shard_map/all_gather | solution.py:66
  40.8 2.9 copy-start.2
  43.6 1.8 copy-start.3
  47.6 46.9 %copy-start.7 = (s32[32,2]{0,1:T(2,128)S(1)}, s32[32,2]{0,1:T(2,128)}, u32[]{:S(2)}) copy-start(s32[32,2]{0,1:T(2,128)} %param.20) | copy-start | bytes 772
  47.6 58.0 %copy-start.6 = (f32[6144]{0:T(1024)S(1)}, f32[6144]{0:T(1024)}, u32[]{:S(2)}) copy-start(f32[6144]{0:T(1024)} %param.18) | copy-start | bytes 73732
  47.6 44.9 %all-to-all-start = ((bf16[8,32,6144]{2,1,0:T(8,128)(2,1)}), bf16[8,32,6144]{2,1,0:T(8,128)(2,1)S(1)}, u32[]{:S(2)}, u32[]{:S(2)}) async-start(bf16[8,32,6144]{2,1,0:T(8,128)(2,1)} %bitcast.99), calls=%async_computation | async-start | bytes 6291456 | tf_op jit(solution)/shard_map/all_to_all | solution.py:96
  54.5 113.6 %all-gather.5.cloned.1.call-start = ((), (), s32[]{:S(2)}) async-start(), calls=%async_computation.7 | async-start | bytes 7077888 | tf_op jit(solution)/shard_map/all_gather | solution.py:136
  93.0 0.9 copy-start.1
  93.9 10.4 %collective-permute-start = (f32[16,6144]{1,0:T(8,128)S(1)}, f32[16,6144]{1,0:T(8,128)S(1)}, u32[]{:S(2)}, u32[]{:S(2)}) collective-permute-start(f32[16,6144]{1,0:T(8,128)S(1)} %slice_select_fusion), channel_id=1, source_target_pairs={{0,1},{1,0},{2,3},{3,2},{4,5},{5,4},{6,7},{7,6},{8,9},{9,8},{10,11... | collective-permute-start | bytes 1179656 | tf_op jit(solution)/shard_map/ppermute | solution.py:104
  105.8 5.7 %collective-permute-start.1 = (bf16[16,6144]{1,0:T(8,128)(2,1)S(1)}, bf16[16,6144]{1,0:T(8,128)(2,1)S(1)}, u32[]{:S(2)}, u32[]{:S(2)}) collective-permute-start(bf16[16,6144]{1,0:T(8,128)(2,1)S(1)} %multiply_convert_fusion.2), channel_id=1, source_target_pairs={{0,1},{1,0},{2,3},{3,2},{4,5},{5,4},{6,7},{7,6},{8,9},{9,8},{10,11... | collective-permute-start | bytes 589832 | tf_op jit(solution)/shard_map/ppermute | solution.py:34
  130.8 80.0 %all-gather.7.cloned.1.call-start = ((), (), s32[]{:S(2)}) async-start(), calls=%async_computation.8 | async-start | bytes 7077888 | tf_op jit(solution)/shard_map/all_gather | solution.py:136
  145.5 109.0 %reduce-scatter.3.cloned.1.call-start = ((), (), s32[]{:S(2)}) async-start(), calls=%async_computation.9 | async-start | bytes 7077888 | tf_op jit(solution)/shard_map/reduce_scatter | solution.py:146
  168.1 8.2 %copy-start.9 = (bf16[512,6144]{1,0:T(8,128)(2,1)S(1)}, bf16[512,6144]{1,0:T(8,128)(2,1)}, u32[]{:S(2)}) copy-start(bf16[512,6144]{1,0:T(8,128)(2,1)} %all-gather.5.cloned.1.call-done) | copy-start | bytes 18874372
  168.1 14.7 %slice-start = ((s8[6291456]{0:T(1024)(128)(4,1)}), s8[4194304]{0:T(1024)(128)(4,1)S(1)}, s32[]{:S(2)}) async-start(s8[6291456]{0:T(1024)(128)(4,1)} %bitcast.113), calls=%async_computation.12 | async-start | bytes 8388608
  176.3 6.5 %slice-start.1 = ((s8[6291456]{0:T(1024)(128)(4,1)}), s8[2097152]{0:T(1024)(128)(4,1)S(1)}, s32[]{:S(2)}) async-start(s8[6291456]{0:T(1024)(128)(4,1)} %bitcast.113), calls=%async_computation.13 | async-start | bytes 4194304
  188.3 110.8 %reduce-scatter.5.cloned.1.call-start = ((), (), s32[]{:S(2)}) async-start(), calls=%async_computation.10 | async-start | bytes 7077888 | tf_op jit(solution)/shard_map/reduce_scatter | solution.py:146
  188.3 22.5 %collective-permute-start.2 = (f32[16,6144]{1,0:T(8,128)S(1)}, f32[16,6144]{1,0:T(8,128)S(1)}, u32[]{:S(2)}, u32[]{:S(2)}) collective-permute-start(f32[16,6144]{1,0:T(8,128)S(1)} %get-tuple-element.9), channel_id=1, source_target_pairs={{0,1},{1,0},{2,3},{3,2},{4,5},{5,4},{6,7},{7,6},{8,9},{9,8},{10,11... | collective-permute-start | bytes 1179656 | tf_op jit(solution)/shard_map/ppermute | solution.py:139
  210.8 8.1 %copy-start.8 = (bf16[512,6144]{1,0:T(8,128)(2,1)S(1)}, bf16[512,6144]{1,0:T(8,128)(2,1)}, u32[]{:S(2)}) copy-start(bf16[512,6144]{1,0:T(8,128)(2,1)} %all-gather.7.cloned.1.call-done) | copy-start | bytes 18874372
  210.9 8.1 %copy-start.4 = (f32[16,6144]{1,0:T(8,128)}, f32[16,6144]{1,0:T(8,128)S(1)}, u32[]{:S(2)}) copy-start(f32[16,6144]{1,0:T(8,128)S(1)} %collective-permute-done.2) | copy-start | bytes 1179652
  210.9 13.9 %slice-start.2 = ((s8[6291456]{0:T(1024)(128)(4,1)}), s8[4194304]{0:T(1024)(128)(4,1)S(1)}, s32[]{:S(2)}) async-start(s8[6291456]{0:T(1024)(128)(4,1)} %bitcast.115), calls=%async_computation.14 | async-start | bytes 8388608
  219.0 5.8 %slice-start.3 = ((s8[6291456]{0:T(1024)(128)(4,1)}), s8[2097152]{0:T(1024)(128)(4,1)S(1)}, s32[]{:S(2)}) async-start(s8[6291456]{0:T(1024)(128)(4,1)} %bitcast.115), calls=%async_computation.15 | async-start | bytes 4194304
  254.5 44.6 %all-to-all-start.3 = ((bf16[8,8,6144]{2,1,0:T(8,128)(2,1)}), bf16[8,8,6144]{2,1,0:T(8,128)(2,1)S(1)}, u32[]{:S(2)}, u32[]{:S(2)}) async-start(bf16[8,8,6144]{2,1,0:T(8,128)(2,1)} %bitcast.104), calls=%async_computation.4 | async-start | bytes 1572864 | tf_op jit(solution)/shard_map/all_to_all | solution.py:148
  299.1 20.7 %all-to-all-start.4 = ((bf16[8,8,6144]{2,1,0:T(8,128)(2,1)}), bf16[8,8,6144]{2,1,0:T(8,128)(2,1)}, u32[]{:S(2)}, u32[]{:S(2)}) async-start(bf16[8,8,6144]{2,1,0:T(8,128)(2,1)} %bitcast.105), calls=%async_computation.6 | async-start | bytes 1572864 | tf_op jit(solution)/shard_map/all_to_all | solution.py:148
  321.0 3.3 copy-start.5
  323.2 10.8 %collective-permute-start.3 = (bf16[32,6144]{1,0:T(8,128)(2,1)S(1)}, bf16[32,6144]{1,0:T(8,128)(2,1)S(1)}, u32[]{:S(2)}, u32[]{:S(2)}) collective-permute-start(bf16[32,6144]{1,0:T(8,128)(2,1)S(1)} %fusion.31), channel_id=1, source_target_pairs={{0,1},{1,0},{2,3},{3,2},{4,5},{5,4},{6,7},{7,6},{8,9},{9,8},{10,11... | collective-permute-start | bytes 1179656 | tf_op jit(solution)/shard_map/ppermute | solution.py:164
Sparse Core Ops, SparseCore 0:
  9.2 29.0 all-gather.8
  130.9 37.0 all-gather.4
  169.8 41.0 all-gather.6
  213.1 41.3 reduce-scatter.2
  256.8 42.2 reduce-scatter.4

commit v8 on v6

--- a/solution.py
+++ b/solution.py
@@ -34,6 +34,26 @@
     other = lax.ppermute(share, "tensor", perm=[(0, 1), (1, 0)])
     low = lax.axis_index("tensor") == 0
     return jnp.concatenate([jnp.where(low, share, other), jnp.where(low, other, share)], axis=0)
+
+
+def gather_leaf(x):
+    rows, width = x.shape
+    n_leaf = lax.axis_size("leaf")
+    n_z = n_leaf // 2
+    index = lax.axis_index("leaf")
+    core = index % 2
+    z = index // 2
+    got = [x]
+    for k in range(1, n_z):
+        perm = [(a * 2 + b, ((a + k) % n_z) * 2 + b) for a in range(n_z) for b in range(2)]
+        got.append(lax.ppermute(x, "leaf", perm=perm))
+    mine = jnp.stack(got)
+    other = lax.ppermute(mine, "leaf", perm=[(j, j ^ 1) for j in range(n_leaf)])
+    both = jnp.concatenate([mine, other], axis=0)
+    zz = jnp.arange(n_z, dtype=jnp.int32)[:, None]
+    cc = jnp.arange(2, dtype=jnp.int32)[None, :]
+    order = jnp.where(cc == core, 0, n_z) + (z - zz) % n_z
+    return jnp.take(both, order.reshape(-1), axis=0).reshape(n_leaf * rows, width)
 
 
 def per_device(
@@ -128,7 +148,7 @@
             concat_axis=0,
             tiled=True,
         ).reshape(-1, width)
-        piece = lax.all_gather(arrived, "leaf", axis=0, tiled=True)
+        piece = gather_leaf(arrived)
         if c == 0:
             piece, share = lax.optimization_barrier((piece, share))
             other_share = lax.ppermute(share, "tensor", perm=[(0, 1), (1, 0)])

time: 341 us -> 390 us (1.14)
  blocking collectives: 31.5 us -> 0 us
  local copies, waits for them, and re-layouts: 8.08 us -> 37.4 us
  starting transfers between devices: 25.7 us -> 45.8 us
  waiting for transfers between devices: 201 us -> 220 us
  other arithmetic: 11.2 us -> 25.1 us
    ppermute x0 -> x8, waiting for transfers between devices: none -> 46.6 us  [the longest x6 46.6 us: gather_leaf(): got.append(lax.ppermute(x, 'leaf', perm=perm))]
    all_gather x2 -> x0, waiting for transfers between devices: 43 us -> none  [per_device(): piece = lax.all_gather(arrived, 'leaf', axis=0, tiled=True)]
    all_to_all x2 -> x0, blocking collectives: 31.5 us -> none  [per_device(): lax.all_to_all(outgoing[:, c * chunk_slots:(c + 1) * chunk_slots], 'exper...]
    all_to_all x0 -> x2, waiting for transfers between devices: none -> 19.7 us  [per_device(): lax.all_to_all(outgoing[:, c * chunk_slots:(c + 1) * chunk_slots], 'exper...]
    reduce_scatter x2, waiting for transfers between devices: 62.5 us -> 46.4 us  [per_device(): part_rows = lax.psum_scatter(down, 'leaf', scatter_dimension=0, tiled=True)]
    ppermute x0 -> x8, starting transfers between devices: none -> 13.5 us  [the longest x6 13.4 us: gather_leaf(): got.append(lax.ppermute(x, 'leaf', perm=perm))]
    gather x0 -> x2, local copies, waits for them, and re-layouts: none -> 12.7 us  [gather_leaf(): jnp.take(both, order.reshape(-1), axis=0).reshape(n_leaf * rows, width)]
    ppermute x1, waiting for transfers between devices: 0.01 us -> 11.1 us  [per_device(): other_share = lax.ppermute(share, 'tensor', perm=[(0, 1), (1, 0)])]
  transfers between devices with their start and end apart: 11 -> 19, of which waited for: 9 -> 14; matrix products, arithmetic and copies ran while one was open for 13% -> 12% of each run, Pallas kernels for 0% -> 0%
where the time goes in v8:
time: 390 us; the launch traced here: 389 us
  waiting for transfers between devices  220 us (56%)
  starting transfers between devices  45.8 us (12%)
  matrix products  42.6 us (11%)
  local copies, waits for them, and re-layouts  37.4 us (10%)
  other arithmetic  25.1 us (6%)
  between operations  18.4 us (5%)
    all_to_all x1, waiting for transfers between devices, per_device(): lax.all_to_all(term.reshape(group, share_rows, width), ('expert', 'tensor...  47 us
    ppermute x6, waiting for transfers between devices, gather_leaf(): got.append(lax.ppermute(x, 'leaf', perm=perm))  46.6 us
    reduce_scatter x2, waiting for transfers between devices, per_device(): part_rows = lax.psum_scatter(down, 'leaf', scatter_dimension=0, tiled=True)  46.4 us
    all_gather x1, waiting for transfers between devices, per_device(): gathered = lax.all_gather(payload, 'leaf', axis=0, tiled=False)  21.9 us
    all_to_all x2, waiting for transfers between devices, per_device(): lax.all_to_all(outgoing[:, c * chunk_slots:(c + 1) * chunk_slots], 'exper...  19.7 us
    dot_general x2, matrix products, per_device(): gate_v = jnp.dot(piece, w_gate[0], preferred_element_type=jnp.float32)  15.4 us
    all_to_all x2, waiting for transfers between devices, per_device(): lax.all_to_all(part_rows.reshape(experts, chunk_slots, width), 'expert',...  13.7 us
    all_to_all x2, starting transfers between devices, per_device(): lax.all_to_all(part_rows.reshape(experts, chunk_slots, width), 'expert',...  13.4 us
  transfers between devices with their start and end apart: 19, of which 14 were waited for; matrix products, arithmetic and copies ran while one was open for 12% of the time, Pallas kernels for 0%

profile of v8, /device:TPU:32, one launch (start us, length us, event | category | flops | bytes accessed | tf_op | source)
XLA Modules:
  0.0 389.4 jit_solution(15446501489034961576)
XLA Ops:
  16.4 21.9 %all-gather.3.cloned.1.call-done = bf16[4160,384]{1,0:T(8,128)(2,1)} async-done(((bf16[520,384]{1,0:T(8,128)(2,1)}), bf16[4160,384]{1,0:T(8,128)(2,1)}) %all-gather.3.cloned.1.call-update) | async-done | bytes 3194896 | tf_op jit(solution)/shard_map/all_gather | solution.py:86
  47.7 6.9 %all-to-all-start = ((bf16[16,16,6144]{2,1,0:T(8,128)(2,1)}), bf16[16,16,6144]{2,1,0:T(8,128)(2,1)S(1)}, u32[]{:S(2)}, u32[]{:S(2)}) async-start(bf16[16,16,6144]{2,1,0:T(8,128)(2,1)} %bitcast.117), calls=%async_computation | async-start | bytes 6291456 | tf_op jit(solution)/shard_map/all_to_all | solution.py:116
  55.4 47.0 %all-to-all-done = bf16[16,16,6144]{2,1,0:T(8,128)(2,1)S(1)} async-done(((bf16[16,16,6144]{2,1,0:T(8,128)(2,1)}), bf16[16,16,6144]{2,1,0:T(8,128)(2,1)S(1)}, u32[]{:S(2)}, u32[]{:S(2)}) %all-to-all-start) | async-done | bytes 3145760 | tf_op jit(solution)/shard_map/all_to_all | solution.py:116
  106.2 4.1 %collective-permute-done = bf16[16,6144]{1,0:T(8,128)(2,1)S(1)} collective-permute-done((bf16[16,6144]{1,0:T(8,128)(2,1)S(1)}, bf16[16,6144]{1,0:T(8,128)(2,1)S(1)}, u32[]{:S(2)}, u32[]{:S(2)}) %collective-permute-start) | collective-permute-done | bytes 196640 | tf_op jit(solution)/shard_map/ppermute | solution.py:34
  114.0 4.5 %all-to-all-start.1 = ((bf16[8,8,6144]{2,1,0:T(8,128)(2,1)}), bf16[8,8,6144]{2,1,0:T(8,128)(2,1)S(1)}, u32[]{:S(2)}, u32[]{:S(2)}) async-start(bf16[8,8,6144]{2,1,0:T(8,128)(2,1)} %get-tuple-element.20), calls=%async_computation.1 | async-start | bytes 1572864 | tf_op jit(solution)/shard_map/all_to_all | solution.py:144
  118.5 11.7 %all-to-all-done.1 = bf16[8,8,6144]{2,1,0:T(8,128)(2,1)S(1)} async-done(((bf16[8,8,6144]{2,1,0:T(8,128)(2,1)}), bf16[8,8,6144]{2,1,0:T(8,128)(2,1)S(1)}, u32[]{:S(2)}, u32[]{:S(2)}) %all-to-all-start.1) | async-done | bytes 786464 | tf_op jit(solution)/shard_map/all_to_all | solution.py:144
  130.3 3.5 all-to-all-start.2
  135.3 2.6 collective-permute-start.2
  138.7 7.9 %all-to-all-done.2 = bf16[8,8,6144]{2,1,0:T(8,128)(2,1)S(1)} async-done(((bf16[8,8,6144]{2,1,0:T(8,128)(2,1)}), bf16[8,8,6144]{2,1,0:T(8,128)(2,1)S(1)}, u32[]{:S(2)}, u32[]{:S(2)}) %all-to-all-start.2) | async-done | bytes 786464 | tf_op jit(solution)/shard_map/all_to_all | solution.py:144
  147.8 2.6 collective-permute-start.6
  151.3 17.9 %collective-permute-done.1 = bf16[64,6144]{1,0:T(8,128)(2,1)S(1)} collective-permute-done((bf16[64,6144]{1,0:T(8,128)(2,1)S(1)}, bf16[64,6144]{1,0:T(8,128)(2,1)S(1)}, u32[]{:S(2)}, u32[]{:S(2)}) %collective-permute-start.1) | collective-permute-done | bytes 786464 | tf_op jit(solution)/shard_map/ppermute | solution.py:49
  169.3 5.0 %collective-permute-start.7 = (bf16[64,6144]{1,0:T(8,128)(2,1)S(1)}, bf16[64,6144]{1,0:T(8,128)(2,1)S(1)}, u32[]{:S(2)}, u32[]{:S(2)}) collective-permute-start(bf16[64,6144]{1,0:T(8,128)(2,1)S(1)} %bitcast.124), channel_id=1, source_target_pairs={{0,96},{16,112},{32,0},{48,16},{64,32},{80,48},{96,64},{112,80},{1... | collective-permute-start | bytes 2359304 | tf_op jit(solution)/shard_map/ppermute | solution.py:49
  176.8 11.6 %collective-permute-done.5 = bf16[64,6144]{1,0:T(8,128)(2,1)S(1)} collective-permute-done((bf16[64,6144]{1,0:T(8,128)(2,1)S(1)}, bf16[64,6144]{1,0:T(8,128)(2,1)S(1)}, u32[]{:S(2)}, u32[]{:S(2)}) %collective-permute-start.5) | collective-permute-done | bytes 786464 | tf_op jit(solution)/shard_map/ppermute | solution.py:49
  188.3 2.7 collective-permute-done.6
  191.0 14.4 %collective-permute-done.7 = bf16[64,6144]{1,0:T(8,128)(2,1)S(1)} collective-permute-done((bf16[64,6144]{1,0:T(8,128)(2,1)S(1)}, bf16[64,6144]{1,0:T(8,128)(2,1)S(1)}, u32[]{:S(2)}, u32[]{:S(2)}) %collective-permute-start.7) | collective-permute-done | bytes 786464 | tf_op jit(solution)/shard_map/ppermute | solution.py:49
  216.1 6.3 %gather_fusion.1 = bf16[8,64,6144]{2,1,0:T(8,128)(2,1)} fusion(bf16[8,64,6144]{2,1,0:T(8,128)(2,1)} %constant_dynamic-update-slice_fusion, s32[1024]{0:T(1024)S(1)} %pad_clamp_fusion.1), kind=kCustom, calls=%fused_computation.clone | custom fusion | bytes 12582944 | tf_op jit(solution)/shard_map/jit(_take)/gather | solution.py:56
  222.5 3.9 %constant_dynamic-update-slice_fusion.5 = bf16[8,64,6144]{2,1,0:T(8,128)(2,1)} fusion(bf16[8,64,6144]{2,1,0:T(8,128)(2,1)} %constant_dynamic-update-slice_fusion.6, bf16[4,64,6144]{2,1,0:T(8,128)(2,1)} %collective-permute-done.8), kind=kLoop, calls=%fused_computation.70 | loop fusion | bytes 6291456 | tf_op jit(solution)/shard_map/concatenate | solution.py:52
  226.4 6.3 %gather_fusion.2 = bf16[8,64,6144]{2,1,0:T(8,128)(2,1)} fusion(bf16[8,64,6144]{2,1,0:T(8,128)(2,1)} %constant_dynamic-update-slice_fusion.5, s32[1024]{0:T(1024)S(1)} %pad_clamp_fusion.1), kind=kCustom, calls=%fused_computation.1.clone | custom fusion | bytes 12582944 | tf_op jit(solution)/shard_map/jit(_take)/gather | solution.py:56
  232.7 10.5 %broadcast_select_fusion.1 = (bf16[8,64,6144]{2,1,0:T(8,128)(2,1)}, bf16[8,64,6144]{2,1,0:T(8,128)(2,1)}) fusion(bf16[8,64,6144]{2,1,0:T(8,128)(2,1)} %gather_fusion.1, pred[8]{0:T(512)(128)(4,1)S(1)} %compare_and_fusion, bf16[8,64,6144]{2,1,0:T(8,128)(2,1)} %gather_fusion.2), kind=kLoop, calls=%fused_computation.18 | loop fusion | flops 6291456 | bytes 25165832 | tf_op jit(solution)/shard_map/jit(_take)/select_n | solution.py:56
  243.3 7.6 %fusion.8 = f32[512,512]{1,0:T(8,128)S(1)} fusion(bf16[512,6144]{1,0:T(8,128)(2,1)} %bitcast.129, bf16[1,6144,512]{2,1,0:T(8,128)(2,1)} %param.23), kind=kOutput, calls=%fused_computation.14 | convolution fusion | flops 3221225472 | bytes 13631488 | tf_op jit(solution)/shard_map/dot_general | solution.py:157
  250.9 3.5 fusion.17
  254.4 5.5 %convolution_convert_fusion.1 = bf16[512,6144]{1,0:T(8,128)(2,1)} fusion(bf16[512,512]{1,0:T(8,128)(2,1)S(1)} %fusion.17, bf16[1,512,6144]{2,1,0:T(8,128)(2,1)S(1)} %bitcast.149), kind=kOutput, calls=%fused_computation.4 | convolution fusion | flops 3224371200 | bytes 13107200 | tf_op jit(solution)/shard_map/dot_general | solution.py:160
  261.3 11.1 %collective-permute-done.9 = f32[16,6144]{1,0:T(8,128)S(1)} collective-permute-done((f32[16,6144]{1,0:T(8,128)S(1)}, f32[16,6144]{1,0:T(8,128)S(1)}, u32[]{:S(2)}, u32[]{:S(2)}) %collective-permute-start.9) | collective-permute-done | bytes 393248 | tf_op jit(solution)/shard_map/ppermute | solution.py:154
  272.4 7.8 %fusion.2 = f32[512,512]{1,0:T(8,128)S(1)} fusion(bf16[512,6144]{1,0:T(8,128)(2,1)} %bitcast.127, bf16[1,6144,512]{2,1,0:T(8,128)(2,1)} %param.24), kind=kOutput, calls=%fused_computation.8 | convolution fusion | flops 3221225472 | bytes 13631488 | tf_op jit(solution)/shard_map/dot_general | solution.py:158
  280.3 7.8 %fusion.6 = f32[512,512]{1,0:T(8,128)S(1)} fusion(bf16[512,6144]{1,0:T(8,128)(2,1)} %bitcast.128, bf16[1,6144,512]{2,1,0:T(8,128)(2,1)} %param.23), kind=kOutput, calls=%fused_computation.12 | convolution fusion | flops 3221225472 | bytes 13631488 | tf_op jit(solution)/shard_map/dot_general | solution.py:157
  288.1 5.4 %convolution_convert_fusion = bf16[512,6144]{1,0:T(8,128)(2,1)} fusion(bf16[1,512,6144]{2,1,0:T(8,128)(2,1)S(1)} %bitcast.151, f32[512,512]{1,0:T(8,128)S(1)} %fusion.2, f32[512,512]{1,0:T(8,128)S(1)} %fusion.6), kind=kOutput, calls=%fused_computation.3 | convolution fusion | flops 3225944064 | bytes 14680064 | tf_op jit(solution)/shard_map/dot_general | solution.py:160
  293.5 8.6 %reduce-scatter.3.cloned.1.call-done = bf16[64,6144]{1,0:T(8,128)(2,1)} async-done(((bf16[512,6144]{1,0:T(8,128)(2,1)}), bf16[64,6144]{1,0:T(8,128)(2,1)}) %reduce-scatter.3.cloned.1.call-update) | async-done | bytes 786448 | tf_op jit(solution)/shard_map/reduce_scatter | solution.py:161
  302.1 6.7 %all-to-all-start.3 = ((bf16[8,8,6144]{2,1,0:T(8,128)(2,1)}), bf16[8,8,6144]{2,1,0:T(8,128)(2,1)S(1)}, u32[]{:S(2)}, u32[]{:S(2)}) async-start(bf16[8,8,6144]{2,1,0:T(8,128)(2,1)} %bitcast.138), calls=%async_computation.4 | async-start | bytes 1572864 | tf_op jit(solution)/shard_map/all_to_all | solution.py:163
  309.1 37.8 %reduce-scatter.5.cloned.1.call-done = bf16[64,6144]{1,0:T(8,128)(2,1)} async-done(((bf16[512,6144]{1,0:T(8,128)(2,1)}), bf16[64,6144]{1,0:T(8,128)(2,1)}) %reduce-scatter.5.cloned.1.call-update) | async-done | bytes 786448 | tf_op jit(solution)/shard_map/reduce_scatter | solution.py:161
  346.8 6.7 %all-to-all-start.4 = ((bf16[8,8,6144]{2,1,0:T(8,128)(2,1)}), bf16[8,8,6144]{2,1,0:T(8,128)(2,1)}, u32[]{:S(2)}, u32[]{:S(2)}) async-start(bf16[8,8,6144]{2,1,0:T(8,128)(2,1)} %bitcast.137), calls=%async_computation.6 | async-start | bytes 1572864 | tf_op jit(solution)/shard_map/all_to_all | solution.py:163
  353.9 13.7 %all-to-all-done.4 = bf16[8,8,6144]{2,1,0:T(8,128)(2,1)} async-done(((bf16[8,8,6144]{2,1,0:T(8,128)(2,1)}), bf16[8,8,6144]{2,1,0:T(8,128)(2,1)}, u32[]{:S(2)}, u32[]{:S(2)}) %all-to-all-start.4) | async-done | bytes 786464 | tf_op jit(solution)/shard_map/all_to_all | solution.py:163
  372.1 9.7 %collective-permute-done.10 = bf16[32,6144]{1,0:T(8,128)(2,1)S(1)} collective-permute-done((bf16[32,6144]{1,0:T(8,128)(2,1)S(1)}, bf16[32,6144]{1,0:T(8,128)(2,1)S(1)}, u32[]{:S(2)}, u32[]{:S(2)}) %collective-permute-start.10) | collective-permute-done | bytes 393248 | tf_op jit(solution)/shard_map/ppermute | solution.py:179
  (133 shorter events, 47.8 us)
Async XLA Ops:
  6.5 347.0 %copy-start = (bf16[6144,8]{0,1:T(8,128)(2,1)S(1)}, bf16[6144,8]{0,1:T(8,128)(2,1)}, u32[]{:S(2)}) copy-start(bf16[6144,8]{0,1:T(8,128)(2,1)} %param.21) | copy-start | bytes 294916
  6.5 31.7 %all-gather.3.cloned.1.call-start = ((), (), s32[]{:S(2)}) async-start(), calls=%async_computation.9 | async-start | bytes 3594240 | tf_op jit(solution)/shard_map/all_gather | solution.py:86
  45.6 9.0 %copy-start.11 = (s32[32,2]{0,1:T(2,128)S(1)}, s32[32,2]{0,1:T(2,128)}, u32[]{:S(2)}) copy-start(s32[32,2]{0,1:T(2,128)} %param.22) | copy-start | bytes 772
  47.7 55.9 %copy-start.10 = (f32[6144]{0:T(1024)S(1)}, f32[6144]{0:T(1024)}, u32[]{:S(2)}) copy-start(f32[6144]{0:T(1024)} %param.20) | copy-start | bytes 73732
  47.7 54.7 %all-to-all-start = ((bf16[16,16,6144]{2,1,0:T(8,128)(2,1)}), bf16[16,16,6144]{2,1,0:T(8,128)(2,1)S(1)}, u32[]{:S(2)}, u32[]{:S(2)}) async-start(bf16[16,16,6144]{2,1,0:T(8,128)(2,1)} %bitcast.117), calls=%async_computation | async-start | bytes 6291456 | tf_op jit(solution)/shard_map/all_to_all | solution.py:116
  103.7 6.6 %collective-permute-start = (bf16[16,6144]{1,0:T(8,128)(2,1)S(1)}, bf16[16,6144]{1,0:T(8,128)(2,1)S(1)}, u32[]{:S(2)}, u32[]{:S(2)}) collective-permute-start(bf16[16,6144]{1,0:T(8,128)(2,1)S(1)} %multiply_convert_fusion.2), channel_id=1, source_target_pairs={{0,1},{1,0},{2,3},{3,2},{4,5},{5,4},{6,7},{7,6},{8,9},{9,8},{10,11... | collective-permute-start | bytes 589832 | tf_op jit(solution)/shard_map/ppermute | solution.py:34
  114.0 16.2 %all-to-all-start.1 = ((bf16[8,8,6144]{2,1,0:T(8,128)(2,1)}), bf16[8,8,6144]{2,1,0:T(8,128)(2,1)S(1)}, u32[]{:S(2)}, u32[]{:S(2)}) async-start(bf16[8,8,6144]{2,1,0:T(8,128)(2,1)} %get-tuple-element.20), calls=%async_computation.1 | async-start | bytes 1572864 | tf_op jit(solution)/shard_map/all_to_all | solution.py:144
  130.3 16.4 %all-to-all-start.2 = ((bf16[8,8,6144]{2,1,0:T(8,128)(2,1)}), bf16[8,8,6144]{2,1,0:T(8,128)(2,1)S(1)}, u32[]{:S(2)}, u32[]{:S(2)}) async-start(bf16[8,8,6144]{2,1,0:T(8,128)(2,1)} %get-tuple-element.21), calls=%async_computation.2 | async-start | bytes 1572864 | tf_op jit(solution)/shard_map/all_to_all | solution.py:144
  133.8 168.3 %reduce-scatter.3.cloned.1.call-start = ((), (), s32[]{:S(2)}) async-start(), calls=%async_computation.7 | async-start | bytes 7077888 | tf_op jit(solution)/shard_map/reduce_scatter | solution.py:161
  134.0 35.2 %collective-permute-start.1 = (bf16[64,6144]{1,0:T(8,128)(2,1)S(1)}, bf16[64,6144]{1,0:T(8,128)(2,1)S(1)}, u32[]{:S(2)}, u32[]{:S(2)}) collective-permute-start(bf16[64,6144]{1,0:T(8,128)(2,1)S(1)} %bitcast.118), channel_id=1, source_target_pairs={{0,32},{16,48},{32,64},{48,80},{64,96},{80,112},{96,0},{112,16},{1... | collective-permute-start | bytes 2359304 | tf_op jit(solution)/shard_map/ppermute | solution.py:49
  135.3 40.0 %collective-permute-start.2 = (bf16[64,6144]{1,0:T(8,128)(2,1)S(1)}, bf16[64,6144]{1,0:T(8,128)(2,1)S(1)}, u32[]{:S(2)}, u32[]{:S(2)}) collective-permute-start(bf16[64,6144]{1,0:T(8,128)(2,1)S(1)} %bitcast.119), channel_id=1, source_target_pairs={{0,64},{16,80},{32,96},{48,112},{64,0},{80,16},{96,32},{112,48},{1... | collective-permute-start | bytes 2359304 | tf_op jit(solution)/shard_map/ppermute | solution.py:49
  137.8 37.4 %collective-permute-start.3 = (bf16[64,6144]{1,0:T(8,128)(2,1)S(1)}, bf16[64,6144]{1,0:T(8,128)(2,1)}, u32[]{:S(2)}, u32[]{:S(2)}) collective-permute-start(bf16[64,6144]{1,0:T(8,128)(2,1)S(1)} %bitcast.120), channel_id=1, source_target_pairs={{0,96},{16,112},{32,0},{48,16},{64,32},{80,48},{96,64},{112,80},{1... | collective-permute-start | bytes 2359304 | tf_op jit(solution)/shard_map/ppermute | solution.py:49
  146.6 41.7 %collective-permute-start.5 = (bf16[64,6144]{1,0:T(8,128)(2,1)S(1)}, bf16[64,6144]{1,0:T(8,128)(2,1)S(1)}, u32[]{:S(2)}, u32[]{:S(2)}) collective-permute-start(bf16[64,6144]{1,0:T(8,128)(2,1)S(1)} %bitcast.122), channel_id=1, source_target_pairs={{0,32},{16,48},{32,64},{48,80},{64,96},{80,112},{96,0},{112,16},{1... | collective-permute-start | bytes 2359304 | tf_op jit(solution)/shard_map/ppermute | solution.py:49
  147.8 43.3 %collective-permute-start.6 = (bf16[64,6144]{1,0:T(8,128)(2,1)S(1)}, bf16[64,6144]{1,0:T(8,128)(2,1)S(1)}, u32[]{:S(2)}, u32[]{:S(2)}) collective-permute-start(bf16[64,6144]{1,0:T(8,128)(2,1)S(1)} %bitcast.123), channel_id=1, source_target_pairs={{0,64},{16,80},{32,96},{48,112},{64,0},{80,16},{96,32},{112,48},{1... | collective-permute-start | bytes 2359304 | tf_op jit(solution)/shard_map/ppermute | solution.py:49
  169.3 36.1 %collective-permute-start.7 = (bf16[64,6144]{1,0:T(8,128)(2,1)S(1)}, bf16[64,6144]{1,0:T(8,128)(2,1)S(1)}, u32[]{:S(2)}, u32[]{:S(2)}) collective-permute-start(bf16[64,6144]{1,0:T(8,128)(2,1)S(1)} %bitcast.124), channel_id=1, source_target_pairs={{0,96},{16,112},{32,0},{48,16},{64,32},{80,48},{96,64},{112,80},{1... | collective-permute-start | bytes 2359304 | tf_op jit(solution)/shard_map/ppermute | solution.py:49
  176.7 37.4 %collective-permute-start.4 = (bf16[4,64,6144]{2,1,0:T(8,128)(2,1)S(1)}, bf16[4,64,6144]{2,1,0:T(8,128)(2,1)S(1)}, u32[]{:S(2)}, u32[]{:S(2)}) collective-permute-start(bf16[4,64,6144]{2,1,0:T(8,128)(2,1)S(1)} %pad_maximum_fusion), channel_id=1, source_target_pairs={{0,16},{16,0},{32,48},{48,32},{64,80},{80,64},{96,112},{112,96},{1... | collective-permute-start | bytes 9437192 | tf_op jit(solution)/shard_map/ppermute | solution.py:51
  207.3 15.2 %collective-permute-start.8 = (bf16[4,64,6144]{2,1,0:T(8,128)(2,1)}, bf16[4,64,6144]{2,1,0:T(8,128)(2,1)}, u32[]{:S(2)}, u32[]{:S(2)}) collective-permute-start(bf16[4,64,6144]{2,1,0:T(8,128)(2,1)} %pad_maximum_fusion.1), channel_id=1, source_target_pairs={{0,16},{16,0},{32,48},{48,32},{64,80},{80,64},{96,112},{112,96},{1... | collective-permute-start | bytes 9437192 | tf_op jit(solution)/shard_map/ppermute | solution.py:51
  232.7 18.1 %slice-start = ((s8[6291456]{0:T(1024)(128)(4,1)}), s8[2097152]{0:T(1024)(128)(4,1)S(1)}, s32[]{:S(2)}) async-start(s8[6291456]{0:T(1024)(128)(4,1)} %bitcast.146), calls=%async_computation.10 | async-start | bytes 4194304
  243.3 7.6 %copy-start.3 = (bf16[8,64,6144]{2,1,0:T(8,128)(2,1)S(1)}, bf16[8,64,6144]{2,1,0:T(8,128)(2,1)}, u32[]{:S(2)}) copy-start(bf16[8,64,6144]{2,1,0:T(8,128)(2,1)} %get-tuple-element.28) | copy-start | bytes 18874372
  243.3 7.6 %slice-start.1 = ((s8[6291456]{0:T(1024)(128)(4,1)}), s8[4194304]{0:T(1024)(128)(4,1)S(1)}, s32[]{:S(2)}) async-start(s8[6291456]{0:T(1024)(128)(4,1)} %bitcast.146), calls=%async_computation.11 | async-start | bytes 8388608
  243.3 11.1 %slice-start.2 = ((s8[6291456]{0:T(1024)(128)(4,1)}), s8[4194304]{0:T(1024)(128)(4,1)S(1)}, s32[]{:S(2)}) async-start(s8[6291456]{0:T(1024)(128)(4,1)} %bitcast.148), calls=%async_computation.12 | async-start | bytes 8388608
  250.9 3.5 slice-start.3
  259.9 86.9 %reduce-scatter.5.cloned.1.call-start = ((), (), s32[]{:S(2)}) async-start(), calls=%async_computation.8 | async-start | bytes 7077888 | tf_op jit(solution)/shard_map/reduce_scatter | solution.py:161
  260.9 11.5 %collective-permute-start.9 = (f32[16,6144]{1,0:T(8,128)S(1)}, f32[16,6144]{1,0:T(8,128)S(1)}, u32[]{:S(2)}, u32[]{:S(2)}) collective-permute-start(f32[16,6144]{1,0:T(8,128)S(1)} %copy-done.2), channel_id=1, source_target_pairs={{0,1},{1,0},{2,3},{3,2},{4,5},{5,4},{6,7},{7,6},{8,9},{9,8},{10,11... | collective-permute-start | bytes 1179656 | tf_op jit(solution)/shard_map/ppermute | solution.py:154
  272.4 7.9 %copy-start.8 = (f32[16,6144]{1,0:T(8,128)}, f32[16,6144]{1,0:T(8,128)S(1)}, u32[]{:S(2)}) copy-start(f32[16,6144]{1,0:T(8,128)S(1)} %collective-permute-done.9) | copy-start | bytes 1179652
  272.4 15.7 %slice-start.4 = ((s8[6291456]{0:T(1024)(128)(4,1)}), s8[4194304]{0:T(1024)(128)(4,1)S(1)}, s32[]{:S(2)}) async-start(s8[6291456]{0:T(1024)(128)(4,1)} %bitcast.150), calls=%async_computation.14 | async-start | bytes 8388608
  280.3 7.8 %slice-start.5 = ((s8[6291456]{0:T(1024)(128)(4,1)}), s8[2097152]{0:T(1024)(128)(4,1)S(1)}, s32[]{:S(2)}) async-start(s8[6291456]{0:T(1024)(128)(4,1)} %bitcast.150), calls=%async_computation.15 | async-start | bytes 4194304
  293.5 60.1 %copy-start.7 = (bf16[16,6144]{1,0:T(8,128)(2,1)S(1)}, bf16[16,6144]{1,0:T(8,128)(2,1)}, u32[]{:S(2)}) copy-start(bf16[16,6144]{1,0:T(8,128)(2,1)} %copy-done.6) | copy-start | bytes 589828
  302.1 44.7 %all-to-all-start.3 = ((bf16[8,8,6144]{2,1,0:T(8,128)(2,1)}), bf16[8,8,6144]{2,1,0:T(8,128)(2,1)S(1)}, u32[]{:S(2)}, u32[]{:S(2)}) async-start(bf16[8,8,6144]{2,1,0:T(8,128)(2,1)} %bitcast.138), calls=%async_computation.4 | async-start | bytes 1572864 | tf_op jit(solution)/shard_map/all_to_all | solution.py:163
  346.8 20.7 %all-to-all-start.4 = ((bf16[8,8,6144]{2,1,0:T(8,128)(2,1)}), bf16[8,8,6144]{2,1,0:T(8,128)(2,1)}, u32[]{:S(2)}, u32[]{:S(2)}) async-start(bf16[8,8,6144]{2,1,0:T(8,128)(2,1)} %bitcast.137), calls=%async_computation.6 | async-start | bytes 1572864 | tf_op jit(solution)/shard_map/all_to_all | solution.py:163
  368.8 3.3 copy-start.9
  371.0 10.8 %collective-permute-start.10 = (bf16[32,6144]{1,0:T(8,128)(2,1)S(1)}, bf16[32,6144]{1,0:T(8,128)(2,1)S(1)}, u32[]{:S(2)}, u32[]{:S(2)}) collective-permute-start(bf16[32,6144]{1,0:T(8,128)(2,1)S(1)} %fusion.31), channel_id=1, source_target_pairs={{0,1},{1,0},{2,3},{3,2},{4,5},{5,4},{6,7},{7,6},{8,9},{9,8},{10,11... | collective-permute-start | bytes 1179656 | tf_op jit(solution)/shard_map/ppermute | solution.py:179
  (5 other events, 7.2 us)
Sparse Core Ops, SparseCore 0:
  9.2 29.0 all-gather.2
  260.0 42.0 reduce-scatter.2
  304.6 42.2 reduce-scatter.4

commit v9 on v6

--- a/solution.py
+++ b/solution.py
@@ -63,17 +63,28 @@
     span_rows = -(-span_rows // 8) * 8
     span_block = jnp.pad(spans.astype(jnp.bfloat16), (0, span_rows * local_width - spans.shape[0]))
     payload = jnp.concatenate([children, span_block.reshape(span_rows, local_width)], axis=0)
-    gathered = lax.all_gather(payload, "leaf", axis=0, tiled=False)
+    n_leaf = lax.axis_size("leaf")
+    n_z = n_leaf // 2
+    core = leaf_index % 2
+    z = leaf_index // 2
+    got = [payload]
+    for k in range(1, n_z):
+        perm = [(a * 2 + b, ((a + k) % n_z) * 2 + b) for a in range(n_z) for b in range(2)]
+        got.append(lax.ppermute(payload, "leaf", perm=perm))
+    swap = [(j, j ^ 1) for j in range(n_leaf)]
+    got = got + [lax.ppermute(block, "leaf", perm=swap) for block in got]
+    gathered = jnp.stack(got)
     span_table = gathered[:, child_rows:].reshape(gathered.shape[0], span_rows * local_width)
     count = child_order.shape[0]
     ids = jnp.arange(count, dtype=jnp.int32)
     inverse = jnp.sum(jnp.where(child_order[None, :] == ids[:, None], ids[None, :], 0), axis=1)
 
     def child_keys(child):
-        holder = child // children_here
+        owner = child // children_here
+        slot = jnp.where(owner % 2 == core, 0, n_z) + (z - owner // 2) % n_z
         offset = (child % children_here) * R
-        rows = lax.dynamic_slice(gathered, (holder, offset, 0), (1, R, local_width))[0]
-        marks = lax.dynamic_slice(span_table, (holder, offset), (1, R))[0]
+        rows = lax.dynamic_slice(gathered, (slot, offset, 0), (1, R, local_width))[0]
+        marks = lax.dynamic_slice(span_table, (slot, offset), (1, R))[0]
         return rows, marks.astype(jnp.int32)
 
     pieces = []

time: 341 us -> 340 us (level)
  waiting for transfers between devices: 201 us -> 192 us
  starting transfers between devices: 25.7 us -> 32.4 us
    all_gather x1 -> x0, waiting for transfers between devices: 21.6 us -> none  [per_device(): gathered = lax.all_gather(payload, 'leaf', axis=0, tiled=False)]
    ppermute x0 -> x7, waiting for transfers between devices: none -> 13.8 us  [the longest x3 12.3 us: per_device(): got.append(lax.ppermute(payload, 'leaf', perm=perm))]
    ppermute x0 -> x7, starting transfers between devices: none -> 6.19 us  [the longest x3 5.68 us: per_device(): got.append(lax.ppermute(payload, 'leaf', perm=perm))]
  transfers between devices with their start and end apart: 11 -> 17, of which waited for: 9 -> 11; matrix products, arithmetic and copies ran while one was open for 13% -> 13% of each run, Pallas kernels for 0% -> 0%
where the time goes in v9:
time: 340 us; the launch traced here: 339 us
  waiting for transfers between devices  192 us (56%)
  matrix products  45.5 us (13%)
  blocking collectives  32.5 us (10%)
  starting transfers between devices  32.4 us (10%)
  between operations  18.9 us (6%)
  other arithmetic  9.42 us (3%)
  local copies, waits for them, and re-layouts  8.3 us (2%)
    reduce_scatter x2, waiting for transfers between devices, per_device(): part_rows = lax.psum_scatter(down, 'leaf', scatter_dimension=0, tiled=True)  62.6 us
    all_to_all x1, waiting for transfers between devices, per_device(): lax.all_to_all(term.reshape(group, share_rows, width), ('expert', 'tensor...  45.7 us
    all_gather x2, waiting for transfers between devices, per_device(): piece = lax.all_gather(arrived, 'leaf', axis=0, tiled=True)  42.5 us
    all_to_all x2, blocking collectives, per_device(): lax.all_to_all(outgoing[:, c * chunk_slots:(c + 1) * chunk_slots], 'exper...  32.5 us
    dot_general x2, matrix products, per_device(): up_v = jnp.dot(piece, w_up[0], preferred_element_type=jnp.float32)  14 us
    dot_general x2, matrix products, per_device(): gate_v = jnp.dot(piece, w_gate[0], preferred_element_type=jnp.float32)  14 us
    all_to_all x2, waiting for transfers between devices, per_device(): lax.all_to_all(part_rows.reshape(experts, chunk_slots, width), 'expert',...  13.6 us
    all_to_all x2, starting transfers between devices, per_device(): lax.all_to_all(part_rows.reshape(experts, chunk_slots, width), 'expert',...  13.4 us
  transfers between devices with their start and end apart: 17, of which 11 were waited for; matrix products, arithmetic and copies ran while one was open for 13% of the time, Pallas kernels for 0%

profile of v9, /device:TPU:32, one launch (start us, length us, event | category | flops | bytes accessed | tf_op | source)
XLA Modules:
  0.0 339.0 jit_solution(9105557310893746125)
XLA Ops:
  6.5 1.2 copy.66
  8.7 2.0 collective-permute-start
  10.7 1.2 collective-permute-start.1
  11.8 2.5 collective-permute-start.2
  22.2 9.5 %collective-permute-done = bf16[520,384]{0,1:T(8,128)(2,1)S(1)} collective-permute-done((bf16[520,384]{0,1:T(8,128)(2,1)S(1)}, bf16[520,384]{0,1:T(8,128)(2,1)S(1)}, u32[]{:S(2)}, u32[]{:S(2)}) %collective-permute-start) | collective-permute-done | bytes 399392 | tf_op jit(solution)/shard_map/ppermute | solution.py:73
  32.3 2.7 collective-permute-done.2
  35.4 1.5 collective-permute-done.6
  39.9 4.2 %fusion.53 = f32[256,6144]{1,0:T(8,128)S(1)} fusion(bf16[256,384]{0,1:T(8,128)(2,1)S(1)} %bitcast.123, bf16[384,6144]{1,0:T(8,128)(2,1)} %param.17), kind=kOutput, calls=%fused_computation.97 | convolution fusion | flops 1207959552 | bytes 11206656 | tf_op jit(solution)/shard_map/dot_general | solution.py:99
  44.3 2.1 convert_element_type.78
  46.3 7.2 %all-to-all-start = ((bf16[16,16,6144]{2,1,0:T(8,128)(2,1)}), bf16[16,16,6144]{2,1,0:T(8,128)(2,1)S(1)}, u32[]{:S(2)}, u32[]{:S(2)}) async-start(bf16[16,16,6144]{2,1,0:T(8,128)(2,1)} %bitcast.113), calls=%async_computation | async-start | bytes 6291456 | tf_op jit(solution)/shard_map/all_to_all | solution.py:107
  54.3 45.7 %all-to-all-done = bf16[16,16,6144]{2,1,0:T(8,128)(2,1)S(1)} async-done(((bf16[16,16,6144]{2,1,0:T(8,128)(2,1)}), bf16[16,16,6144]{2,1,0:T(8,128)(2,1)S(1)}, u32[]{:S(2)}, u32[]{:S(2)}) %all-to-all-start) | async-done | bytes 3145760 | tf_op jit(solution)/shard_map/all_to_all | solution.py:107
  101.3 2.8 collective-permute-start.7
  104.2 4.0 %collective-permute-done.7 = bf16[16,6144]{1,0:T(8,128)(2,1)S(1)} collective-permute-done((bf16[16,6144]{1,0:T(8,128)(2,1)S(1)}, bf16[16,6144]{1,0:T(8,128)(2,1)S(1)}, u32[]{:S(2)}, u32[]{:S(2)}) %collective-permute-start.7) | collective-permute-done | bytes 196640 | tf_op jit(solution)/shard_map/ppermute | solution.py:34
  108.2 1.2 broadcast_select_fusion.3
  110.1 17.8 %all_to_all.25 = bf16[8,8,6144]{2,1,0:T(8,128)(2,1)} all-to-all(bf16[8,8,6144]{2,1,0:T(8,128)(2,1)S(1)} %get-tuple-element.19), channel_id=1, replica_groups=mesh['leaf'=8,'expert'=8,'tensor'=2] {'expert'}, dimensions={0} | all-to-all | bytes 1572864 | tf_op jit(solution)/shard_map/all_to_all | solution.py:135
  128.0 14.6 %all_to_all.26 = bf16[8,8,6144]{2,1,0:T(8,128)(2,1)} all-to-all(bf16[8,8,6144]{2,1,0:T(8,128)(2,1)S(1)} %get-tuple-element.20), channel_id=1, replica_groups=mesh['leaf'=8,'expert'=8,'tensor'=2] {'expert'}, dimensions={0} | all-to-all | bytes 1572864 | tf_op jit(solution)/shard_map/all_to_all | solution.py:135
  142.9 22.4 %all-gather.3.cloned.1.call-done = bf16[512,6144]{1,0:T(8,128)(2,1)} async-done(((bf16[64,6144]{1,0:T(8,128)(2,1)}), bf16[512,6144]{1,0:T(8,128)(2,1)}) %all-gather.3.cloned.1.call-update) | async-done | bytes 6291472 | tf_op jit(solution)/shard_map/all_gather | solution.py:142
  165.3 8.2 %fusion.8 = f32[512,512]{1,0:T(8,128)S(1)} fusion(bf16[512,6144]{1,0:T(8,128)(2,1)} %all-gather.3.cloned.1.call-done, bf16[1,6144,512]{2,1,0:T(8,128)(2,1)} %param.21), kind=kOutput, calls=%fused_computation.12 | convolution fusion | flops 3221225472 | bytes 13631488 | tf_op jit(solution)/shard_map/dot_general | solution.py:148
  173.5 6.4 %fusion.17 = bf16[512,512]{1,0:T(8,128)(2,1)S(1)} fusion(bf16[512,6144]{1,0:T(8,128)(2,1)S(1)} %copy-done.7, bf16[1,6144,512]{2,1,0:T(8,128)(2,1)} %param.22, f32[512,512]{1,0:T(8,128)S(1)} %fusion.8), kind=kOutput, calls=%fused_computation.23 | convolution fusion | flops 3222798336 | bytes 14155776 | tf_op jit(solution)/shard_map/dot_general | solution.py:149
  180.0 5.4 %convolution_convert_fusion.1 = bf16[512,6144]{1,0:T(8,128)(2,1)} fusion(bf16[512,512]{1,0:T(8,128)(2,1)S(1)} %fusion.17, bf16[1,512,6144]{2,1,0:T(8,128)(2,1)S(1)} %bitcast.127), kind=kOutput, calls=%fused_computation.2 | convolution fusion | flops 3224371200 | bytes 13107200 | tf_op jit(solution)/shard_map/dot_general | solution.py:151
  186.4 1.5 collective-permute-start.8
  187.9 20.1 %all-gather.5.cloned.1.call-done = bf16[512,6144]{1,0:T(8,128)(2,1)} async-done(((bf16[64,6144]{1,0:T(8,128)(2,1)}), bf16[512,6144]{1,0:T(8,128)(2,1)}) %all-gather.5.cloned.1.call-update) | async-done | bytes 6291472 | tf_op jit(solution)/shard_map/all_gather | solution.py:142
  208.0 7.6 %fusion.2 = f32[512,512]{1,0:T(8,128)S(1)} fusion(bf16[512,6144]{1,0:T(8,128)(2,1)} %all-gather.5.cloned.1.call-done, bf16[1,6144,512]{2,1,0:T(8,128)(2,1)} %param.22), kind=kOutput, calls=%fused_computation.6 | convolution fusion | flops 3221225472 | bytes 13631488 | tf_op jit(solution)/shard_map/dot_general | solution.py:149
  215.7 5.7 %fusion.6 = f32[512,512]{1,0:T(8,128)S(1)} fusion(bf16[512,6144]{1,0:T(8,128)(2,1)S(1)} %copy-done.6, bf16[1,6144,512]{2,1,0:T(8,128)(2,1)} %param.21), kind=kOutput, calls=%fused_computation.10 | convolution fusion | flops 3221225472 | bytes 13631488 | tf_op jit(solution)/shard_map/dot_general | solution.py:148
  221.4 5.4 %convolution_convert_fusion = bf16[512,6144]{1,0:T(8,128)(2,1)} fusion(bf16[1,512,6144]{2,1,0:T(8,128)(2,1)S(1)} %bitcast.129, f32[512,512]{1,0:T(8,128)S(1)} %fusion.2, f32[512,512]{1,0:T(8,128)S(1)} %fusion.6), kind=kOutput, calls=%fused_computation.1 | convolution fusion | flops 3225944064 | bytes 14680064 | tf_op jit(solution)/shard_map/dot_general | solution.py:151
  226.9 25.0 %reduce-scatter.3.cloned.1.call-done = bf16[64,6144]{1,0:T(8,128)(2,1)} async-done(((bf16[512,6144]{1,0:T(8,128)(2,1)}), bf16[64,6144]{1,0:T(8,128)(2,1)}) %reduce-scatter.3.cloned.1.call-update) | async-done | bytes 786448 | tf_op jit(solution)/shard_map/reduce_scatter | solution.py:152
  251.8 6.7 %all-to-all-start.3 = ((bf16[8,8,6144]{2,1,0:T(8,128)(2,1)}), bf16[8,8,6144]{2,1,0:T(8,128)(2,1)S(1)}, u32[]{:S(2)}, u32[]{:S(2)}) async-start(bf16[8,8,6144]{2,1,0:T(8,128)(2,1)} %bitcast.118), calls=%async_computation.4 | async-start | bytes 1572864 | tf_op jit(solution)/shard_map/all_to_all | solution.py:154
  258.8 37.7 %reduce-scatter.5.cloned.1.call-done = bf16[64,6144]{1,0:T(8,128)(2,1)} async-done(((bf16[512,6144]{1,0:T(8,128)(2,1)}), bf16[64,6144]{1,0:T(8,128)(2,1)}) %reduce-scatter.5.cloned.1.call-update) | async-done | bytes 786448 | tf_op jit(solution)/shard_map/reduce_scatter | solution.py:152
  296.4 6.7 %all-to-all-start.4 = ((bf16[8,8,6144]{2,1,0:T(8,128)(2,1)}), bf16[8,8,6144]{2,1,0:T(8,128)(2,1)}, u32[]{:S(2)}, u32[]{:S(2)}) async-start(bf16[8,8,6144]{2,1,0:T(8,128)(2,1)} %bitcast.119), calls=%async_computation.6 | async-start | bytes 1572864 | tf_op jit(solution)/shard_map/all_to_all | solution.py:154
  303.4 13.6 %all-to-all-done.4 = bf16[8,8,6144]{2,1,0:T(8,128)(2,1)} async-done(((bf16[8,8,6144]{2,1,0:T(8,128)(2,1)}), bf16[8,8,6144]{2,1,0:T(8,128)(2,1)}, u32[]{:S(2)}, u32[]{:S(2)}) %all-to-all-start.4) | async-done | bytes 786464 | tf_op jit(solution)/shard_map/all_to_all | solution.py:154
  317.1 1.2 pad_maximum_fusion
  321.7 9.6 %collective-permute-done.9 = bf16[32,6144]{1,0:T(8,128)(2,1)S(1)} collective-permute-done((bf16[32,6144]{1,0:T(8,128)(2,1)S(1)}, bf16[32,6144]{1,0:T(8,128)(2,1)S(1)}, u32[]{:S(2)}, u32[]{:S(2)}) %collective-permute-start.9) | collective-permute-done | bytes 393248 | tf_op jit(solution)/shard_map/ppermute | solution.py:170
  (108 shorter events, 16.5 us)
Async XLA Ops:
  6.5 296.6 %copy-start = (bf16[6144,8]{0,1:T(8,128)(2,1)S(1)}, bf16[6144,8]{0,1:T(8,128)(2,1)}, u32[]{:S(2)}) copy-start(bf16[6144,8]{0,1:T(8,128)(2,1)} %param.19) | copy-start | bytes 294916
  8.7 23.0 %collective-permute-start = (bf16[520,384]{0,1:T(8,128)(2,1)S(1)}, bf16[520,384]{0,1:T(8,128)(2,1)S(1)}, u32[]{:S(2)}, u32[]{:S(2)}) collective-permute-start(bf16[520,384]{0,1:T(8,128)(2,1)S(1)} %pad_maximum_fusion.1), channel_id=1, source_target_pairs={{0,32},{16,48},{32,64},{48,80},{64,96},{80,112},{96,0},{112,16},{1... | collective-permute-start | bytes 1198088 | tf_op jit(solution)/shard_map/ppermute | solution.py:73
  10.7 21.1 %collective-permute-start.1 = (bf16[520,384]{0,1:T(8,128)(2,1)S(1)}, bf16[520,384]{0,1:T(8,128)(2,1)S(1)}, u32[]{:S(2)}, u32[]{:S(2)}) collective-permute-start(bf16[520,384]{0,1:T(8,128)(2,1)S(1)} %pad_maximum_fusion.1), channel_id=1, source_target_pairs={{0,64},{16,80},{32,96},{48,112},{64,0},{80,16},{96,32},{112,48},{1... | collective-permute-start | bytes 1198088 | tf_op jit(solution)/shard_map/ppermute | solution.py:73
  11.8 23.2 %collective-permute-start.2 = (bf16[520,384]{0,1:T(8,128)(2,1)S(1)}, bf16[520,384]{0,1:T(8,128)(2,1)S(1)}, u32[]{:S(2)}, u32[]{:S(2)}) collective-permute-start(bf16[520,384]{0,1:T(8,128)(2,1)S(1)} %pad_maximum_fusion.1), channel_id=1, source_target_pairs={{0,96},{16,112},{32,0},{48,16},{64,32},{80,48},{96,64},{112,80},{1... | collective-permute-start | bytes 1198088 | tf_op jit(solution)/shard_map/ppermute | solution.py:73
  14.3 20.8 %collective-permute-start.3 = (bf16[520,384]{0,1:T(8,128)(2,1)S(1)}, bf16[520,384]{0,1:T(8,128)(2,1)S(1)}, u32[]{:S(2)}, u32[]{:S(2)}) collective-permute-start(bf16[520,384]{0,1:T(8,128)(2,1)S(1)} %pad_maximum_fusion.1), channel_id=1, source_target_pairs={{0,16},{16,0},{32,48},{48,32},{64,80},{80,64},{96,112},{112,96},{1... | collective-permute-start | bytes 1198088 | tf_op jit(solution)/shard_map/ppermute | solution.py:75
  31.7 3.6 %collective-permute-start.4 = (bf16[520,384]{0,1:T(8,128)(2,1)S(1)}, bf16[520,384]{0,1:T(8,128)(2,1)S(1)}, u32[]{:S(2)}, u32[]{:S(2)}) collective-permute-start(bf16[520,384]{0,1:T(8,128)(2,1)S(1)} %collective-permute-done), channel_id=1, source_target_pairs={{0,16},{16,0},{32,48},{48,32},{64,80},{80,64},{96,112},{112,96},{1... | collective-permute-start | bytes 1198088 | tf_op jit(solution)/shard_map/ppermute | solution.py:75
  31.7 3.6 %collective-permute-start.5 = (bf16[520,384]{0,1:T(8,128)(2,1)S(1)}, bf16[520,384]{0,1:T(8,128)(2,1)S(1)}, u32[]{:S(2)}, u32[]{:S(2)}) collective-permute-start(bf16[520,384]{0,1:T(8,128)(2,1)S(1)} %collective-permute-done.1), channel_id=1, source_target_pairs={{0,16},{16,0},{32,48},{48,32},{64,80},{80,64},{96,112},{112,96},{1... | collective-permute-start | bytes 1198088 | tf_op jit(solution)/shard_map/ppermute | solution.py:75
  35.0 1.9 collective-permute-start.6
  35.2 2.9 copy-start.8
  39.9 4.2 %copy-start.3 = (bf16[256,384]{1,0:T(8,128)(2,1)S(1)}, bf16[256,384]{1,0:T(8,128)(2,1)}, u32[]{:S(2)}) copy-start(bf16[256,384]{1,0:T(8,128)(2,1)} %param.12) | copy-start | bytes 589828
  46.3 7.2 %copy-start.5 = (s32[32,2]{0,1:T(2,128)S(1)}, s32[32,2]{0,1:T(2,128)}, u32[]{:S(2)}) copy-start(s32[32,2]{0,1:T(2,128)} %param.20) | copy-start | bytes 772
  46.3 54.9 %copy-start.4 = (f32[6144]{0:T(1024)S(1)}, f32[6144]{0:T(1024)}, u32[]{:S(2)}) copy-start(f32[6144]{0:T(1024)} %param.18) | copy-start | bytes 73732
  46.3 53.7 %all-to-all-start = ((bf16[16,16,6144]{2,1,0:T(8,128)(2,1)}), bf16[16,16,6144]{2,1,0:T(8,128)(2,1)S(1)}, u32[]{:S(2)}, u32[]{:S(2)}) async-start(bf16[16,16,6144]{2,1,0:T(8,128)(2,1)} %bitcast.113), calls=%async_computation | async-start | bytes 6291456 | tf_op jit(solution)/shard_map/all_to_all | solution.py:107
  53.5 111.8 %all-gather.3.cloned.1.call-start = ((), (), s32[]{:S(2)}) async-start(), calls=%async_computation.7 | async-start | bytes 7077888 | tf_op jit(solution)/shard_map/all_gather | solution.py:142
  100.5 0.7 copy-start.1
  101.3 6.9 %collective-permute-start.7 = (bf16[16,6144]{1,0:T(8,128)(2,1)S(1)}, bf16[16,6144]{1,0:T(8,128)(2,1)S(1)}, u32[]{:S(2)}, u32[]{:S(2)}) collective-permute-start(bf16[16,6144]{1,0:T(8,128)(2,1)S(1)} %multiply_convert_fusion.2), channel_id=1, source_target_pairs={{0,1},{1,0},{2,3},{3,2},{4,5},{5,4},{6,7},{7,6},{8,9},{9,8},{10,11... | collective-permute-start | bytes 589832 | tf_op jit(solution)/shard_map/ppermute | solution.py:34
  127.9 80.1 %all-gather.5.cloned.1.call-start = ((), (), s32[]{:S(2)}) async-start(), calls=%async_computation.8 | async-start | bytes 7077888 | tf_op jit(solution)/shard_map/all_gather | solution.py:142
  142.6 109.2 %reduce-scatter.3.cloned.1.call-start = ((), (), s32[]{:S(2)}) async-start(), calls=%async_computation.9 | async-start | bytes 7077888 | tf_op jit(solution)/shard_map/reduce_scatter | solution.py:152
  165.2 8.3 %copy-start.7 = (bf16[512,6144]{1,0:T(8,128)(2,1)S(1)}, bf16[512,6144]{1,0:T(8,128)(2,1)}, u32[]{:S(2)}) copy-start(bf16[512,6144]{1,0:T(8,128)(2,1)} %all-gather.3.cloned.1.call-done) | copy-start | bytes 18874372
  165.3 14.7 %slice-start = ((s8[6291456]{0:T(1024)(128)(4,1)}), s8[4194304]{0:T(1024)(128)(4,1)S(1)}, s32[]{:S(2)}) async-start(s8[6291456]{0:T(1024)(128)(4,1)} %bitcast.126), calls=%async_computation.11 | async-start | bytes 8388608
  173.5 6.4 %slice-start.1 = ((s8[6291456]{0:T(1024)(128)(4,1)}), s8[2097152]{0:T(1024)(128)(4,1)S(1)}, s32[]{:S(2)}) async-start(s8[6291456]{0:T(1024)(128)(4,1)} %bitcast.126), calls=%async_computation.12 | async-start | bytes 4194304
  185.4 1.0 copy-start.2
  185.4 111.0 %reduce-scatter.5.cloned.1.call-start = ((), (), s32[]{:S(2)}) async-start(), calls=%async_computation.10 | async-start | bytes 7077888 | tf_op jit(solution)/shard_map/reduce_scatter | solution.py:152
  186.4 21.6 %collective-permute-start.8 = (f32[16,6144]{1,0:T(8,128)S(1)}, f32[16,6144]{1,0:T(8,128)S(1)}, u32[]{:S(2)}, u32[]{:S(2)}) collective-permute-start(f32[16,6144]{1,0:T(8,128)S(1)} %copy-done.2), channel_id=1, source_target_pairs={{0,1},{1,0},{2,3},{3,2},{4,5},{5,4},{6,7},{7,6},{8,9},{9,8},{10,11... | collective-permute-start | bytes 1179656 | tf_op jit(solution)/shard_map/ppermute | solution.py:145
  208.0 7.6 %copy-start.6 = (bf16[512,6144]{1,0:T(8,128)(2,1)S(1)}, bf16[512,6144]{1,0:T(8,128)(2,1)}, u32[]{:S(2)}) copy-start(bf16[512,6144]{1,0:T(8,128)(2,1)} %all-gather.5.cloned.1.call-done) | copy-start | bytes 18874372
  208.0 13.4 %slice-start.2 = ((s8[6291456]{0:T(1024)(128)(4,1)}), s8[4194304]{0:T(1024)(128)(4,1)S(1)}, s32[]{:S(2)}) async-start(s8[6291456]{0:T(1024)(128)(4,1)} %bitcast.128), calls=%async_computation.13 | async-start | bytes 8388608
  215.6 5.8 %slice-start.3 = ((s8[6291456]{0:T(1024)(128)(4,1)}), s8[2097152]{0:T(1024)(128)(4,1)S(1)}, s32[]{:S(2)}) async-start(s8[6291456]{0:T(1024)(128)(4,1)} %bitcast.128), calls=%async_computation.14 | async-start | bytes 4194304
  251.8 44.6 %all-to-all-start.3 = ((bf16[8,8,6144]{2,1,0:T(8,128)(2,1)}), bf16[8,8,6144]{2,1,0:T(8,128)(2,1)S(1)}, u32[]{:S(2)}, u32[]{:S(2)}) async-start(bf16[8,8,6144]{2,1,0:T(8,128)(2,1)} %bitcast.118), calls=%async_computation.4 | async-start | bytes 1572864 | tf_op jit(solution)/shard_map/all_to_all | solution.py:154
  296.4 20.7 %all-to-all-start.4 = ((bf16[8,8,6144]{2,1,0:T(8,128)(2,1)}), bf16[8,8,6144]{2,1,0:T(8,128)(2,1)}, u32[]{:S(2)}, u32[]{:S(2)}) async-start(bf16[8,8,6144]{2,1,0:T(8,128)(2,1)} %bitcast.119), calls=%async_computation.6 | async-start | bytes 1572864 | tf_op jit(solution)/shard_map/all_to_all | solution.py:154
  320.5 10.8 %collective-permute-start.9 = (bf16[32,6144]{1,0:T(8,128)(2,1)S(1)}, bf16[32,6144]{1,0:T(8,128)(2,1)S(1)}, u32[]{:S(2)}, u32[]{:S(2)}) collective-permute-start(bf16[32,6144]{1,0:T(8,128)(2,1)S(1)} %fusion.31), channel_id=1, source_target_pairs={{0,1},{1,0},{2,3},{3,2},{4,5},{5,4},{6,7},{7,6},{8,9},{9,8},{10,11... | collective-permute-start | bytes 1179656 | tf_op jit(solution)/shard_map/ppermute | solution.py:170
Sparse Core Ops, SparseCore 0:
  128.0 37.1 all-gather.2
  166.9 41.0 all-gather.4
  210.4 41.3 reduce-scatter.2
  254.1 42.2 reduce-scatter.4

commit v10 on v9

--- a/solution.py
+++ b/solution.py
@@ -34,6 +34,25 @@
     other = lax.ppermute(share, "tensor", perm=[(0, 1), (1, 0)])
     low = lax.axis_index("tensor") == 0
     return jnp.concatenate([jnp.where(low, share, other), jnp.where(low, other, share)], axis=0)
+
+
+def leaf_spread(x):
+    n_leaf = lax.axis_size("leaf")
+    n_z = n_leaf // 2
+    got = [x]
+    for k in range(1, n_z):
+        perm = [(a * 2 + b, ((a + k) % n_z) * 2 + b) for a in range(n_z) for b in range(2)]
+        got.append(lax.ppermute(x, "leaf", perm=perm))
+    swap = [(j, j ^ 1) for j in range(n_leaf)]
+    return got + [lax.ppermute(block, "leaf", perm=swap) for block in got]
+
+
+def leaf_order():
+    n_leaf = lax.axis_size("leaf")
+    n_z = n_leaf // 2
+    index = lax.axis_index("leaf")
+    owner = jnp.arange(n_leaf, dtype=jnp.int32)
+    return jnp.where(owner % 2 == index % 2, 0, n_z) + (index // 2 - owner // 2) % n_z
 
 
 def per_device(
@@ -130,25 +149,33 @@
     outgoing = outgoing.reshape(experts, capacity, width)
     chunks = 2
     chunk_slots = capacity // chunks
-    returned = []
-    for c in range(chunks):
-        arrived = lax.all_to_all(
+    arrivals = [
+        lax.all_to_all(
             outgoing[:, c * chunk_slots : (c + 1) * chunk_slots],
             "expert",
             split_axis=0,
             concat_axis=0,
             tiled=True,
         ).reshape(-1, width)
-        piece = lax.all_gather(arrived, "leaf", axis=0, tiled=True)
-        if c == 0:
-            piece, share = lax.optimization_barrier((piece, share))
-            other_share = lax.ppermute(share, "tensor", perm=[(0, 1), (1, 0)])
-        else:
+        for c in range(chunks)
+    ]
+    first = lax.all_gather(arrivals[0], "leaf", axis=0, tiled=True)
+    spread = leaf_spread(arrivals[1])
+    first, share, *spread = lax.optimization_barrier((first, share, *spread))
+    other_share = lax.ppermute(share, "tensor", perm=[(0, 1), (1, 0)])
+    pieces_in = [first, jnp.concatenate(spread, axis=0)]
+    returned = []
+    for c in range(chunks):
+        piece = pieces_in[c]
+        if c == 1:
             piece, other_share = lax.optimization_barrier((piece, other_share))
         gate_v = jnp.dot(piece, w_gate[0], preferred_element_type=jnp.float32)
         up_v = jnp.dot(piece, w_up[0], preferred_element_type=jnp.float32)
         hidden = (jax.nn.silu(gate_v) * up_v).astype(jnp.bfloat16)
         down = jnp.dot(hidden, w_down[0], preferred_element_type=jnp.float32).astype(jnp.bfloat16)
+        if c != 0:
+            blocks = down.reshape(lax.axis_size("leaf"), -1, width)
+            down = jnp.take(blocks, leaf_order(), axis=0).reshape(-1, width)
         part_rows = lax.psum_scatter(down, "leaf", scatter_dimension=0, tiled=True)
         returned.append(
             lax.all_to_all(

time: 340 us -> 351 us (1.032)
  local copies, waits for them, and re-layouts: 8.3 us -> 19.9 us
  waiting for transfers between devices: 192 us -> 183 us
  other arithmetic: 9.42 us -> 16.7 us
  starting transfers between devices: 32.4 us -> 37 us
    ppermute x0 -> x7, waiting for transfers between devices: none -> 49.3 us  [the longest x3 49.2 us: leaf_spread(): got.append(lax.ppermute(x, 'leaf', perm=perm))]
    all_gather x2 -> x1, waiting for transfers between devices: 42.5 us -> 0.31 us  [per_device(): first = lax.all_gather(arrivals[0], 'leaf', axis=0, tiled=True)]
    reduce_scatter x2, waiting for transfers between devices: 62.6 us -> 40.3 us  [per_device(): part_rows = lax.psum_scatter(down, 'leaf', scatter_dimension=0, tiled=True)]
    ppermute x1, waiting for transfers between devices: 0.01 us -> 6.95 us  [per_device(): other_share = lax.ppermute(share, 'tensor', perm=[(0, 1), (1, 0)])]
    gather x0 -> x1, local copies, waits for them, and re-layouts: none -> 6.47 us  [per_device(): down = jnp.take(blocks, leaf_order(), axis=0).reshape(-1, width)]
    select_n x0 -> x2, other arithmetic: none -> 6.22 us  [per_device(): down = jnp.take(blocks, leaf_order(), axis=0).reshape(-1, width)]
    dot_general x2, matrix products: 14 us -> 9 us  [per_device(): gate_v = jnp.dot(piece, w_gate[0], preferred_element_type=jnp.float32)]
    ppermute x0 -> x7, starting transfers between devices: none -> 4.75 us  [the longest x3 4.39 us: leaf_spread(): got.append(lax.ppermute(x, 'leaf', perm=perm))]
  transfers between devices with their start and end apart: 17 -> 23, of which waited for: 11 -> 14; matrix products, arithmetic and copies ran while one was open for 13% -> 10% of each run, Pallas kernels for 0% -> 0%
where the time goes in v10:
time: 351 us; the launch traced here: 350 us
  waiting for transfers between devices  183 us (52%)
  matrix products  43.1 us (12%)
  starting transfers between devices  37 us (11%)
  blocking collectives  32 us (9%)
  local copies, waits for them, and re-layouts  19.9 us (6%)
  between operations  19.2 us (5%)
  other arithmetic  16.7 us (5%)
    ppermute x3, waiting for transfers between devices, leaf_spread(): got.append(lax.ppermute(x, 'leaf', perm=perm))  49.2 us
    all_to_all x1, waiting for transfers between devices, per_device(): lax.all_to_all(term.reshape(group, share_rows, width), ('expert', 'tensor...  45.8 us
    reduce_scatter x2, waiting for transfers between devices, per_device(): part_rows = lax.psum_scatter(down, 'leaf', scatter_dimension=0, tiled=True)  40.3 us
    all_to_all x2, blocking collectives, per_device(): lax.all_to_all(outgoing[:, c * chunk_slots:(c + 1) * chunk_slots], 'exper...  32 us
    dot_general x2, matrix products, per_device(): up_v = jnp.dot(piece, w_up[0], preferred_element_type=jnp.float32)  13.9 us
    all_to_all x2, waiting for transfers between devices, per_device(): lax.all_to_all(part_rows.reshape(experts, chunk_slots, width), 'expert',...  13.7 us
    dot_general x2, matrix products, per_device(): jnp.dot(hidden, w_down[0], preferred_element_type=jnp.float32)  13.5 us
    all_to_all x2, starting transfers between devices, per_device(): lax.all_to_all(part_rows.reshape(experts, chunk_slots, width), 'expert',...  13.4 us
  transfers between devices with their start and end apart: 23, of which 14 were waited for; matrix products, arithmetic and copies ran while one was open for 10% of the time, Pallas kernels for 0%

profile of v10, /device:TPU:32, one launch (start us, length us, event | category | flops | bytes accessed | tf_op | source)
XLA Modules:
  0.0 350.4 jit_solution(18058204620086758133)
XLA Ops:
  8.7 2.0 collective-permute-start
  11.8 2.5 collective-permute-start.2
  22.5 9.2 %collective-permute-done = bf16[520,384]{0,1:T(8,128)(2,1)S(1)} collective-permute-done((bf16[520,384]{0,1:T(8,128)(2,1)S(1)}, bf16[520,384]{0,1:T(8,128)(2,1)S(1)}, u32[]{:S(2)}, u32[]{:S(2)}) %collective-permute-start) | collective-permute-done | bytes 399392 | tf_op jit(solution)/shard_map/ppermute | solution.py:92
  32.3 2.7 collective-permute-done.2
  35.4 1.5 collective-permute-done.6
  39.9 4.2 %fusion.56 = f32[256,6144]{1,0:T(8,128)S(1)} fusion(bf16[256,384]{0,1:T(8,128)(2,1)S(1)} %bitcast.128, bf16[384,6144]{1,0:T(8,128)(2,1)} %param.17), kind=kOutput, calls=%fused_computation.135 | convolution fusion | flops 1207959552 | bytes 11206656 | tf_op jit(solution)/shard_map/dot_general | solution.py:118
  44.3 2.1 convert_element_type.78
  46.3 7.2 %all-to-all-start = ((bf16[16,16,6144]{2,1,0:T(8,128)(2,1)}), bf16[16,16,6144]{2,1,0:T(8,128)(2,1)S(1)}, u32[]{:S(2)}, u32[]{:S(2)}) async-start(bf16[16,16,6144]{2,1,0:T(8,128)(2,1)} %bitcast.113), calls=%async_computation | async-start | bytes 6291456 | tf_op jit(solution)/shard_map/all_to_all | solution.py:126
  54.3 45.8 %all-to-all-done = bf16[16,16,6144]{2,1,0:T(8,128)(2,1)S(1)} async-done(((bf16[16,16,6144]{2,1,0:T(8,128)(2,1)}), bf16[16,16,6144]{2,1,0:T(8,128)(2,1)S(1)}, u32[]{:S(2)}, u32[]{:S(2)}) %all-to-all-start) | async-done | bytes 3145760 | tf_op jit(solution)/shard_map/all_to_all | solution.py:126
  101.4 2.8 collective-permute-start.7
  104.3 4.0 %collective-permute-done.7 = bf16[16,6144]{1,0:T(8,128)(2,1)S(1)} collective-permute-done((bf16[16,6144]{1,0:T(8,128)(2,1)S(1)}, bf16[16,6144]{1,0:T(8,128)(2,1)S(1)}, u32[]{:S(2)}, u32[]{:S(2)}) %collective-permute-start.7) | collective-permute-done | bytes 196640 | tf_op jit(solution)/shard_map/ppermute | solution.py:34
  110.2 17.8 %all_to_all.25 = bf16[8,8,6144]{2,1,0:T(8,128)(2,1)} all-to-all(bf16[8,8,6144]{2,1,0:T(8,128)(2,1)S(1)} %get-tuple-element.36), channel_id=1, replica_groups=mesh['leaf'=8,'expert'=8,'tensor'=2] {'expert'}, dimensions={0} | all-to-all | bytes 1572864 | tf_op jit(solution)/shard_map/all_to_all | solution.py:153
  128.0 14.2 %all_to_all.26 = bf16[8,8,6144]{2,1,0:T(8,128)(2,1)S(1)} all-to-all(bf16[8,8,6144]{2,1,0:T(8,128)(2,1)S(1)} %get-tuple-element.35), channel_id=1, replica_groups=mesh['leaf'=8,'expert'=8,'tensor'=2] {'expert'}, dimensions={0} | all-to-all | bytes 1572864 | tf_op jit(solution)/shard_map/all_to_all | solution.py:153
  143.2 2.6 collective-permute-start.9
  146.6 32.8 %collective-permute-done.8 = bf16[64,6144]{1,0:T(8,128)(2,1)S(1)} collective-permute-done((bf16[64,6144]{1,0:T(8,128)(2,1)S(1)}, bf16[64,6144]{1,0:T(8,128)(2,1)S(1)}, u32[]{:S(2)}, u32[]{:S(2)}) %collective-permute-start.8) | collective-permute-done | bytes 786464 | tf_op jit(solution)/shard_map/ppermute | solution.py:45
  180.0 16.2 %collective-permute-done.10 = bf16[64,6144]{1,0:T(8,128)(2,1)S(1)} collective-permute-done((bf16[64,6144]{1,0:T(8,128)(2,1)S(1)}, bf16[64,6144]{1,0:T(8,128)(2,1)S(1)}, u32[]{:S(2)}, u32[]{:S(2)}) %collective-permute-start.10) | collective-permute-done | bytes 786464 | tf_op jit(solution)/shard_map/ppermute | solution.py:45
  199.0 8.1 %fusion.4 = f32[512,512]{1,0:T(8,128)S(1)} fusion(bf16[512,6144]{1,0:T(8,128)(2,1)} %all-gather.2.cloned.1.call-done, bf16[1,6144,512]{2,1,0:T(8,128)(2,1)} %param.22), kind=kOutput, calls=%fused_computation.10 | convolution fusion | flops 3221225472 | bytes 13631488 | tf_op jit(solution)/shard_map/dot_general | solution.py:173
  207.1 5.6 %fusion.8 = f32[512,512]{1,0:T(8,128)S(1)} fusion(bf16[512,6144]{1,0:T(8,128)(2,1)S(1)} %copy-done.13, bf16[1,6144,512]{2,1,0:T(8,128)(2,1)} %param.21), kind=kOutput, calls=%fused_computation.14 | convolution fusion | flops 3221225472 | bytes 13631488 | tf_op jit(solution)/shard_map/dot_general | solution.py:172
  212.7 8.2 %convolution_convert_fusion.1 = bf16[512,6144]{1,0:T(8,128)(2,1)} fusion(bf16[1,512,6144]{2,1,0:T(8,128)(2,1)} %param.23, f32[512,512]{1,0:T(8,128)S(1)} %fusion.4, f32[512,512]{1,0:T(8,128)S(1)} %fusion.8), kind=kOutput, calls=%fused_computation.3 | convolution fusion | flops 3225944064 | bytes 14680064 | tf_op jit(solution)/shard_map/dot_general | solution.py:175
  221.8 1.5 collective-permute-start.15
  226.2 7.0 %collective-permute-done.15 = f32[16,6144]{1,0:T(8,128)} collective-permute-done((f32[16,6144]{1,0:T(8,128)S(1)}, f32[16,6144]{1,0:T(8,128)}, u32[]{:S(2)}, u32[]{:S(2)}) %collective-permute-start.15) | collective-permute-done | bytes 393248 | tf_op jit(solution)/shard_map/ppermute | solution.py:165
  233.2 5.8 %fusion.2 = f32[512,512]{1,0:T(8,128)S(1)} fusion(bf16[512,6144]{1,0:T(8,128)(2,1)S(1)} %constant_dynamic-update-slice_fusion, bf16[1,6144,512]{2,1,0:T(8,128)(2,1)} %param.22), kind=kOutput, calls=%fused_computation.8 | convolution fusion | flops 3221225472 | bytes 13631488 | tf_op jit(solution)/shard_map/dot_general | solution.py:173
  239.1 3.4 fusion.6
  242.5 5.4 %convolution_convert_fusion = bf16[512,6144]{1,0:T(8,128)(2,1)} fusion(bf16[1,512,6144]{2,1,0:T(8,128)(2,1)S(1)} %bitcast.134, f32[512,512]{1,0:T(8,128)S(1)} %fusion.2, f32[512,512]{1,0:T(8,128)S(1)} %fusion.6), kind=kOutput, calls=%fused_computation.2 | convolution fusion | flops 3225944064 | bytes 14680064 | tf_op jit(solution)/shard_map/dot_general | solution.py:175
  247.9 6.5 %gather_fusion = bf16[8,64,6144]{2,1,0:T(8,128)(2,1)} fusion(bf16[8,64,6144]{2,1,0:T(8,128)(2,1)} %bitcast.114, s32[1024]{0:T(1024)S(1)} %pad_clamp_fusion.1), kind=kCustom, calls=%fused_computation | custom fusion | bytes 12582944 | tf_op jit(solution)/shard_map/jit(_take)/gather | solution.py:178
  254.3 6.2 %bitcast_select_fusion = bf16[512,6144]{1,0:T(8,128)(2,1)} fusion(bf16[8,64,6144]{2,1,0:T(8,128)(2,1)} %gather_fusion, pred[512]{0:T(512)(128)(4,1)S(1)} %broadcast_in_dim.81), kind=kLoop, calls=%fused_computation.5 | loop fusion | flops 3145728 | bytes 12583424 | tf_op jit(solution)/shard_map/jit(_take)/select_n | solution.py:178
  260.6 2.5 reduce-scatter.3.cloned.1.call-done
  263.1 6.7 %all-to-all-start.3 = ((bf16[8,8,6144]{2,1,0:T(8,128)(2,1)}), bf16[8,8,6144]{2,1,0:T(8,128)(2,1)S(1)}, u32[]{:S(2)}, u32[]{:S(2)}) async-start(bf16[8,8,6144]{2,1,0:T(8,128)(2,1)} %bitcast.123), calls=%async_computation.4 | async-start | bytes 1572864 | tf_op jit(solution)/shard_map/all_to_all | solution.py:181
  270.0 37.8 %reduce-scatter.5.cloned.1.call-done = bf16[64,6144]{1,0:T(8,128)(2,1)} async-done(((bf16[512,6144]{1,0:T(8,128)(2,1)}), bf16[64,6144]{1,0:T(8,128)(2,1)}) %reduce-scatter.5.cloned.1.call-update) | async-done | bytes 786448 | tf_op jit(solution)/shard_map/reduce_scatter | solution.py:179
  307.8 6.7 %all-to-all-start.4 = ((bf16[8,8,6144]{2,1,0:T(8,128)(2,1)}), bf16[8,8,6144]{2,1,0:T(8,128)(2,1)}, u32[]{:S(2)}, u32[]{:S(2)}) async-start(bf16[8,8,6144]{2,1,0:T(8,128)(2,1)} %bitcast.124), calls=%async_computation.6 | async-start | bytes 1572864 | tf_op jit(solution)/shard_map/all_to_all | solution.py:181
  314.8 13.7 %all-to-all-done.4 = bf16[8,8,6144]{2,1,0:T(8,128)(2,1)} async-done(((bf16[8,8,6144]{2,1,0:T(8,128)(2,1)}), bf16[8,8,6144]{2,1,0:T(8,128)(2,1)}, u32[]{:S(2)}, u32[]{:S(2)}) %all-to-all-start.4) | async-done | bytes 786464 | tf_op jit(solution)/shard_map/all_to_all | solution.py:181
  334.0 8.7 %collective-permute-done.16 = bf16[32,6144]{1,0:T(8,128)(2,1)S(1)} collective-permute-done((bf16[32,6144]{1,0:T(8,128)(2,1)S(1)}, bf16[32,6144]{1,0:T(8,128)(2,1)S(1)}, u32[]{:S(2)}, u32[]{:S(2)}) %collective-permute-start.16) | collective-permute-done | bytes 393248 | tf_op jit(solution)/shard_map/ppermute | solution.py:197
  (146 shorter events, 29.8 us)
Async XLA Ops:
  6.5 308.0 %copy-start = (bf16[6144,8]{0,1:T(8,128)(2,1)S(1)}, bf16[6144,8]{0,1:T(8,128)(2,1)}, u32[]{:S(2)}) copy-start(bf16[6144,8]{0,1:T(8,128)(2,1)} %param.19) | copy-start | bytes 294916
  8.7 23.0 %collective-permute-start = (bf16[520,384]{0,1:T(8,128)(2,1)S(1)}, bf16[520,384]{0,1:T(8,128)(2,1)S(1)}, u32[]{:S(2)}, u32[]{:S(2)}) collective-permute-start(bf16[520,384]{0,1:T(8,128)(2,1)S(1)} %pad_maximum_fusion.1), channel_id=1, source_target_pairs={{0,32},{16,48},{32,64},{48,80},{64,96},{80,112},{96,0},{112,16},{1... | collective-permute-start | bytes 1198088 | tf_op jit(solution)/shard_map/ppermute | solution.py:92
  10.7 21.1 %collective-permute-start.1 = (bf16[520,384]{0,1:T(8,128)(2,1)S(1)}, bf16[520,384]{0,1:T(8,128)(2,1)S(1)}, u32[]{:S(2)}, u32[]{:S(2)}) collective-permute-start(bf16[520,384]{0,1:T(8,128)(2,1)S(1)} %pad_maximum_fusion.1), channel_id=1, source_target_pairs={{0,64},{16,80},{32,96},{48,112},{64,0},{80,16},{96,32},{112,48},{1... | collective-permute-start | bytes 1198088 | tf_op jit(solution)/shard_map/ppermute | solution.py:92
  11.8 23.2 %collective-permute-start.2 = (bf16[520,384]{0,1:T(8,128)(2,1)S(1)}, bf16[520,384]{0,1:T(8,128)(2,1)S(1)}, u32[]{:S(2)}, u32[]{:S(2)}) collective-permute-start(bf16[520,384]{0,1:T(8,128)(2,1)S(1)} %pad_maximum_fusion.1), channel_id=1, source_target_pairs={{0,96},{16,112},{32,0},{48,16},{64,32},{80,48},{96,64},{112,80},{1... | collective-permute-start | bytes 1198088 | tf_op jit(solution)/shard_map/ppermute | solution.py:92
  14.3 20.8 %collective-permute-start.3 = (bf16[520,384]{0,1:T(8,128)(2,1)S(1)}, bf16[520,384]{0,1:T(8,128)(2,1)S(1)}, u32[]{:S(2)}, u32[]{:S(2)}) collective-permute-start(bf16[520,384]{0,1:T(8,128)(2,1)S(1)} %pad_maximum_fusion.1), channel_id=1, source_target_pairs={{0,16},{16,0},{32,48},{48,32},{64,80},{80,64},{96,112},{112,96},{1... | collective-permute-start | bytes 1198088 | tf_op jit(solution)/shard_map/ppermute | solution.py:94
  18.4 19.6 %copy-start.14 = (f32[3,16]{1,0:T(4,128)S(1)}, f32[3,16]{1,0:T(4,128)}, u32[]{:S(2)}) copy-start(f32[3,16]{1,0:T(4,128)} %param.16) | copy-start | bytes 580
  31.7 3.5 %collective-permute-start.4 = (bf16[520,384]{0,1:T(8,128)(2,1)S(1)}, bf16[520,384]{0,1:T(8,128)(2,1)S(1)}, u32[]{:S(2)}, u32[]{:S(2)}) collective-permute-start(bf16[520,384]{0,1:T(8,128)(2,1)S(1)} %collective-permute-done), channel_id=1, source_target_pairs={{0,16},{16,0},{32,48},{48,32},{64,80},{80,64},{96,112},{112,96},{1... | collective-permute-start | bytes 1198088 | tf_op jit(solution)/shard_map/ppermute | solution.py:94
  31.7 3.6 %collective-permute-start.5 = (bf16[520,384]{0,1:T(8,128)(2,1)S(1)}, bf16[520,384]{0,1:T(8,128)(2,1)S(1)}, u32[]{:S(2)}, u32[]{:S(2)}) collective-permute-start(bf16[520,384]{0,1:T(8,128)(2,1)S(1)} %collective-permute-done.1), channel_id=1, source_target_pairs={{0,16},{16,0},{32,48},{48,32},{64,80},{80,64},{96,112},{112,96},{1... | collective-permute-start | bytes 1198088 | tf_op jit(solution)/shard_map/ppermute | solution.py:94
  35.0 1.9 collective-permute-start.6
  39.9 4.2 %copy-start.3 = (bf16[256,384]{1,0:T(8,128)(2,1)S(1)}, bf16[256,384]{1,0:T(8,128)(2,1)}, u32[]{:S(2)}) copy-start(bf16[256,384]{1,0:T(8,128)(2,1)} %param.12) | copy-start | bytes 589828
  44.3 9.3 %copy-start.12 = (s32[32,2]{0,1:T(2,128)S(1)}, s32[32,2]{0,1:T(2,128)}, u32[]{:S(2)}) copy-start(s32[32,2]{0,1:T(2,128)} %param.20) | copy-start | bytes 772
  46.3 55.0 %copy-start.11 = (f32[6144]{0:T(1024)S(1)}, f32[6144]{0:T(1024)}, u32[]{:S(2)}) copy-start(f32[6144]{0:T(1024)} %param.18) | copy-start | bytes 73732
  46.3 53.8 %all-to-all-start = ((bf16[16,16,6144]{2,1,0:T(8,128)(2,1)}), bf16[16,16,6144]{2,1,0:T(8,128)(2,1)S(1)}, u32[]{:S(2)}, u32[]{:S(2)}) async-start(bf16[16,16,6144]{2,1,0:T(8,128)(2,1)} %bitcast.113), calls=%async_computation | async-start | bytes 6291456 | tf_op jit(solution)/shard_map/all_to_all | solution.py:126
  53.5 145.5 %all-gather.2.cloned.1.call-start = ((), (), s32[]{:S(2)}) async-start(), calls=%async_computation.7 | async-start | bytes 7077888 | tf_op jit(solution)/shard_map/all_gather | solution.py:162
  101.4 6.9 %collective-permute-start.7 = (bf16[16,6144]{1,0:T(8,128)(2,1)S(1)}, bf16[16,6144]{1,0:T(8,128)(2,1)S(1)}, u32[]{:S(2)}, u32[]{:S(2)}) collective-permute-start(bf16[16,6144]{1,0:T(8,128)(2,1)S(1)} %multiply_convert_fusion.4), channel_id=1, source_target_pairs={{0,1},{1,0},{2,3},{3,2},{4,5},{5,4},{6,7},{7,6},{8,9},{9,8},{10,11... | collective-permute-start | bytes 589832 | tf_op jit(solution)/shard_map/ppermute | solution.py:34
  128.0 135.1 %reduce-scatter.3.cloned.1.call-start = ((), (), s32[]{:S(2)}) async-start(), calls=%async_computation.8 | async-start | bytes 7077888 | tf_op jit(solution)/shard_map/reduce_scatter | solution.py:179
  142.3 37.2 %collective-permute-start.8 = (bf16[64,6144]{1,0:T(8,128)(2,1)S(1)}, bf16[64,6144]{1,0:T(8,128)(2,1)S(1)}, u32[]{:S(2)}, u32[]{:S(2)}) collective-permute-start(bf16[64,6144]{1,0:T(8,128)(2,1)S(1)} %bitcast.116), channel_id=1, source_target_pairs={{0,32},{16,48},{32,64},{48,80},{64,96},{80,112},{96,0},{112,16},{1... | collective-permute-start | bytes 2359304 | tf_op jit(solution)/shard_map/ppermute | solution.py:45
  143.2 36.5 %collective-permute-start.9 = (bf16[64,6144]{1,0:T(8,128)(2,1)S(1)}, bf16[64,6144]{1,0:T(8,128)(2,1)S(1)}, u32[]{:S(2)}, u32[]{:S(2)}) collective-permute-start(bf16[64,6144]{1,0:T(8,128)(2,1)S(1)} %bitcast.117), channel_id=1, source_target_pairs={{0,64},{16,80},{32,96},{48,112},{64,0},{80,16},{96,32},{112,48},{1... | collective-permute-start | bytes 2359304 | tf_op jit(solution)/shard_map/ppermute | solution.py:45
  145.8 50.5 %collective-permute-start.10 = (bf16[64,6144]{1,0:T(8,128)(2,1)S(1)}, bf16[64,6144]{1,0:T(8,128)(2,1)S(1)}, u32[]{:S(2)}, u32[]{:S(2)}) collective-permute-start(bf16[64,6144]{1,0:T(8,128)(2,1)S(1)} %bitcast.118), channel_id=1, source_target_pairs={{0,96},{16,112},{32,0},{48,16},{64,32},{80,48},{96,64},{112,80},{1... | collective-permute-start | bytes 2359304 | tf_op jit(solution)/shard_map/ppermute | solution.py:45
  146.6 49.6 %collective-permute-start.11 = (bf16[64,6144]{1,0:T(8,128)(2,1)S(1)}, bf16[64,6144]{1,0:T(8,128)(2,1)S(1)}, u32[]{:S(2)}, u32[]{:S(2)}) collective-permute-start(bf16[64,6144]{1,0:T(8,128)(2,1)S(1)} %bitcast.119), channel_id=1, source_target_pairs={{0,16},{16,0},{32,48},{48,32},{64,80},{80,64},{96,112},{112,96},{1... | collective-permute-start | bytes 2359304 | tf_op jit(solution)/shard_map/ppermute | solution.py:47
  179.5 16.8 %collective-permute-start.12 = (bf16[64,6144]{1,0:T(8,128)(2,1)S(1)}, bf16[64,6144]{1,0:T(8,128)(2,1)S(1)}, u32[]{:S(2)}, u32[]{:S(2)}) collective-permute-start(bf16[64,6144]{1,0:T(8,128)(2,1)S(1)} %collective-permute-done.8), channel_id=1, source_target_pairs={{0,16},{16,0},{32,48},{48,32},{64,80},{80,64},{96,112},{112,96},{1... | collective-permute-start | bytes 2359304 | tf_op jit(solution)/shard_map/ppermute | solution.py:47
  179.6 16.6 %collective-permute-start.13 = (bf16[64,6144]{1,0:T(8,128)(2,1)S(1)}, bf16[64,6144]{1,0:T(8,128)(2,1)S(1)}, u32[]{:S(2)}, u32[]{:S(2)}) collective-permute-start(bf16[64,6144]{1,0:T(8,128)(2,1)S(1)} %collective-permute-done.9), channel_id=1, source_target_pairs={{0,16},{16,0},{32,48},{48,32},{64,80},{80,64},{96,112},{112,96},{1... | collective-permute-start | bytes 2359304 | tf_op jit(solution)/shard_map/ppermute | solution.py:47
  196.2 2.4 collective-permute-start.14
  199.0 8.1 %copy-start.13 = (bf16[512,6144]{1,0:T(8,128)(2,1)S(1)}, bf16[512,6144]{1,0:T(8,128)(2,1)}, u32[]{:S(2)}) copy-start(bf16[512,6144]{1,0:T(8,128)(2,1)} %all-gather.2.cloned.1.call-done) | copy-start | bytes 18874372
  220.9 86.9 %reduce-scatter.5.cloned.1.call-start = ((), (), s32[]{:S(2)}) async-start(), calls=%async_computation.9 | async-start | bytes 7077888 | tf_op jit(solution)/shard_map/reduce_scatter | solution.py:179
  221.8 11.4 %collective-permute-start.15 = (f32[16,6144]{1,0:T(8,128)S(1)}, f32[16,6144]{1,0:T(8,128)}, u32[]{:S(2)}, u32[]{:S(2)}) collective-permute-start(f32[16,6144]{1,0:T(8,128)S(1)} %copy-done.2), channel_id=1, source_target_pairs={{0,1},{1,0},{2,3},{3,2},{4,5},{5,4},{6,7},{7,6},{8,9},{9,8},{10,11... | collective-permute-start | bytes 1179656 | tf_op jit(solution)/shard_map/ppermute | solution.py:165
  224.9 14.1 %slice-start = ((s8[6291456]{0:T(1024)(128)(4,1)}), s8[4194304]{0:T(1024)(128)(4,1)S(1)}, s32[]{:S(2)}) async-start(s8[6291456]{0:T(1024)(128)(4,1)} %bitcast.131), calls=%async_computation.10 | async-start | bytes 8388608
  226.2 12.8 %slice-start.1 = ((s8[6291456]{0:T(1024)(128)(4,1)}), s8[2097152]{0:T(1024)(128)(4,1)S(1)}, s32[]{:S(2)}) async-start(s8[6291456]{0:T(1024)(128)(4,1)} %bitcast.131), calls=%async_computation.11 | async-start | bytes 4194304
  233.2 9.3 %slice-start.2 = ((s8[6291456]{0:T(1024)(128)(4,1)}), s8[4194304]{0:T(1024)(128)(4,1)S(1)}, s32[]{:S(2)}) async-start(s8[6291456]{0:T(1024)(128)(4,1)} %bitcast.133), calls=%async_computation.12 | async-start | bytes 8388608
  263.1 44.7 %all-to-all-start.3 = ((bf16[8,8,6144]{2,1,0:T(8,128)(2,1)}), bf16[8,8,6144]{2,1,0:T(8,128)(2,1)S(1)}, u32[]{:S(2)}, u32[]{:S(2)}) async-start(bf16[8,8,6144]{2,1,0:T(8,128)(2,1)} %bitcast.123), calls=%async_computation.4 | async-start | bytes 1572864 | tf_op jit(solution)/shard_map/all_to_all | solution.py:181
  307.8 20.7 %all-to-all-start.4 = ((bf16[8,8,6144]{2,1,0:T(8,128)(2,1)}), bf16[8,8,6144]{2,1,0:T(8,128)(2,1)}, u32[]{:S(2)}, u32[]{:S(2)}) async-start(bf16[8,8,6144]{2,1,0:T(8,128)(2,1)} %bitcast.124), calls=%async_computation.6 | async-start | bytes 1572864 | tf_op jit(solution)/shard_map/all_to_all | solution.py:181
  331.9 10.8 %collective-permute-start.16 = (bf16[32,6144]{1,0:T(8,128)(2,1)S(1)}, bf16[32,6144]{1,0:T(8,128)(2,1)S(1)}, u32[]{:S(2)}, u32[]{:S(2)}) collective-permute-start(bf16[32,6144]{1,0:T(8,128)(2,1)S(1)} %fusion.25), channel_id=1, source_target_pairs={{0,1},{1,0},{2,3},{3,2},{4,5},{5,4},{6,7},{7,6},{8,9},{9,8},{10,11... | collective-permute-start | bytes 1179656 | tf_op jit(solution)/shard_map/ppermute | solution.py:197
  (10 other events, 20.5 us)
Sparse Core Ops, SparseCore 0:
  128.1 70.8 all-gather.1
  221.0 42.0 reduce-scatter.2
  265.5 42.2 reduce-scatter.4

commit v11 on v9

--- a/solution.py
+++ b/solution.py
@@ -24,8 +24,10 @@
     top = jnp.max(scores, axis=-1, keepdims=True)
     weights = jnp.exp(scores - top)
     total = jnp.sum(weights, axis=-1, keepdims=True)
-    values = jnp.einsum(
-        "hqk,khd->hqd", weights, k.astype(jnp.float32), precision=lax.Precision.HIGHEST
+    high = weights.astype(jnp.bfloat16)
+    low = (weights - high.astype(jnp.float32)).astype(jnp.bfloat16)
+    values = jnp.einsum("hqk,khd->hqd", high, k, preferred_element_type=jnp.float32) + jnp.einsum(
+        "hqk,khd->hqd", low, k, preferred_element_type=jnp.float32
     )
     return (values / total).transpose(1, 0, 2).reshape(rows, local_width).astype(jnp.bfloat16)
 

time: 340 us -> 338 us (level)
  no operation moved by 1% of the time
where the time goes in v11:
time: 338 us
  waiting for transfers between devices  192 us (57%)
  matrix products  43 us (13%)
  starting transfers between devices  32.4 us (10%)
  blocking collectives  32.4 us (10%)
  between operations  18.6 us (6%)
  other arithmetic  9.42 us (3%)
  local copies, waits for them, and re-layouts  9.29 us (3%)
    reduce_scatter x2, waiting for transfers between devices, per_device(): part_rows = lax.psum_scatter(down, 'leaf', scatter_dimension=0, tiled=True)  62.6 us
    all_to_all x1, waiting for transfers between devices, per_device(): lax.all_to_all(term.reshape(group, share_rows, width), ('expert', 'tensor...  45.8 us
    all_gather x2, waiting for transfers between devices, per_device(): piece = lax.all_gather(arrived, 'leaf', axis=0, tiled=True)  42.5 us
    all_to_all x2, blocking collectives, per_device(): lax.all_to_all(outgoing[:, c * chunk_slots:(c + 1) * chunk_slots], 'exper...  32.4 us
    dot_general x2, matrix products, per_device(): up_v = jnp.dot(piece, w_up[0], preferred_element_type=jnp.float32)  14 us
    dot_general x2, matrix products, per_device(): gate_v = jnp.dot(piece, w_gate[0], preferred_element_type=jnp.float32)  14 us
    all_to_all x2, waiting for transfers between devices, per_device(): lax.all_to_all(part_rows.reshape(experts, chunk_slots, width), 'expert',...  13.7 us
    all_to_all x2, starting transfers between devices, per_device(): lax.all_to_all(part_rows.reshape(experts, chunk_slots, width), 'expert',...  13.4 us
  transfers between devices with their start and end apart: 17, of which 11 were waited for; matrix products, arithmetic and copies ran while one was open for 13% of the time, Pallas kernels for 0%

profile of v11, /device:TPU:32, one launch (start us, length us, event | category | flops | bytes accessed | tf_op | source)
XLA Modules:
  0.0 337.6 jit_solution(6291394186603698562)
XLA Ops:
  6.5 1.2 copy.74
  8.7 2.0 collective-permute-start
  10.7 1.2 collective-permute-start.1
  11.8 2.5 collective-permute-start.2
  21.9 9.8 %collective-permute-done = bf16[520,384]{0,1:T(8,128)(2,1)S(1)} collective-permute-done((bf16[520,384]{0,1:T(8,128)(2,1)S(1)}, bf16[520,384]{0,1:T(8,128)(2,1)S(1)}, u32[]{:S(2)}, u32[]{:S(2)}) %collective-permute-start) | collective-permute-done | bytes 399392 | tf_op jit(solution)/shard_map/ppermute | solution.py:75
  32.3 2.7 collective-permute-done.2
  35.4 1.5 collective-permute-done.6
  40.9 1.8 fusion.50
  42.9 2.1 convert_element_type.89
  45.0 7.2 %all-to-all-start = ((bf16[16,16,6144]{2,1,0:T(8,128)(2,1)}), bf16[16,16,6144]{2,1,0:T(8,128)(2,1)S(1)}, u32[]{:S(2)}, u32[]{:S(2)}) async-start(bf16[16,16,6144]{2,1,0:T(8,128)(2,1)} %bitcast.114), calls=%async_computation | async-start | bytes 6291456 | tf_op jit(solution)/shard_map/all_to_all | solution.py:109
  52.9 45.8 %all-to-all-done = bf16[16,16,6144]{2,1,0:T(8,128)(2,1)S(1)} async-done(((bf16[16,16,6144]{2,1,0:T(8,128)(2,1)}), bf16[16,16,6144]{2,1,0:T(8,128)(2,1)S(1)}, u32[]{:S(2)}, u32[]{:S(2)}) %all-to-all-start) | async-done | bytes 3145760 | tf_op jit(solution)/shard_map/all_to_all | solution.py:109
  100.0 2.8 collective-permute-start.7
  102.9 4.0 %collective-permute-done.7 = bf16[16,6144]{1,0:T(8,128)(2,1)S(1)} collective-permute-done((bf16[16,6144]{1,0:T(8,128)(2,1)S(1)}, bf16[16,6144]{1,0:T(8,128)(2,1)S(1)}, u32[]{:S(2)}, u32[]{:S(2)}) %collective-permute-start.7) | collective-permute-done | bytes 196640 | tf_op jit(solution)/shard_map/ppermute | solution.py:36
  106.9 1.2 broadcast_select_fusion.3
  108.8 17.8 %all_to_all.25 = bf16[8,8,6144]{2,1,0:T(8,128)(2,1)} all-to-all(bf16[8,8,6144]{2,1,0:T(8,128)(2,1)S(1)} %get-tuple-element.19), channel_id=1, replica_groups=mesh['leaf'=8,'expert'=8,'tensor'=2] {'expert'}, dimensions={0} | all-to-all | bytes 1572864 | tf_op jit(solution)/shard_map/all_to_all | solution.py:137
  126.6 14.6 %all_to_all.26 = bf16[8,8,6144]{2,1,0:T(8,128)(2,1)} all-to-all(bf16[8,8,6144]{2,1,0:T(8,128)(2,1)S(1)} %get-tuple-element.20), channel_id=1, replica_groups=mesh['leaf'=8,'expert'=8,'tensor'=2] {'expert'}, dimensions={0} | all-to-all | bytes 1572864 | tf_op jit(solution)/shard_map/all_to_all | solution.py:137
  141.5 22.4 %all-gather.3.cloned.1.call-done = bf16[512,6144]{1,0:T(8,128)(2,1)} async-done(((bf16[64,6144]{1,0:T(8,128)(2,1)}), bf16[512,6144]{1,0:T(8,128)(2,1)}) %all-gather.3.cloned.1.call-update) | async-done | bytes 6291472 | tf_op jit(solution)/shard_map/all_gather | solution.py:144
  163.9 8.2 %fusion.8 = f32[512,512]{1,0:T(8,128)S(1)} fusion(bf16[512,6144]{1,0:T(8,128)(2,1)} %all-gather.3.cloned.1.call-done, bf16[1,6144,512]{2,1,0:T(8,128)(2,1)} %param.21), kind=kOutput, calls=%fused_computation.12 | convolution fusion | flops 3221225472 | bytes 13631488 | tf_op jit(solution)/shard_map/dot_general | solution.py:150
  172.2 6.4 %fusion.14 = bf16[512,512]{1,0:T(8,128)(2,1)S(1)} fusion(bf16[512,6144]{1,0:T(8,128)(2,1)S(1)} %copy-done.7, bf16[1,6144,512]{2,1,0:T(8,128)(2,1)} %param.22, f32[512,512]{1,0:T(8,128)S(1)} %fusion.8), kind=kOutput, calls=%fused_computation.22 | convolution fusion | flops 3222798336 | bytes 14155776 | tf_op jit(solution)/shard_map/dot_general | solution.py:151
  178.6 5.4 %convolution_convert_fusion.1 = bf16[512,6144]{1,0:T(8,128)(2,1)} fusion(bf16[512,512]{1,0:T(8,128)(2,1)S(1)} %fusion.14, bf16[1,512,6144]{2,1,0:T(8,128)(2,1)S(1)} %bitcast.130), kind=kOutput, calls=%fused_computation.2 | convolution fusion | flops 3224371200 | bytes 13107200 | tf_op jit(solution)/shard_map/dot_general | solution.py:153
  185.0 1.5 collective-permute-start.8
  186.5 20.2 %all-gather.5.cloned.1.call-done = bf16[512,6144]{1,0:T(8,128)(2,1)} async-done(((bf16[64,6144]{1,0:T(8,128)(2,1)}), bf16[512,6144]{1,0:T(8,128)(2,1)}) %all-gather.5.cloned.1.call-update) | async-done | bytes 6291472 | tf_op jit(solution)/shard_map/all_gather | solution.py:144
  206.7 7.6 %fusion.2 = f32[512,512]{1,0:T(8,128)S(1)} fusion(bf16[512,6144]{1,0:T(8,128)(2,1)} %all-gather.5.cloned.1.call-done, bf16[1,6144,512]{2,1,0:T(8,128)(2,1)} %param.22), kind=kOutput, calls=%fused_computation.6 | convolution fusion | flops 3221225472 | bytes 13631488 | tf_op jit(solution)/shard_map/dot_general | solution.py:151
  214.3 5.7 %fusion.6 = f32[512,512]{1,0:T(8,128)S(1)} fusion(bf16[512,6144]{1,0:T(8,128)(2,1)S(1)} %copy-done.6, bf16[1,6144,512]{2,1,0:T(8,128)(2,1)} %param.21), kind=kOutput, calls=%fused_computation.10 | convolution fusion | flops 3221225472 | bytes 13631488 | tf_op jit(solution)/shard_map/dot_general | solution.py:150
  220.1 5.4 %convolution_convert_fusion = bf16[512,6144]{1,0:T(8,128)(2,1)} fusion(bf16[1,512,6144]{2,1,0:T(8,128)(2,1)S(1)} %bitcast.132, f32[512,512]{1,0:T(8,128)S(1)} %fusion.2, f32[512,512]{1,0:T(8,128)S(1)} %fusion.6), kind=kOutput, calls=%fused_computation.1 | convolution fusion | flops 3225944064 | bytes 14680064 | tf_op jit(solution)/shard_map/dot_general | solution.py:153
  225.5 25.0 %reduce-scatter.3.cloned.1.call-done = bf16[64,6144]{1,0:T(8,128)(2,1)} async-done(((bf16[512,6144]{1,0:T(8,128)(2,1)}), bf16[64,6144]{1,0:T(8,128)(2,1)}) %reduce-scatter.3.cloned.1.call-update) | async-done | bytes 786448 | tf_op jit(solution)/shard_map/reduce_scatter | solution.py:154
  250.5 6.7 %all-to-all-start.3 = ((bf16[8,8,6144]{2,1,0:T(8,128)(2,1)}), bf16[8,8,6144]{2,1,0:T(8,128)(2,1)S(1)}, u32[]{:S(2)}, u32[]{:S(2)}) async-start(bf16[8,8,6144]{2,1,0:T(8,128)(2,1)} %bitcast.121), calls=%async_computation.4 | async-start | bytes 1572864 | tf_op jit(solution)/shard_map/all_to_all | solution.py:156
  257.4 37.6 %reduce-scatter.5.cloned.1.call-done = bf16[64,6144]{1,0:T(8,128)(2,1)} async-done(((bf16[512,6144]{1,0:T(8,128)(2,1)}), bf16[64,6144]{1,0:T(8,128)(2,1)}) %reduce-scatter.5.cloned.1.call-update) | async-done | bytes 786448 | tf_op jit(solution)/shard_map/reduce_scatter | solution.py:154
  295.0 6.7 %all-to-all-start.4 = ((bf16[8,8,6144]{2,1,0:T(8,128)(2,1)}), bf16[8,8,6144]{2,1,0:T(8,128)(2,1)}, u32[]{:S(2)}, u32[]{:S(2)}) async-start(bf16[8,8,6144]{2,1,0:T(8,128)(2,1)} %bitcast.122), calls=%async_computation.6 | async-start | bytes 1572864 | tf_op jit(solution)/shard_map/all_to_all | solution.py:156
  302.1 13.6 %all-to-all-done.4 = bf16[8,8,6144]{2,1,0:T(8,128)(2,1)} async-done(((bf16[8,8,6144]{2,1,0:T(8,128)(2,1)}), bf16[8,8,6144]{2,1,0:T(8,128)(2,1)}, u32[]{:S(2)}, u32[]{:S(2)}) %all-to-all-start.4) | async-done | bytes 786464 | tf_op jit(solution)/shard_map/all_to_all | solution.py:156
  315.7 1.2 pad_maximum_fusion
  320.3 9.7 %collective-permute-done.9 = bf16[32,6144]{1,0:T(8,128)(2,1)S(1)} collective-permute-done((bf16[32,6144]{1,0:T(8,128)(2,1)S(1)}, bf16[32,6144]{1,0:T(8,128)(2,1)S(1)}, u32[]{:S(2)}, u32[]{:S(2)}) %collective-permute-start.9) | collective-permute-done | bytes 393248 | tf_op jit(solution)/shard_map/ppermute | solution.py:172
  (114 shorter events, 17.5 us)
Async XLA Ops:
  6.5 295.2 %copy-start = (bf16[6144,8]{0,1:T(8,128)(2,1)S(1)}, bf16[6144,8]{0,1:T(8,128)(2,1)}, u32[]{:S(2)}) copy-start(bf16[6144,8]{0,1:T(8,128)(2,1)} %param.19) | copy-start | bytes 294916
  8.7 23.0 %collective-permute-start = (bf16[520,384]{0,1:T(8,128)(2,1)S(1)}, bf16[520,384]{0,1:T(8,128)(2,1)S(1)}, u32[]{:S(2)}, u32[]{:S(2)}) collective-permute-start(bf16[520,384]{0,1:T(8,128)(2,1)S(1)} %pad_maximum_fusion.1), channel_id=1, source_target_pairs={{0,32},{16,48},{32,64},{48,80},{64,96},{80,112},{96,0},{112,16},{1... | collective-permute-start | bytes 1198088 | tf_op jit(solution)/shard_map/ppermute | solution.py:75
  10.7 21.1 %collective-permute-start.1 = (bf16[520,384]{0,1:T(8,128)(2,1)S(1)}, bf16[520,384]{0,1:T(8,128)(2,1)S(1)}, u32[]{:S(2)}, u32[]{:S(2)}) collective-permute-start(bf16[520,384]{0,1:T(8,128)(2,1)S(1)} %pad_maximum_fusion.1), channel_id=1, source_target_pairs={{0,64},{16,80},{32,96},{48,112},{64,0},{80,16},{96,32},{112,48},{1... | collective-permute-start | bytes 1198088 | tf_op jit(solution)/shard_map/ppermute | solution.py:75
  11.8 23.2 %collective-permute-start.2 = (bf16[520,384]{0,1:T(8,128)(2,1)S(1)}, bf16[520,384]{0,1:T(8,128)(2,1)S(1)}, u32[]{:S(2)}, u32[]{:S(2)}) collective-permute-start(bf16[520,384]{0,1:T(8,128)(2,1)S(1)} %pad_maximum_fusion.1), channel_id=1, source_target_pairs={{0,96},{16,112},{32,0},{48,16},{64,32},{80,48},{96,64},{112,80},{1... | collective-permute-start | bytes 1198088 | tf_op jit(solution)/shard_map/ppermute | solution.py:75
  14.3 20.8 %collective-permute-start.3 = (bf16[520,384]{0,1:T(8,128)(2,1)S(1)}, bf16[520,384]{0,1:T(8,128)(2,1)S(1)}, u32[]{:S(2)}, u32[]{:S(2)}) collective-permute-start(bf16[520,384]{0,1:T(8,128)(2,1)S(1)} %pad_maximum_fusion.1), channel_id=1, source_target_pairs={{0,16},{16,0},{32,48},{48,32},{64,80},{80,64},{96,112},{112,96},{1... | collective-permute-start | bytes 1198088 | tf_op jit(solution)/shard_map/ppermute | solution.py:77
  31.7 3.6 %collective-permute-start.4 = (bf16[520,384]{0,1:T(8,128)(2,1)S(1)}, bf16[520,384]{0,1:T(8,128)(2,1)S(1)}, u32[]{:S(2)}, u32[]{:S(2)}) collective-permute-start(bf16[520,384]{0,1:T(8,128)(2,1)S(1)} %collective-permute-done), channel_id=1, source_target_pairs={{0,16},{16,0},{32,48},{48,32},{64,80},{80,64},{96,112},{112,96},{1... | collective-permute-start | bytes 1198088 | tf_op jit(solution)/shard_map/ppermute | solution.py:77
  31.7 3.6 %collective-permute-start.5 = (bf16[520,384]{0,1:T(8,128)(2,1)S(1)}, bf16[520,384]{0,1:T(8,128)(2,1)S(1)}, u32[]{:S(2)}, u32[]{:S(2)}) collective-permute-start(bf16[520,384]{0,1:T(8,128)(2,1)S(1)} %collective-permute-done.1), channel_id=1, source_target_pairs={{0,16},{16,0},{32,48},{48,32},{64,80},{80,64},{96,112},{112,96},{1... | collective-permute-start | bytes 1198088 | tf_op jit(solution)/shard_map/ppermute | solution.py:77
  35.0 1.9 collective-permute-start.6
  35.2 2.9 copy-start.8
  37.1 2.8 slice-start
  38.8 2.2 slice-start.1
  40.9 1.9 copy-start.3
  44.9 7.2 %copy-start.5 = (s32[32,2]{0,1:T(2,128)S(1)}, s32[32,2]{0,1:T(2,128)}, u32[]{:S(2)}) copy-start(s32[32,2]{0,1:T(2,128)} %param.20) | copy-start | bytes 772
  44.9 54.9 %copy-start.4 = (f32[6144]{0:T(1024)S(1)}, f32[6144]{0:T(1024)}, u32[]{:S(2)}) copy-start(f32[6144]{0:T(1024)} %param.18) | copy-start | bytes 73732
  45.0 53.7 %all-to-all-start = ((bf16[16,16,6144]{2,1,0:T(8,128)(2,1)}), bf16[16,16,6144]{2,1,0:T(8,128)(2,1)S(1)}, u32[]{:S(2)}, u32[]{:S(2)}) async-start(bf16[16,16,6144]{2,1,0:T(8,128)(2,1)} %bitcast.114), calls=%async_computation | async-start | bytes 6291456 | tf_op jit(solution)/shard_map/all_to_all | solution.py:109
  52.1 111.8 %all-gather.3.cloned.1.call-start = ((), (), s32[]{:S(2)}) async-start(), calls=%async_computation.7 | async-start | bytes 7077888 | tf_op jit(solution)/shard_map/all_gather | solution.py:144
  99.1 0.7 copy-start.1
  100.0 6.9 %collective-permute-start.7 = (bf16[16,6144]{1,0:T(8,128)(2,1)S(1)}, bf16[16,6144]{1,0:T(8,128)(2,1)S(1)}, u32[]{:S(2)}, u32[]{:S(2)}) collective-permute-start(bf16[16,6144]{1,0:T(8,128)(2,1)S(1)} %multiply_convert_fusion.2), channel_id=1, source_target_pairs={{0,1},{1,0},{2,3},{3,2},{4,5},{5,4},{6,7},{7,6},{8,9},{9,8},{10,11... | collective-permute-start | bytes 589832 | tf_op jit(solution)/shard_map/ppermute | solution.py:36
  126.6 80.1 %all-gather.5.cloned.1.call-start = ((), (), s32[]{:S(2)}) async-start(), calls=%async_computation.8 | async-start | bytes 7077888 | tf_op jit(solution)/shard_map/all_gather | solution.py:144
  141.3 109.2 %reduce-scatter.3.cloned.1.call-start = ((), (), s32[]{:S(2)}) async-start(), calls=%async_computation.9 | async-start | bytes 7077888 | tf_op jit(solution)/shard_map/reduce_scatter | solution.py:154
  163.9 8.3 %copy-start.7 = (bf16[512,6144]{1,0:T(8,128)(2,1)S(1)}, bf16[512,6144]{1,0:T(8,128)(2,1)}, u32[]{:S(2)}) copy-start(bf16[512,6144]{1,0:T(8,128)(2,1)} %all-gather.3.cloned.1.call-done) | copy-start | bytes 18874372
  163.9 14.7 %slice-start.2 = ((s8[6291456]{0:T(1024)(128)(4,1)}), s8[4194304]{0:T(1024)(128)(4,1)S(1)}, s32[]{:S(2)}) async-start(s8[6291456]{0:T(1024)(128)(4,1)} %bitcast.129), calls=%async_computation.13 | async-start | bytes 8388608
  172.1 6.4 %slice-start.3 = ((s8[6291456]{0:T(1024)(128)(4,1)}), s8[2097152]{0:T(1024)(128)(4,1)S(1)}, s32[]{:S(2)}) async-start(s8[6291456]{0:T(1024)(128)(4,1)} %bitcast.129), calls=%async_computation.14 | async-start | bytes 4194304
  184.0 1.0 copy-start.2
  184.1 111.0 %reduce-scatter.5.cloned.1.call-start = ((), (), s32[]{:S(2)}) async-start(), calls=%async_computation.10 | async-start | bytes 7077888 | tf_op jit(solution)/shard_map/reduce_scatter | solution.py:154
  185.0 21.6 %collective-permute-start.8 = (f32[16,6144]{1,0:T(8,128)S(1)}, f32[16,6144]{1,0:T(8,128)S(1)}, u32[]{:S(2)}, u32[]{:S(2)}) collective-permute-start(f32[16,6144]{1,0:T(8,128)S(1)} %copy-done.2), channel_id=1, source_target_pairs={{0,1},{1,0},{2,3},{3,2},{4,5},{5,4},{6,7},{7,6},{8,9},{9,8},{10,11... | collective-permute-start | bytes 1179656 | tf_op jit(solution)/shard_map/ppermute | solution.py:147
  206.7 7.6 %copy-start.6 = (bf16[512,6144]{1,0:T(8,128)(2,1)S(1)}, bf16[512,6144]{1,0:T(8,128)(2,1)}, u32[]{:S(2)}) copy-start(bf16[512,6144]{1,0:T(8,128)(2,1)} %all-gather.5.cloned.1.call-done) | copy-start | bytes 18874372
  206.7 13.4 %slice-start.4 = ((s8[6291456]{0:T(1024)(128)(4,1)}), s8[4194304]{0:T(1024)(128)(4,1)S(1)}, s32[]{:S(2)}) async-start(s8[6291456]{0:T(1024)(128)(4,1)} %bitcast.131), calls=%async_computation.15 | async-start | bytes 8388608
  214.3 5.8 %slice-start.5 = ((s8[6291456]{0:T(1024)(128)(4,1)}), s8[2097152]{0:T(1024)(128)(4,1)S(1)}, s32[]{:S(2)}) async-start(s8[6291456]{0:T(1024)(128)(4,1)} %bitcast.131), calls=%async_computation.16 | async-start | bytes 4194304
  250.5 44.6 %all-to-all-start.3 = ((bf16[8,8,6144]{2,1,0:T(8,128)(2,1)}), bf16[8,8,6144]{2,1,0:T(8,128)(2,1)S(1)}, u32[]{:S(2)}, u32[]{:S(2)}) async-start(bf16[8,8,6144]{2,1,0:T(8,128)(2,1)} %bitcast.121), calls=%async_computation.4 | async-start | bytes 1572864 | tf_op jit(solution)/shard_map/all_to_all | solution.py:156
  295.0 20.7 %all-to-all-start.4 = ((bf16[8,8,6144]{2,1,0:T(8,128)(2,1)}), bf16[8,8,6144]{2,1,0:T(8,128)(2,1)}, u32[]{:S(2)}, u32[]{:S(2)}) async-start(bf16[8,8,6144]{2,1,0:T(8,128)(2,1)} %bitcast.122), calls=%async_computation.6 | async-start | bytes 1572864 | tf_op jit(solution)/shard_map/all_to_all | solution.py:156
  319.2 10.8 %collective-permute-start.9 = (bf16[32,6144]{1,0:T(8,128)(2,1)S(1)}, bf16[32,6144]{1,0:T(8,128)(2,1)S(1)}, u32[]{:S(2)}, u32[]{:S(2)}) collective-permute-start(bf16[32,6144]{1,0:T(8,128)(2,1)S(1)} %fusion.26), channel_id=1, source_target_pairs={{0,1},{1,0},{2,3},{3,2},{4,5},{5,4},{6,7},{7,6},{8,9},{9,8},{10,11... | collective-permute-start | bytes 1179656 | tf_op jit(solution)/shard_map/ppermute | solution.py:172
Sparse Core Ops, SparseCore 0:
  126.7 37.1 all-gather.2
  165.6 41.0 all-gather.4
  209.1 41.3 reduce-scatter.2
  252.7 42.2 reduce-scatter.4

commit v12 on v11

--- a/solution.py
+++ b/solution.py
@@ -16,11 +16,8 @@
     q = queries.reshape(rows, heads_here, head_size)
     k = keys.reshape(key_count, heads_here, head_size)
     scores = jnp.einsum("qhd,khd->hqk", q, k, preferred_element_type=jnp.float32) * scale
-    span_hot = (key_spans[:, None] == jnp.arange(span_count, dtype=jnp.int32)[None, :]).astype(
-        jnp.float32
-    )
-    bias = jnp.dot(span_hot, span_bias.T, precision=lax.Precision.HIGHEST)
-    scores = scores + bias.T[:, None, :]
+    bias = jnp.take(span_bias, key_spans, axis=1)
+    scores = scores + bias[:, None, :]
     top = jnp.max(scores, axis=-1, keepdims=True)
     weights = jnp.exp(scores - top)
     total = jnp.sum(weights, axis=-1, keepdims=True)

time: 338 us -> 339 us (level)
    unnamed x40 -> x39, local copies, waits for them, and re-layouts: 5.32 us -> 7.11 us
where the time goes in v12:
time: 339 us
  waiting for transfers between devices  191 us (56%)
  matrix products  42.7 us (13%)
  blocking collectives  32.5 us (10%)
  starting transfers between devices  32.4 us (10%)
  between operations  18.6 us (5%)
  local copies, waits for them, and re-layouts  12.1 us (4%)
  other arithmetic  9.67 us (3%)
    reduce_scatter x2, waiting for transfers between devices, per_device(): part_rows = lax.psum_scatter(down, 'leaf', scatter_dimension=0, tiled=True)  62.6 us
    all_to_all x1, waiting for transfers between devices, per_device(): lax.all_to_all(term.reshape(group, share_rows, width), ('expert', 'tensor...  45.7 us
    all_gather x2, waiting for transfers between devices, per_device(): piece = lax.all_gather(arrived, 'leaf', axis=0, tiled=True)  42.6 us
    all_to_all x2, blocking collectives, per_device(): lax.all_to_all(outgoing[:, c * chunk_slots:(c + 1) * chunk_slots], 'exper...  32.5 us
    dot_general x2, matrix products, per_device(): up_v = jnp.dot(piece, w_up[0], preferred_element_type=jnp.float32)  14 us
    dot_general x2, matrix products, per_device(): gate_v = jnp.dot(piece, w_gate[0], preferred_element_type=jnp.float32)  14 us
    all_to_all x2, waiting for transfers between devices, per_device(): lax.all_to_all(part_rows.reshape(experts, chunk_slots, width), 'expert',...  13.6 us
    all_to_all x2, starting transfers between devices, per_device(): lax.all_to_all(part_rows.reshape(experts, chunk_slots, width), 'expert',...  13.4 us
  transfers between devices with their start and end apart: 17, of which 11 were waited for; matrix products, arithmetic and copies ran while one was open for 13% of the time, Pallas kernels for 0%

profile of v12, /device:TPU:32, one launch (start us, length us, event | category | flops | bytes accessed | tf_op | source)
XLA Modules:
  0.0 338.6 jit_solution(3642441205755202172)
XLA Ops:
  6.5 1.2 copy.82
  8.7 2.0 collective-permute-start
  10.7 1.2 collective-permute-start.1
  11.8 2.5 collective-permute-start.2
  22.6 9.1 %collective-permute-done = bf16[520,384]{0,1:T(8,128)(2,1)S(1)} collective-permute-done((bf16[520,384]{0,1:T(8,128)(2,1)S(1)}, bf16[520,384]{0,1:T(8,128)(2,1)S(1)}, u32[]{:S(2)}, u32[]{:S(2)}) %collective-permute-start) | collective-permute-done | bytes 399392 | tf_op jit(solution)/shard_map/ppermute | solution.py:72
  32.3 2.7 collective-permute-done.2
  41.9 1.8 fusion.49
  43.9 2.1 convert_element_type.118
  45.9 7.2 %all-to-all-start = ((bf16[16,16,6144]{2,1,0:T(8,128)(2,1)}), bf16[16,16,6144]{2,1,0:T(8,128)(2,1)S(1)}, u32[]{:S(2)}, u32[]{:S(2)}) async-start(bf16[16,16,6144]{2,1,0:T(8,128)(2,1)} %bitcast.118), calls=%async_computation | async-start | bytes 6291456 | tf_op jit(solution)/shard_map/all_to_all | solution.py:106
  53.9 45.7 %all-to-all-done = bf16[16,16,6144]{2,1,0:T(8,128)(2,1)S(1)} async-done(((bf16[16,16,6144]{2,1,0:T(8,128)(2,1)}), bf16[16,16,6144]{2,1,0:T(8,128)(2,1)S(1)}, u32[]{:S(2)}, u32[]{:S(2)}) %all-to-all-start) | async-done | bytes 3145760 | tf_op jit(solution)/shard_map/all_to_all | solution.py:106
  101.0 2.8 collective-permute-start.7
  103.8 4.0 %collective-permute-done.7 = bf16[16,6144]{1,0:T(8,128)(2,1)S(1)} collective-permute-done((bf16[16,6144]{1,0:T(8,128)(2,1)S(1)}, bf16[16,6144]{1,0:T(8,128)(2,1)S(1)}, u32[]{:S(2)}, u32[]{:S(2)}) %collective-permute-start.7) | collective-permute-done | bytes 196640 | tf_op jit(solution)/shard_map/ppermute | solution.py:33
  107.8 1.2 broadcast_select_fusion.3
  109.7 17.8 %all_to_all.25 = bf16[8,8,6144]{2,1,0:T(8,128)(2,1)} all-to-all(bf16[8,8,6144]{2,1,0:T(8,128)(2,1)S(1)} %get-tuple-element.17), channel_id=1, replica_groups=mesh['leaf'=8,'expert'=8,'tensor'=2] {'expert'}, dimensions={0} | all-to-all | bytes 1572864 | tf_op jit(solution)/shard_map/all_to_all | solution.py:134
  127.6 14.6 %all_to_all.26 = bf16[8,8,6144]{2,1,0:T(8,128)(2,1)} all-to-all(bf16[8,8,6144]{2,1,0:T(8,128)(2,1)S(1)} %get-tuple-element.18), channel_id=1, replica_groups=mesh['leaf'=8,'expert'=8,'tensor'=2] {'expert'}, dimensions={0} | all-to-all | bytes 1572864 | tf_op jit(solution)/shard_map/all_to_all | solution.py:134
  142.5 22.4 %all-gather.3.cloned.1.call-done = bf16[512,6144]{1,0:T(8,128)(2,1)} async-done(((bf16[64,6144]{1,0:T(8,128)(2,1)}), bf16[512,6144]{1,0:T(8,128)(2,1)}) %all-gather.3.cloned.1.call-update) | async-done | bytes 6291472 | tf_op jit(solution)/shard_map/all_gather | solution.py:141
  164.9 8.2 %fusion.8 = f32[512,512]{1,0:T(8,128)S(1)} fusion(bf16[512,6144]{1,0:T(8,128)(2,1)} %all-gather.3.cloned.1.call-done, bf16[1,6144,512]{2,1,0:T(8,128)(2,1)} %param.21), kind=kOutput, calls=%fused_computation.13 | convolution fusion | flops 3221225472 | bytes 13631488 | tf_op jit(solution)/shard_map/dot_general | solution.py:147
  173.2 6.4 %fusion.14 = bf16[512,512]{1,0:T(8,128)(2,1)S(1)} fusion(bf16[512,6144]{1,0:T(8,128)(2,1)S(1)} %copy-done.7, bf16[1,6144,512]{2,1,0:T(8,128)(2,1)} %param.22, f32[512,512]{1,0:T(8,128)S(1)} %fusion.8), kind=kOutput, calls=%fused_computation.23 | convolution fusion | flops 3222798336 | bytes 14155776 | tf_op jit(solution)/shard_map/dot_general | solution.py:148
  179.6 5.4 %convolution_convert_fusion.1 = bf16[512,6144]{1,0:T(8,128)(2,1)} fusion(bf16[512,512]{1,0:T(8,128)(2,1)S(1)} %fusion.14, bf16[1,512,6144]{2,1,0:T(8,128)(2,1)S(1)} %bitcast.139), kind=kOutput, calls=%fused_computation.3 | convolution fusion | flops 3224371200 | bytes 13107200 | tf_op jit(solution)/shard_map/dot_general | solution.py:150
  186.0 1.5 collective-permute-start.8
  187.5 20.2 %all-gather.5.cloned.1.call-done = bf16[512,6144]{1,0:T(8,128)(2,1)} async-done(((bf16[64,6144]{1,0:T(8,128)(2,1)}), bf16[512,6144]{1,0:T(8,128)(2,1)}) %all-gather.5.cloned.1.call-update) | async-done | bytes 6291472 | tf_op jit(solution)/shard_map/all_gather | solution.py:141
  207.7 7.6 %fusion.2 = f32[512,512]{1,0:T(8,128)S(1)} fusion(bf16[512,6144]{1,0:T(8,128)(2,1)} %all-gather.5.cloned.1.call-done, bf16[1,6144,512]{2,1,0:T(8,128)(2,1)} %param.22), kind=kOutput, calls=%fused_computation.7 | convolution fusion | flops 3221225472 | bytes 13631488 | tf_op jit(solution)/shard_map/dot_general | solution.py:148
  215.3 5.7 %fusion.6 = f32[512,512]{1,0:T(8,128)S(1)} fusion(bf16[512,6144]{1,0:T(8,128)(2,1)S(1)} %copy-done.6, bf16[1,6144,512]{2,1,0:T(8,128)(2,1)} %param.21), kind=kOutput, calls=%fused_computation.11 | convolution fusion | flops 3221225472 | bytes 13631488 | tf_op jit(solution)/shard_map/dot_general | solution.py:147
  221.1 5.4 %convolution_convert_fusion = bf16[512,6144]{1,0:T(8,128)(2,1)} fusion(bf16[1,512,6144]{2,1,0:T(8,128)(2,1)S(1)} %bitcast.141, f32[512,512]{1,0:T(8,128)S(1)} %fusion.2, f32[512,512]{1,0:T(8,128)S(1)} %fusion.6), kind=kOutput, calls=%fused_computation.2 | convolution fusion | flops 3225944064 | bytes 14680064 | tf_op jit(solution)/shard_map/dot_general | solution.py:150
  226.5 25.0 %reduce-scatter.3.cloned.1.call-done = bf16[64,6144]{1,0:T(8,128)(2,1)} async-done(((bf16[512,6144]{1,0:T(8,128)(2,1)}), bf16[64,6144]{1,0:T(8,128)(2,1)}) %reduce-scatter.3.cloned.1.call-update) | async-done | bytes 786448 | tf_op jit(solution)/shard_map/reduce_scatter | solution.py:151
  251.5 6.7 %all-to-all-start.3 = ((bf16[8,8,6144]{2,1,0:T(8,128)(2,1)}), bf16[8,8,6144]{2,1,0:T(8,128)(2,1)S(1)}, u32[]{:S(2)}, u32[]{:S(2)}) async-start(bf16[8,8,6144]{2,1,0:T(8,128)(2,1)} %bitcast.125), calls=%async_computation.4 | async-start | bytes 1572864 | tf_op jit(solution)/shard_map/all_to_all | solution.py:153
  258.4 37.6 %reduce-scatter.5.cloned.1.call-done = bf16[64,6144]{1,0:T(8,128)(2,1)} async-done(((bf16[512,6144]{1,0:T(8,128)(2,1)}), bf16[64,6144]{1,0:T(8,128)(2,1)}) %reduce-scatter.5.cloned.1.call-update) | async-done | bytes 786448 | tf_op jit(solution)/shard_map/reduce_scatter | solution.py:151
  296.1 6.7 %all-to-all-start.4 = ((bf16[8,8,6144]{2,1,0:T(8,128)(2,1)}), bf16[8,8,6144]{2,1,0:T(8,128)(2,1)}, u32[]{:S(2)}, u32[]{:S(2)}) async-start(bf16[8,8,6144]{2,1,0:T(8,128)(2,1)} %bitcast.126), calls=%async_computation.6 | async-start | bytes 1572864 | tf_op jit(solution)/shard_map/all_to_all | solution.py:153
  303.1 13.6 %all-to-all-done.4 = bf16[8,8,6144]{2,1,0:T(8,128)(2,1)} async-done(((bf16[8,8,6144]{2,1,0:T(8,128)(2,1)}), bf16[8,8,6144]{2,1,0:T(8,128)(2,1)}, u32[]{:S(2)}, u32[]{:S(2)}) %all-to-all-start.4) | async-done | bytes 786464 | tf_op jit(solution)/shard_map/all_to_all | solution.py:153
  316.7 1.2 pad_maximum_fusion
  321.3 9.7 %collective-permute-done.9 = bf16[32,6144]{1,0:T(8,128)(2,1)S(1)} collective-permute-done((bf16[32,6144]{1,0:T(8,128)(2,1)S(1)}, bf16[32,6144]{1,0:T(8,128)(2,1)S(1)}, u32[]{:S(2)}, u32[]{:S(2)}) %collective-permute-start.9) | collective-permute-done | bytes 393248 | tf_op jit(solution)/shard_map/ppermute | solution.py:169
  331.0 1.1 maximum_add_fusion
  (117 shorter events, 19.6 us)
Async XLA Ops:
  6.5 296.3 %copy-start = (bf16[6144,8]{0,1:T(8,128)(2,1)S(1)}, bf16[6144,8]{0,1:T(8,128)(2,1)}, u32[]{:S(2)}) copy-start(bf16[6144,8]{0,1:T(8,128)(2,1)} %param.19) | copy-start | bytes 294916
  8.7 23.0 %collective-permute-start = (bf16[520,384]{0,1:T(8,128)(2,1)S(1)}, bf16[520,384]{0,1:T(8,128)(2,1)S(1)}, u32[]{:S(2)}, u32[]{:S(2)}) collective-permute-start(bf16[520,384]{0,1:T(8,128)(2,1)S(1)} %pad_maximum_fusion.1), channel_id=1, source_target_pairs={{0,32},{16,48},{32,64},{48,80},{64,96},{80,112},{96,0},{112,16},{1... | collective-permute-start | bytes 1198088 | tf_op jit(solution)/shard_map/ppermute | solution.py:72
  10.7 21.1 %collective-permute-start.1 = (bf16[520,384]{0,1:T(8,128)(2,1)S(1)}, bf16[520,384]{0,1:T(8,128)(2,1)S(1)}, u32[]{:S(2)}, u32[]{:S(2)}) collective-permute-start(bf16[520,384]{0,1:T(8,128)(2,1)S(1)} %pad_maximum_fusion.1), channel_id=1, source_target_pairs={{0,64},{16,80},{32,96},{48,112},{64,0},{80,16},{96,32},{112,48},{1... | collective-permute-start | bytes 1198088 | tf_op jit(solution)/shard_map/ppermute | solution.py:72
  11.8 23.2 %collective-permute-start.2 = (bf16[520,384]{0,1:T(8,128)(2,1)S(1)}, bf16[520,384]{0,1:T(8,128)(2,1)S(1)}, u32[]{:S(2)}, u32[]{:S(2)}) collective-permute-start(bf16[520,384]{0,1:T(8,128)(2,1)S(1)} %pad_maximum_fusion.1), channel_id=1, source_target_pairs={{0,96},{16,112},{32,0},{48,16},{64,32},{80,48},{96,64},{112,80},{1... | collective-permute-start | bytes 1198088 | tf_op jit(solution)/shard_map/ppermute | solution.py:72
  14.3 20.8 %collective-permute-start.3 = (bf16[520,384]{0,1:T(8,128)(2,1)S(1)}, bf16[520,384]{0,1:T(8,128)(2,1)}, u32[]{:S(2)}, u32[]{:S(2)}) collective-permute-start(bf16[520,384]{0,1:T(8,128)(2,1)S(1)} %pad_maximum_fusion.1), channel_id=1, source_target_pairs={{0,16},{16,0},{32,48},{48,32},{64,80},{80,64},{96,112},{112,96},{1... | collective-permute-start | bytes 1198088 | tf_op jit(solution)/shard_map/ppermute | solution.py:74
  31.7 4.6 %collective-permute-start.4 = (bf16[520,384]{0,1:T(8,128)(2,1)S(1)}, bf16[520,384]{0,1:T(8,128)(2,1)S(1)}, u32[]{:S(2)}, u32[]{:S(2)}) collective-permute-start(bf16[520,384]{0,1:T(8,128)(2,1)S(1)} %collective-permute-done), channel_id=1, source_target_pairs={{0,16},{16,0},{32,48},{48,32},{64,80},{80,64},{96,112},{112,96},{1... | collective-permute-start | bytes 1198088 | tf_op jit(solution)/shard_map/ppermute | solution.py:74
  31.7 4.6 %collective-permute-start.5 = (bf16[520,384]{0,1:T(8,128)(2,1)S(1)}, bf16[520,384]{0,1:T(8,128)(2,1)S(1)}, u32[]{:S(2)}, u32[]{:S(2)}) collective-permute-start(bf16[520,384]{0,1:T(8,128)(2,1)S(1)} %collective-permute-done.1), channel_id=1, source_target_pairs={{0,16},{16,0},{32,48},{48,32},{64,80},{80,64},{96,112},{112,96},{1... | collective-permute-start | bytes 1198088 | tf_op jit(solution)/shard_map/ppermute | solution.py:74
  35.0 1.9 collective-permute-start.6
  37.3 3.6 %slice-start = ((s8[4718592]{0:T(1024)(128)(4,1)}), s8[524288]{0:T(1024)(128)(4,1)S(1)}, s32[]{:S(2)}) async-start(s8[4718592]{0:T(1024)(128)(4,1)} %bitcast.120), calls=%async_computation.11 | async-start | bytes 1048576
  39.7 2.2 slice-start.1
  41.9 1.9 copy-start.3
  45.9 7.2 %copy-start.5 = (s32[32,2]{0,1:T(2,128)S(1)}, s32[32,2]{0,1:T(2,128)}, u32[]{:S(2)}) copy-start(s32[32,2]{0,1:T(2,128)} %param.20) | copy-start | bytes 772
  45.9 54.9 %copy-start.4 = (f32[6144]{0:T(1024)S(1)}, f32[6144]{0:T(1024)}, u32[]{:S(2)}) copy-start(f32[6144]{0:T(1024)} %param.18) | copy-start | bytes 73732
  45.9 53.7 %all-to-all-start = ((bf16[16,16,6144]{2,1,0:T(8,128)(2,1)}), bf16[16,16,6144]{2,1,0:T(8,128)(2,1)S(1)}, u32[]{:S(2)}, u32[]{:S(2)}) async-start(bf16[16,16,6144]{2,1,0:T(8,128)(2,1)} %bitcast.118), calls=%async_computation | async-start | bytes 6291456 | tf_op jit(solution)/shard_map/all_to_all | solution.py:106
  53.1 111.8 %all-gather.3.cloned.1.call-start = ((), (), s32[]{:S(2)}) async-start(), calls=%async_computation.7 | async-start | bytes 7077888 | tf_op jit(solution)/shard_map/all_gather | solution.py:141
  100.1 0.7 copy-start.1
  101.0 6.9 %collective-permute-start.7 = (bf16[16,6144]{1,0:T(8,128)(2,1)S(1)}, bf16[16,6144]{1,0:T(8,128)(2,1)S(1)}, u32[]{:S(2)}, u32[]{:S(2)}) collective-permute-start(bf16[16,6144]{1,0:T(8,128)(2,1)S(1)} %multiply_convert_fusion.2), channel_id=1, source_target_pairs={{0,1},{1,0},{2,3},{3,2},{4,5},{5,4},{6,7},{7,6},{8,9},{9,8},{10,11... | collective-permute-start | bytes 589832 | tf_op jit(solution)/shard_map/ppermute | solution.py:33
  127.6 80.1 %all-gather.5.cloned.1.call-start = ((), (), s32[]{:S(2)}) async-start(), calls=%async_computation.8 | async-start | bytes 7077888 | tf_op jit(solution)/shard_map/all_gather | solution.py:141
  142.3 109.2 %reduce-scatter.3.cloned.1.call-start = ((), (), s32[]{:S(2)}) async-start(), calls=%async_computation.9 | async-start | bytes 7077888 | tf_op jit(solution)/shard_map/reduce_scatter | solution.py:151
  164.9 8.2 %copy-start.7 = (bf16[512,6144]{1,0:T(8,128)(2,1)S(1)}, bf16[512,6144]{1,0:T(8,128)(2,1)}, u32[]{:S(2)}) copy-start(bf16[512,6144]{1,0:T(8,128)(2,1)} %all-gather.3.cloned.1.call-done) | copy-start | bytes 18874372
  164.9 14.7 %slice-start.2 = ((s8[6291456]{0:T(1024)(128)(4,1)}), s8[4194304]{0:T(1024)(128)(4,1)S(1)}, s32[]{:S(2)}) async-start(s8[6291456]{0:T(1024)(128)(4,1)} %bitcast.138), calls=%async_computation.13 | async-start | bytes 8388608
  173.2 6.5 %slice-start.3 = ((s8[6291456]{0:T(1024)(128)(4,1)}), s8[2097152]{0:T(1024)(128)(4,1)S(1)}, s32[]{:S(2)}) async-start(s8[6291456]{0:T(1024)(128)(4,1)} %bitcast.138), calls=%async_computation.14 | async-start | bytes 4194304
  185.0 1.0 copy-start.2
  185.0 111.0 %reduce-scatter.5.cloned.1.call-start = ((), (), s32[]{:S(2)}) async-start(), calls=%async_computation.10 | async-start | bytes 7077888 | tf_op jit(solution)/shard_map/reduce_scatter | solution.py:151
  186.0 21.7 %collective-permute-start.8 = (f32[16,6144]{1,0:T(8,128)S(1)}, f32[16,6144]{1,0:T(8,128)S(1)}, u32[]{:S(2)}, u32[]{:S(2)}) collective-permute-start(f32[16,6144]{1,0:T(8,128)S(1)} %copy-done.2), channel_id=1, source_target_pairs={{0,1},{1,0},{2,3},{3,2},{4,5},{5,4},{6,7},{7,6},{8,9},{9,8},{10,11... | collective-permute-start | bytes 1179656 | tf_op jit(solution)/shard_map/ppermute | solution.py:144
  207.7 7.6 %copy-start.6 = (bf16[512,6144]{1,0:T(8,128)(2,1)S(1)}, bf16[512,6144]{1,0:T(8,128)(2,1)}, u32[]{:S(2)}) copy-start(bf16[512,6144]{1,0:T(8,128)(2,1)} %all-gather.5.cloned.1.call-done) | copy-start | bytes 18874372
  207.7 13.4 %slice-start.4 = ((s8[6291456]{0:T(1024)(128)(4,1)}), s8[4194304]{0:T(1024)(128)(4,1)S(1)}, s32[]{:S(2)}) async-start(s8[6291456]{0:T(1024)(128)(4,1)} %bitcast.140), calls=%async_computation.15 | async-start | bytes 8388608
  215.3 5.8 %slice-start.5 = ((s8[6291456]{0:T(1024)(128)(4,1)}), s8[2097152]{0:T(1024)(128)(4,1)S(1)}, s32[]{:S(2)}) async-start(s8[6291456]{0:T(1024)(128)(4,1)} %bitcast.140), calls=%async_computation.16 | async-start | bytes 4194304
  251.5 44.6 %all-to-all-start.3 = ((bf16[8,8,6144]{2,1,0:T(8,128)(2,1)}), bf16[8,8,6144]{2,1,0:T(8,128)(2,1)S(1)}, u32[]{:S(2)}, u32[]{:S(2)}) async-start(bf16[8,8,6144]{2,1,0:T(8,128)(2,1)} %bitcast.125), calls=%async_computation.4 | async-start | bytes 1572864 | tf_op jit(solution)/shard_map/all_to_all | solution.py:153
  296.1 20.7 %all-to-all-start.4 = ((bf16[8,8,6144]{2,1,0:T(8,128)(2,1)}), bf16[8,8,6144]{2,1,0:T(8,128)(2,1)}, u32[]{:S(2)}, u32[]{:S(2)}) async-start(bf16[8,8,6144]{2,1,0:T(8,128)(2,1)} %bitcast.126), calls=%async_computation.6 | async-start | bytes 1572864 | tf_op jit(solution)/shard_map/all_to_all | solution.py:153
  320.2 10.8 %collective-permute-start.9 = (bf16[32,6144]{1,0:T(8,128)(2,1)S(1)}, bf16[32,6144]{1,0:T(8,128)(2,1)S(1)}, u32[]{:S(2)}, u32[]{:S(2)}) collective-permute-start(bf16[32,6144]{1,0:T(8,128)(2,1)S(1)} %fusion.26), channel_id=1, source_target_pairs={{0,1},{1,0},{2,3},{3,2},{4,5},{5,4},{6,7},{7,6},{8,9},{9,8},{10,11... | collective-permute-start | bytes 1179656 | tf_op jit(solution)/shard_map/ppermute | solution.py:169
Sparse Core Ops, SparseCore 0:
  127.7 37.2 all-gather.2
  166.6 41.0 all-gather.4
  210.1 41.3 reduce-scatter.2
  253.8 42.2 reduce-scatter.4
